TPU v7x, 512 devices: a whole 4x8x8 slice. The times are simulated.
512 devices in a mesh: sp: 128 (over z, x, y_hi, core), hd: 4 (over y_lo).
Axes of the slice: x: 4, y: 8 (y_hi: 2, y_lo: 4; y = y_hi * 4 + y_lo), z: 8, core: 2. Of those that a mesh axis runs over, the one named last changes fastest.
Arguments:
- query: bfloat16 [128, 3, 128, 2560], P('sp', None, None, 'hd'), may hold values from -8 to 8
- keys: bfloat16 [128, 3, 128, 2560], P('sp', None, None, 'hd'), may hold values from -8 to 8
- values: bfloat16 [128, 3, 128, 2560], P('sp', None, None, 'hd'), may hold values from -6 to 6
- cache_keys: bfloat16 [128, 8, 128, 2560], P('sp', None, None, 'hd'), may hold values from -6 to 6
- cache_values: bfloat16 [128, 8, 128, 2560], P('sp', None, None, 'hd'), may hold values from -6 to 6
- q_gain: float32 [2560], P('hd'), may hold values from 0.1 to 1.9
- k_gain: float32 [2560], P('hd'), may hold values from 0.1 to 1.9
- window_margins: int32 [128, 4], P('sp'), may hold values from 0 to 4
- cache_frames: int32 [128, 9, 2], replicated, may hold values from -1 to 7, as said below
Outputs:
- attn_out: bfloat16 [128, 3, 128, 2560], P('sp', None, None, 'hd')
Inputs may be any that keep to these rules, and one draw needn't show every extreme that they name: cache_frames[t, d, c] is a cached frame or -1 for an empty slot; it is -1 wherever the neighbour tile t + dh * 8 + dw lies outside the grid; the frames listed for one t and d differ.
All inputs are finite; a program needn't handle non-finite values.
Results may differ from a plain program's by a relative error of at most 0.012.
Values may be sent and summed in bfloat16 or wider, within the bound.
No kernel may reach another device: no remote copies, remote signals or barrier semaphores. Data moves between devices by JAX's collectives and lax.ppermute only.
A program may use at most 64 MiB of HBM per device.

v0:
```python
import jax
import jax.numpy as jnp
from jax import lax
from jax.sharding import PartitionSpec as P

HS = 128
TH = 8
TW = 16
GW = 8
HALO = 4


EPSILON = 1e-06
MASKED = -1e30


def shifted(x, axis, by):
    size = lax.axis_size(axis)
    pairs = [(i, i + by) for i in range(size) if 0 <= i + by < size]
    return lax.ppermute(x, axis, pairs)


def edge_part(grid, row_step, col_step):
    if row_step == -1:
        grid = grid[:, TH - HALO :]
    elif row_step == 1:
        grid = grid[:, :HALO]
    if col_step == -1:
        grid = grid[:, :, TW - HALO :]
    elif col_step == 1:
        grid = grid[:, :, :HALO]
    return grid


def slot_of(row_step, col_step):
    return 3 * (row_step + 1) + (col_step + 1)


def normalize(tensor, gain, row_total, width_all):
    wide = tensor.astype(jnp.float32)
    factor = lax.rsqrt(row_total / width_all + EPSILON)
    return (wide * factor[..., None] * gain).astype(jnp.bfloat16)


def body(
    query, keys, values, cache_keys, cache_values, q_gain, k_gain, window_margins, cache_frames
):
    frames_now = query.shape[1]
    tile_len = query.shape[2]
    channels = query.shape[3]
    width_all = channels * lax.axis_size("hd")
    query_wide = query[0].astype(jnp.float32)
    keys_wide = keys[0].astype(jnp.float32)
    query_total, keys_total = lax.psum(
        (jnp.sum(query_wide * query_wide, axis=-1), jnp.sum(keys_wide * keys_wide, axis=-1)), "hd"
    )
    query_normed = normalize(query[0], q_gain, query_total, width_all)
    keys_normed = normalize(keys[0], k_gain, keys_total, width_all)
    key_grid = keys_normed.reshape(frames_now, TH, TW, channels)
    value_grid = values[0].reshape(frames_now, TH, TW, channels)
    own_place = lax.axis_index("sp")
    tile_count = lax.axis_size("sp")
    grid_rows = tile_count // GW
    own_cache_k = cache_keys[0]
    own_cache_v = cache_values[0]

    def blocks_for(target, slot_index):
        safe_target = jnp.clip(target, 0, tile_count - 1)
        listed = lax.dynamic_index_in_dim(cache_frames, safe_target, 0, keepdims=False)[slot_index]
        wanted = jnp.maximum(listed, 0)
        return (own_cache_k[wanted], own_cache_v[wanted])

    center_k, center_v = blocks_for(own_place, 4)
    arrived = {}
    for row_step in (-1, 0, 1):
        for col_step in (-1, 0, 1):
            if not (row_step == 0 and col_step == 0):
                shift_by = -(row_step * GW + col_step)
                block_k, block_v = blocks_for(own_place + shift_by, slot_of(row_step, col_step))
                arrived[row_step, col_step] = shifted(
                    (
                        edge_part(key_grid, row_step, col_step),
                        edge_part(value_grid, row_step, col_step),
                        block_k,
                        block_v,
                    ),
                    "sp",
                    shift_by,
                )
    arrived[0, 0] = (key_grid, value_grid, center_k, center_v)
    bands_k = []
    bands_v = []
    for row_step in (-1, 0, 1):
        bands_k.append(
            jnp.concatenate([arrived[row_step, col_step][0] for col_step in (-1, 0, 1)], axis=2)
        )
        bands_v.append(
            jnp.concatenate([arrived[row_step, col_step][1] for col_step in (-1, 0, 1)], axis=2)
        )
    window_k = jnp.concatenate(bands_k, axis=1)
    window_v = jnp.concatenate(bands_v, axis=1)
    cache_list_k = []
    cache_list_v = []
    for row_step in (-1, 0, 1):
        for col_step in (-1, 0, 1):
            cache_list_k.append(arrived[row_step, col_step][2])
            cache_list_v.append(arrived[row_step, col_step][3])
    flat_wk = window_k.reshape(-1, channels)
    flat_wv = window_v.reshape(-1, channels)
    flat_ck = jnp.stack(cache_list_k).reshape(-1, channels)
    flat_cv = jnp.stack(cache_list_v).reshape(-1, channels)
    flat_q = query_normed.reshape(-1, channels)
    margins = window_margins[0]
    tile_row = own_place // GW
    tile_col = own_place % GW
    row_pos = jnp.arange(TH + 2 * HALO, dtype=jnp.int32)
    row_global = tile_row * TH - HALO + row_pos
    row_valid = (
        (row_global >= 0)
        & (row_global < grid_rows * TH)
        & (row_pos >= HALO - margins[0])
        & (row_pos < HALO + TH + margins[1])
    )
    col_pos = jnp.arange(TW + 2 * HALO, dtype=jnp.int32)
    col_global = tile_col * TW - HALO + col_pos
    col_valid = (
        (col_global >= 0)
        & (col_global < GW * TW)
        & (col_pos >= HALO - margins[2])
        & (col_pos < HALO + TW + margins[3])
    )
    window_valid = jnp.broadcast_to(
        (row_valid[:, None] & col_valid[None, :])[None], (frames_now, TH + 2 * HALO, TW + 2 * HALO)
    ).reshape(-1)
    own_listed = lax.dynamic_index_in_dim(cache_frames, own_place, 0, keepdims=False)
    cache_valid = jnp.broadcast_to(
        (own_listed >= 0)[:, :, None], (9, own_listed.shape[1], tile_len)
    ).reshape(-1)
    score_scale = HS ** (-0.5)

    def attend(head_index):
        chan_start = head_index * HS
        head_q = lax.dynamic_slice_in_dim(flat_q, chan_start, HS, 1)
        head_wk = lax.dynamic_slice_in_dim(flat_wk, chan_start, HS, 1)
        head_wv = lax.dynamic_slice_in_dim(flat_wv, chan_start, HS, 1)
        head_ck = lax.dynamic_slice_in_dim(flat_ck, chan_start, HS, 1)
        head_cv = lax.dynamic_slice_in_dim(flat_cv, chan_start, HS, 1)
        window_scores = (
            jnp.einsum("qc,kc->qk", head_q, head_wk, preferred_element_type=jnp.float32)
            * score_scale
        )
        window_scores = jnp.where(window_valid[None, :], window_scores, MASKED)
        cache_scores = (
            jnp.einsum("qc,kc->qk", head_q, head_ck, preferred_element_type=jnp.float32)
            * score_scale
        )
        cache_scores = jnp.where(cache_valid[None, :], cache_scores, MASKED)
        row_top = jnp.maximum(jnp.max(window_scores, axis=1), jnp.max(cache_scores, axis=1))
        window_exp = jnp.exp(window_scores - row_top[:, None])
        cache_exp = jnp.exp(cache_scores - row_top[:, None])
        row_total = jnp.sum(window_exp, axis=1) + jnp.sum(cache_exp, axis=1)
        window_probs = (window_exp / row_total[:, None]).astype(jnp.bfloat16)
        cache_probs = (cache_exp / row_total[:, None]).astype(jnp.bfloat16)
        mixed_out = jnp.dot(window_probs, head_wv, preferred_element_type=jnp.float32) + jnp.dot(
            cache_probs, head_cv, preferred_element_type=jnp.float32
        )
        return mixed_out.astype(jnp.bfloat16)

    heads_out = lax.map(attend, jnp.arange(channels // HS, dtype=jnp.int32))
    result = jnp.transpose(heads_out, (1, 0, 2)).reshape(1, frames_now, tile_len, channels)
    return result


def solution(mesh):
    return jax.shard_map(
        body,
        mesh=mesh,
        in_specs=(
            P("sp", None, None, "hd"),
            P("sp", None, None, "hd"),
            P("sp", None, None, "hd"),
            P("sp", None, None, "hd"),
            P("sp", None, None, "hd"),
            P("hd"),
            P("hd"),
            P("sp", None),
            P(),
        ),
        out_specs=P("sp", None, None, "hd"),
        check_vma=False,
    )
```

profile of v0, /device:TPU:252, one launch (start us, length us, event | category | flops | bytes accessed | tf_op | source)
XLA Modules:
  0.0 353.4 jit_solution(16964164066640025706)
XLA Ops:
  1.6 9.5 %all-reduce = (f32[3,128]{1,0:T(4,128)S(1)}, f32[3,128]{1,0:T(4,128)S(1)}) all-reduce(f32[3,128]{1,0:T(4,128)S(1)} %get-tuple-element.159, f32[3,128]{1,0:T(4,128)S(1)} %get-tuple-element.158), channel_id=1, replica_groups=mesh['sp'=128,'hd'=4] {'hd'}, use_global_device_ids=true, to_apply=%region_1.0 | all-reduce | flops 768 | bytes 6144 | tf_op jit(solution)/shard_map/psum | solution.py:54
  13.2 2.8 collective-permute-start
  16.0 12.0 %collective-permute-start.2 = (bf16[3,4,4,640]{3,2,1,0:T(4,128)(2,1)}, bf16[3,4,4,640]{3,2,1,0:T(4,128)(2,1)S(1)}, u32[]{:S(2)}, u32[]{:S(2)}) collective-permute-start(bf16[3,4,4,640]{3,2,1,0:T(4,128)(2,1)} %get-tuple-element.149), channel_id=1, source_target_pairs={{0,28},{4,32},{8,36},{12,40},{16,44},{20,48},{24,52},{28,56},{32,6... | collective-permute-start | bytes 184328 | tf_op jit(solution)/shard_map/ppermute | solution.py:20
  28.0 1.9 collective-permute-start.5
  30.0 8.0 %collective-permute-start.7 = (bf16[3,4,4,640]{3,2,1,0:T(4,128)(2,1)}, bf16[3,4,4,640]{3,2,1,0:T(4,128)(2,1)}, u32[]{:S(2)}, u32[]{:S(2)}) collective-permute-start(bf16[3,4,4,640]{3,2,1,0:T(4,128)(2,1)} %get-tuple-element.147), channel_id=1, source_target_pairs={{36,0},{40,4},{44,8},{48,12},{52,16},{56,20},{60,24},{64,28},{68,3... | collective-permute-start | bytes 184328 | tf_op jit(solution)/shard_map/ppermute | solution.py:20
  38.8 6.6 %collective-permute-start.1 = (bf16[3,4,16,640]{3,2,1,0:T(8,128)(2,1)}, bf16[3,4,16,640]{3,2,1,0:T(8,128)(2,1)S(1)}, u32[]{:S(2)}, u32[]{:S(2)}) collective-permute-start(bf16[3,4,16,640]{3,2,1,0:T(8,128)(2,1)} %get-tuple-element.150), channel_id=1, source_target_pairs={{0,32},{4,36},{8,40},{12,44},{16,48},{20,52},{24,56},{28,60},{32,6... | collective-permute-start | bytes 737288 | tf_op jit(solution)/shard_map/ppermute | solution.py:20
  46.2 1.8 fusion.44
  48.1 1.9 fusion.45
  55.6 2.0 fusion.23
  57.7 1.9 collective-permute-start.6
  59.6 2.0 collective-permute-start.16
  61.7 12.9 %collective-permute-start.18 = (bf16[3,4,4,640]{3,2,1,0:T(4,128)(2,1)}, bf16[3,4,4,640]{3,2,1,0:T(4,128)(2,1)}, u32[]{:S(2)}, u32[]{:S(2)}) collective-permute-start(bf16[3,4,4,640]{3,2,1,0:T(4,128)(2,1)} %get-tuple-element.141), channel_id=1, source_target_pairs={{0,28},{4,32},{8,36},{12,40},{16,44},{20,48},{24,52},{28,56},{32,6... | collective-permute-start | bytes 184328 | tf_op jit(solution)/shard_map/ppermute | solution.py:20
  74.6 1.9 collective-permute-start.3
  76.5 7.6 %collective-permute-start.4 = (bf16[3,8,4,640]{3,2,1,0:T(4,128)(2,1)}, bf16[3,8,4,640]{3,2,1,0:T(4,128)(2,1)}, u32[]{:S(2)}, u32[]{:S(2)}) collective-permute-start(bf16[3,8,4,640]{3,2,1,0:T(4,128)(2,1)} %get-tuple-element.153), channel_id=1, source_target_pairs={{4,0},{8,4},{12,8},{16,12},{20,16},{24,20},{28,24},{32,28},{36,32}... | collective-permute-start | bytes 368648 | tf_op jit(solution)/shard_map/ppermute | solution.py:20
  84.1 1.9 collective-permute-start.21
  107.1 7.8 %collective-permute-start.23 = (bf16[3,4,4,640]{3,2,1,0:T(4,128)(2,1)}, bf16[3,4,4,640]{3,2,1,0:T(4,128)(2,1)}, u32[]{:S(2)}, u32[]{:S(2)}) collective-permute-start(bf16[3,4,4,640]{3,2,1,0:T(4,128)(2,1)} %get-tuple-element.139), channel_id=1, source_target_pairs={{36,0},{40,4},{44,8},{48,12},{52,16},{56,20},{60,24},{64,28},{68,3... | collective-permute-start | bytes 184328 | tf_op jit(solution)/shard_map/ppermute | solution.py:20
  117.7 9.2 %collective-permute-start.8 = (bf16[2,128,640]{2,1,0:T(8,128)(2,1)}, bf16[2,128,640]{2,1,0:T(8,128)(2,1)S(1)}, u32[]{:S(2)}, u32[]{:S(2)}) collective-permute-start(bf16[2,128,640]{2,1,0:T(8,128)(2,1)} %gather_fusion), channel_id=1, source_target_pairs={{0,36},{4,40},{8,44},{12,48},{16,52},{20,56},{24,60},{28,64},{32,6... | collective-permute-start | bytes 983048 | tf_op jit(solution)/shard_map/ppermute | solution.py:20
  126.9 1.9 collective-permute-start.17
  128.8 5.4 %collective-permute-start.22 = (bf16[3,4,16,640]{3,2,1,0:T(8,128)(2,1)}, bf16[3,4,16,640]{3,2,1,0:T(8,128)(2,1)S(1)}, u32[]{:S(2)}, u32[]{:S(2)}) collective-permute-start(bf16[3,4,16,640]{3,2,1,0:T(8,128)(2,1)} %get-tuple-element.143), channel_id=1, source_target_pairs={{32,0},{36,4},{40,8},{44,12},{48,16},{52,20},{56,24},{60,28},{64,3... | collective-permute-start | bytes 737288 | tf_op jit(solution)/shard_map/ppermute | solution.py:20
  134.3 1.9 collective-permute-start.19
  136.3 7.7 %collective-permute-start.20 = (bf16[3,8,4,640]{3,2,1,0:T(4,128)(2,1)}, bf16[3,8,4,640]{3,2,1,0:T(4,128)(2,1)S(1)}, u32[]{:S(2)}, u32[]{:S(2)}) collective-permute-start(bf16[3,8,4,640]{3,2,1,0:T(4,128)(2,1)} %get-tuple-element.145), channel_id=1, source_target_pairs={{4,0},{8,4},{12,8},{16,12},{20,16},{24,20},{28,24},{32,28},{36,32}... | collective-permute-start | bytes 368648 | tf_op jit(solution)/shard_map/ppermute | solution.py:20
  143.9 4.2 %maximum_maximum_fusion = bf16[3,16,24,640]{3,2,1,0:T(8,128)(2,1)S(1)} fusion(bf16[3,4,4,640]{3,2,1,0:T(4,128)(2,1)} %collective-permute-done.7, bf16[3,4,16,640]{3,2,1,0:T(8,128)(2,1)} %collective-permute-done.6, bf16[3,4,4,640]{3,2,1,0:T(4,128)(2,1)} %collective-permute-done.5, bf16[3,8,4,640]{3,2,1,0:T(4,128)(2,1)} %collective-permute-done.4, ...), kind=kLoop, calls=%fused_computation.45 | loop fusion | flops 13271040 | bytes 2949120 | tf_op jit(solution)/shard_map/concatenate | solution.py:100
  148.2 4.2 %collective-permute-start.9 = (bf16[2,128,640]{2,1,0:T(8,128)(2,1)}, bf16[2,128,640]{2,1,0:T(8,128)(2,1)S(1)}, u32[]{:S(2)}, u32[]{:S(2)}) collective-permute-start(bf16[2,128,640]{2,1,0:T(8,128)(2,1)} %gather_fusion.1), channel_id=1, source_target_pairs={{0,32},{4,36},{8,40},{12,44},{16,48},{20,52},{24,56},{28,60},{32,6... | collective-permute-start | bytes 983048 | tf_op jit(solution)/shard_map/ppermute | solution.py:20
  152.4 3.7 %collective-permute-start.10 = (bf16[2,128,640]{2,1,0:T(8,128)(2,1)}, bf16[2,128,640]{2,1,0:T(8,128)(2,1)S(1)}, u32[]{:S(2)}, u32[]{:S(2)}) collective-permute-start(bf16[2,128,640]{2,1,0:T(8,128)(2,1)} %gather_fusion.2), channel_id=1, source_target_pairs={{0,28},{4,32},{8,36},{12,40},{16,44},{20,48},{24,52},{28,56},{32,6... | collective-permute-start | bytes 983048 | tf_op jit(solution)/shard_map/ppermute | solution.py:20
  156.1 3.9 %collective-permute-start.11 = (bf16[2,128,640]{2,1,0:T(8,128)(2,1)}, bf16[2,128,640]{2,1,0:T(8,128)(2,1)S(1)}, u32[]{:S(2)}, u32[]{:S(2)}) collective-permute-start(bf16[2,128,640]{2,1,0:T(8,128)(2,1)} %gather_fusion.3), channel_id=1, source_target_pairs={{0,4},{4,8},{8,12},{12,16},{16,20},{20,24},{24,28},{28,32},{32,36}... | collective-permute-start | bytes 983048 | tf_op jit(solution)/shard_map/ppermute | solution.py:20
  160.1 7.1 %collective-permute-start.12 = (bf16[2,128,640]{2,1,0:T(8,128)(2,1)}, bf16[2,128,640]{2,1,0:T(8,128)(2,1)S(1)}, u32[]{:S(2)}, u32[]{:S(2)}) collective-permute-start(bf16[2,128,640]{2,1,0:T(8,128)(2,1)} %gather_fusion.5), channel_id=1, source_target_pairs={{4,0},{8,4},{12,8},{16,12},{20,16},{24,20},{28,24},{32,28},{36,32}... | collective-permute-start | bytes 983048 | tf_op jit(solution)/shard_map/ppermute | solution.py:20
  167.2 5.0 %maximum_maximum_fusion.1 = bf16[3,16,24,640]{3,2,1,0:T(8,128)(2,1)} fusion(bf16[3,4,4,640]{3,2,1,0:T(4,128)(2,1)} %collective-permute-done.23, bf16[3,4,16,640]{3,2,1,0:T(8,128)(2,1)S(1)} %collective-permute-done.22, bf16[3,4,4,640]{3,2,1,0:T(4,128)(2,1)} %collective-permute-done.21, bf16[3,8,4,640]{3,2,1,0:T(4,128)(2,1)S(1)} %collective-permute-done.20, ...), kind=kLoop, calls=%fused_computation.46 | loop fusion | flops 13271040 | bytes 2949120 | tf_op jit(solution)/shard_map/concatenate | solution.py:101
  172.2 4.4 %collective-permute-start.13 = (bf16[2,128,640]{2,1,0:T(8,128)(2,1)S(1)}, bf16[2,128,640]{2,1,0:T(8,128)(2,1)S(1)}, u32[]{:S(2)}, u32[]{:S(2)}) collective-permute-start(bf16[2,128,640]{2,1,0:T(8,128)(2,1)S(1)} %copy-done.13), channel_id=1, source_target_pairs={{28,0},{32,4},{36,8},{40,12},{44,16},{48,20},{52,24},{56,28},{60,3... | collective-permute-start | bytes 983048 | tf_op jit(solution)/shard_map/ppermute | solution.py:20
  176.8 5.3 %collective-permute-start.14 = (bf16[2,128,640]{2,1,0:T(8,128)(2,1)S(1)}, bf16[2,128,640]{2,1,0:T(8,128)(2,1)S(1)}, u32[]{:S(2)}, u32[]{:S(2)}) collective-permute-start(bf16[2,128,640]{2,1,0:T(8,128)(2,1)S(1)} %copy-done.11), channel_id=1, source_target_pairs={{32,0},{36,4},{40,8},{44,12},{48,16},{52,20},{56,24},{60,28},{64,3... | collective-permute-start | bytes 983048 | tf_op jit(solution)/shard_map/ppermute | solution.py:20
  182.1 9.2 %collective-permute-start.24 = (bf16[2,128,640]{2,1,0:T(8,128)(2,1)S(1)}, bf16[2,128,640]{2,1,0:T(8,128)(2,1)S(1)}, u32[]{:S(2)}, u32[]{:S(2)}) collective-permute-start(bf16[2,128,640]{2,1,0:T(8,128)(2,1)S(1)} %copy-done.17), channel_id=1, source_target_pairs={{0,36},{4,40},{8,44},{12,48},{16,52},{20,56},{24,60},{28,64},{32,6... | collective-permute-start | bytes 983048 | tf_op jit(solution)/shard_map/ppermute | solution.py:20
  191.4 4.1 %collective-permute-start.25 = (bf16[2,128,640]{2,1,0:T(8,128)(2,1)S(1)}, bf16[2,128,640]{2,1,0:T(8,128)(2,1)S(1)}, u32[]{:S(2)}, u32[]{:S(2)}) collective-permute-start(bf16[2,128,640]{2,1,0:T(8,128)(2,1)S(1)} %copy-done.16), channel_id=1, source_target_pairs={{0,32},{4,36},{8,40},{12,44},{16,48},{20,52},{24,56},{28,60},{32,6... | collective-permute-start | bytes 983048 | tf_op jit(solution)/shard_map/ppermute | solution.py:20
  195.7 6.8 %collective-permute-done.24 = bf16[2,128,640]{2,1,0:T(8,128)(2,1)S(1)} collective-permute-done((bf16[2,128,640]{2,1,0:T(8,128)(2,1)S(1)}, bf16[2,128,640]{2,1,0:T(8,128)(2,1)S(1)}, u32[]{:S(2)}, u32[]{:S(2)}) %collective-permute-start.24) | collective-permute-done | bytes 327712 | tf_op jit(solution)/shard_map/ppermute | solution.py:20
  202.4 4.9 %collective-permute-start.26 = (bf16[2,128,640]{2,1,0:T(8,128)(2,1)S(1)}, bf16[2,128,640]{2,1,0:T(8,128)(2,1)S(1)}, u32[]{:S(2)}, u32[]{:S(2)}) collective-permute-start(bf16[2,128,640]{2,1,0:T(8,128)(2,1)S(1)} %copy-done.15), channel_id=1, source_target_pairs={{0,28},{4,32},{8,36},{12,40},{16,44},{20,48},{24,52},{28,56},{32,6... | collective-permute-start | bytes 983048 | tf_op jit(solution)/shard_map/ppermute | solution.py:20
  207.4 13.1 %collective-permute-done.25 = bf16[2,128,640]{2,1,0:T(8,128)(2,1)S(1)} collective-permute-done((bf16[2,128,640]{2,1,0:T(8,128)(2,1)S(1)}, bf16[2,128,640]{2,1,0:T(8,128)(2,1)S(1)}, u32[]{:S(2)}, u32[]{:S(2)}) %collective-permute-start.25) | collective-permute-done | bytes 327712 | tf_op jit(solution)/shard_map/ppermute | solution.py:20
  220.5 1.9 collective-permute-start.27
  222.5 5.7 %collective-permute-start.15 = (bf16[2,128,640]{2,1,0:T(8,128)(2,1)S(1)}, bf16[2,128,640]{2,1,0:T(8,128)(2,1)S(1)}, u32[]{:S(2)}, u32[]{:S(2)}) collective-permute-start(bf16[2,128,640]{2,1,0:T(8,128)(2,1)S(1)} %copy-done.12), channel_id=1, source_target_pairs={{36,0},{40,4},{44,8},{48,12},{52,16},{56,20},{60,24},{64,28},{68,3... | collective-permute-start | bytes 983048 | tf_op jit(solution)/shard_map/ppermute | solution.py:20
  228.3 17.5 %collective-permute-done.27 = bf16[2,128,640]{2,1,0:T(8,128)(2,1)S(1)} collective-permute-done((bf16[2,128,640]{2,1,0:T(8,128)(2,1)S(1)}, bf16[2,128,640]{2,1,0:T(8,128)(2,1)S(1)}, u32[]{:S(2)}, u32[]{:S(2)}) %collective-permute-start.27) | collective-permute-done | bytes 327712 | tf_op jit(solution)/shard_map/ppermute | solution.py:20
  245.8 1.9 collective-permute-start.28
  247.8 1.9 collective-permute-start.29
  249.8 6.0 %collective-permute-start.30 = (bf16[2,128,640]{2,1,0:T(8,128)(2,1)S(1)}, bf16[2,128,640]{2,1,0:T(8,128)(2,1)S(1)}, u32[]{:S(2)}, u32[]{:S(2)}) collective-permute-start(bf16[2,128,640]{2,1,0:T(8,128)(2,1)S(1)} %copy-done.7), channel_id=1, source_target_pairs={{32,0},{36,4},{40,8},{44,12},{48,16},{52,20},{56,24},{60,28},{64,3... | collective-permute-start | bytes 983048 | tf_op jit(solution)/shard_map/ppermute | solution.py:20
  255.9 6.5 %collective-permute-start.31 = (bf16[2,128,640]{2,1,0:T(8,128)(2,1)S(1)}, bf16[2,128,640]{2,1,0:T(8,128)(2,1)S(1)}, u32[]{:S(2)}, u32[]{:S(2)}) collective-permute-start(bf16[2,128,640]{2,1,0:T(8,128)(2,1)S(1)} %copy-done.10), channel_id=1, source_target_pairs={{36,0},{40,4},{44,8},{48,12},{52,16},{56,20},{60,24},{64,28},{68,3... | collective-permute-start | bytes 983048 | tf_op jit(solution)/shard_map/ppermute | solution.py:20
  262.6 8.4 %collective-permute-done.29 = bf16[2,128,640]{2,1,0:T(8,128)(2,1)S(1)} collective-permute-done((bf16[2,128,640]{2,1,0:T(8,128)(2,1)S(1)}, bf16[2,128,640]{2,1,0:T(8,128)(2,1)S(1)}, u32[]{:S(2)}, u32[]{:S(2)}) %collective-permute-start.29) | collective-permute-done | bytes 327712 | tf_op jit(solution)/shard_map/ppermute | solution.py:20
  271.0 8.2 %collective-permute-done.30 = bf16[2,128,640]{2,1,0:T(8,128)(2,1)S(1)} collective-permute-done((bf16[2,128,640]{2,1,0:T(8,128)(2,1)S(1)}, bf16[2,128,640]{2,1,0:T(8,128)(2,1)S(1)}, u32[]{:S(2)}, u32[]{:S(2)}) %collective-permute-start.30) | collective-permute-done | bytes 327712 | tf_op jit(solution)/shard_map/ppermute | solution.py:20
  282.3 68.3 %while.11 = (s32[]{:T(128)}, bf16[5,384,128]{2,1,0:T(8,128)(2,1)}, s32[5]{0:T(128)S(1)}, bf16[384,640]{1,0:T(8,128)(2,1)}, bf16[1152,640]{1,0:T(8,128)(2,1)S(1)}...) while((s32[]{:T(128)}, bf16[5,384,128]{2,1,0:T(8,128)(2,1)}, ...), condition=%wide.region_9.10_spmd.clone, body=%wide.region_4.9_spmd.clone.sunk | while | flops 690191616 | bytes 32581108 | solution.py:169
  283.7 3.6 %fusion.61 = (f32[384]{0:T(512)S(1)}, f32[384,2304]{1,0:T(8,128)}) fusion(bf16[2304,640]{1,0:T(8,128)(2,1)} %get-tuple-element.262, s32[]{:T(128)S(6)} %select_n.66, bf16[384,640]{1,0:T(8,128)(2,1)} %get-tuple-element.260, pred[2304]{0:T(1024)(128)(4,1)S(1)} %broadcast_in_dim.102), kind=kOutput, calls=%fused_computation.115.clone.1 | convolution fusion | flops 229146240 | bytes 4231936 | tf_op jit(solution)/shard_map/while/body/eval_jaxpr/qc,kc->qk/dot_general | solution.py:154
  288.8 2.8 fusion.64
  292.0 1.9 fusion.65
  293.9 2.1 fusion.66
  297.3 3.6 %fusion.61 = (f32[384]{0:T(512)S(1)}, f32[384,2304]{1,0:T(8,128)}) fusion(bf16[2304,640]{1,0:T(8,128)(2,1)} %get-tuple-element.262, s32[]{:T(128)S(6)} %select_n.66, bf16[384,640]{1,0:T(8,128)(2,1)} %get-tuple-element.260, pred[2304]{0:T(1024)(128)(4,1)S(1)} %broadcast_in_dim.102), kind=kOutput, calls=%fused_computation.115.clone.1 | convolution fusion | flops 229146240 | bytes 4231936 | tf_op jit(solution)/shard_map/while/body/eval_jaxpr/qc,kc->qk/dot_general | solution.py:154
  302.5 2.8 fusion.64
  305.7 1.9 fusion.65
  307.5 2.1 fusion.66
  311.0 3.6 %fusion.61 = (f32[384]{0:T(512)S(1)}, f32[384,2304]{1,0:T(8,128)}) fusion(bf16[2304,640]{1,0:T(8,128)(2,1)} %get-tuple-element.262, s32[]{:T(128)S(6)} %select_n.66, bf16[384,640]{1,0:T(8,128)(2,1)} %get-tuple-element.260, pred[2304]{0:T(1024)(128)(4,1)S(1)} %broadcast_in_dim.102), kind=kOutput, calls=%fused_computation.115.clone.1 | convolution fusion | flops 229146240 | bytes 4231936 | tf_op jit(solution)/shard_map/while/body/eval_jaxpr/qc,kc->qk/dot_general | solution.py:154
  316.1 2.8 fusion.64
  319.3 1.9 fusion.65
  321.2 2.1 fusion.66
  324.7 3.6 %fusion.61 = (f32[384]{0:T(512)S(1)}, f32[384,2304]{1,0:T(8,128)}) fusion(bf16[2304,640]{1,0:T(8,128)(2,1)} %get-tuple-element.262, s32[]{:T(128)S(6)} %select_n.66, bf16[384,640]{1,0:T(8,128)(2,1)} %get-tuple-element.260, pred[2304]{0:T(1024)(128)(4,1)S(1)} %broadcast_in_dim.102), kind=kOutput, calls=%fused_computation.115.clone.1 | convolution fusion | flops 229146240 | bytes 4231936 | tf_op jit(solution)/shard_map/while/body/eval_jaxpr/qc,kc->qk/dot_general | solution.py:154
  329.8 2.8 fusion.64
  333.0 1.9 fusion.65
  334.9 2.1 fusion.66
  338.3 3.6 %fusion.61 = (f32[384]{0:T(512)S(1)}, f32[384,2304]{1,0:T(8,128)}) fusion(bf16[2304,640]{1,0:T(8,128)(2,1)} %get-tuple-element.262, s32[]{:T(128)S(6)} %select_n.66, bf16[384,640]{1,0:T(8,128)(2,1)} %get-tuple-element.260, pred[2304]{0:T(1024)(128)(4,1)S(1)} %broadcast_in_dim.102), kind=kOutput, calls=%fused_computation.115.clone.1 | convolution fusion | flops 229146240 | bytes 4231936 | tf_op jit(solution)/shard_map/while/body/eval_jaxpr/qc,kc->qk/dot_general | solution.py:154
  343.4 2.8 fusion.64
  346.6 1.9 fusion.65
  348.5 2.1 fusion.66
  (197 shorter events, 52.3 us)
Async XLA Ops:
  0.0 86.0 %copy-start = (bf16[1,8,128,640]{3,2,1,0:T(8,128)(2,1)S(1)}, bf16[1,8,128,640]{3,2,1,0:T(8,128)(2,1)}, u32[]{:S(2)}) copy-start(bf16[1,8,128,640]{3,2,1,0:T(8,128)(2,1)} %param.14) | copy-start | bytes 3932164
  0.0 51.8 %copy-start.21 = (s32[128,9,2]{0,2,1:T(2,128)S(1)}, s32[128,9,2]{0,2,1:T(2,128)}, u32[]{:S(2)}) copy-start(s32[128,9,2]{0,2,1:T(2,128)} %param.19) | copy-start | bytes 27652
  0.0 52.2 %copy-start.23 = (s32[1,4]{1,0:T(1,128)S(1)}, s32[1,4]{1,0:T(1,128)}, u32[]{:S(2)}) copy-start(s32[1,4]{1,0:T(1,128)} %param.18) | copy-start | bytes 52
  0.0 55.6 %copy-start.24 = (f32[640]{0:T(1024)S(1)}, f32[640]{0:T(1024)}, u32[]{:S(2)}) copy-start(f32[640]{0:T(1024)} %param.16) | copy-start | bytes 7684
  13.2 44.5 %collective-permute-start = (bf16[3,4,4,640]{3,2,1,0:T(4,128)(2,1)}, bf16[3,4,4,640]{3,2,1,0:T(4,128)(2,1)S(1)}, u32[]{:S(2)}, u32[]{:S(2)}) collective-permute-start(bf16[3,4,4,640]{3,2,1,0:T(4,128)(2,1)} %get-tuple-element.146), channel_id=1, source_target_pairs={{0,36},{4,40},{8,44},{12,48},{16,52},{20,56},{24,60},{28,64},{32,6... | collective-permute-start | bytes 184328 | tf_op jit(solution)/shard_map/ppermute | solution.py:20
  16.0 43.6 %collective-permute-start.2 = (bf16[3,4,4,640]{3,2,1,0:T(4,128)(2,1)}, bf16[3,4,4,640]{3,2,1,0:T(4,128)(2,1)S(1)}, u32[]{:S(2)}, u32[]{:S(2)}) collective-permute-start(bf16[3,4,4,640]{3,2,1,0:T(4,128)(2,1)} %get-tuple-element.149), channel_id=1, source_target_pairs={{0,28},{4,32},{8,36},{12,40},{16,44},{20,48},{24,52},{28,56},{32,6... | collective-permute-start | bytes 184328 | tf_op jit(solution)/shard_map/ppermute | solution.py:20
  28.0 33.6 %collective-permute-start.5 = (bf16[3,4,4,640]{3,2,1,0:T(4,128)(2,1)}, bf16[3,4,4,640]{3,2,1,0:T(4,128)(2,1)}, u32[]{:S(2)}, u32[]{:S(2)}) collective-permute-start(bf16[3,4,4,640]{3,2,1,0:T(4,128)(2,1)} %get-tuple-element.148), channel_id=1, source_target_pairs={{28,0},{32,4},{36,8},{40,12},{44,16},{48,20},{52,24},{56,28},{60,3... | collective-permute-start | bytes 184328 | tf_op jit(solution)/shard_map/ppermute | solution.py:20
  30.0 58.7 %copy-start.2 = (bf16[1,8,128,640]{3,2,1,0:T(8,128)(2,1)S(1)}, bf16[1,8,128,640]{3,2,1,0:T(8,128)(2,1)}, u32[]{:S(2)}) copy-start(bf16[1,8,128,640]{3,2,1,0:T(8,128)(2,1)} %param.15) | copy-start | bytes 3932164
  30.0 44.6 %collective-permute-start.7 = (bf16[3,4,4,640]{3,2,1,0:T(4,128)(2,1)}, bf16[3,4,4,640]{3,2,1,0:T(4,128)(2,1)}, u32[]{:S(2)}, u32[]{:S(2)}) collective-permute-start(bf16[3,4,4,640]{3,2,1,0:T(4,128)(2,1)} %get-tuple-element.147), channel_id=1, source_target_pairs={{36,0},{40,4},{44,8},{48,12},{52,16},{56,20},{60,24},{64,28},{68,3... | collective-permute-start | bytes 184328 | tf_op jit(solution)/shard_map/ppermute | solution.py:20
  38.8 95.5 %collective-permute-start.1 = (bf16[3,4,16,640]{3,2,1,0:T(8,128)(2,1)}, bf16[3,4,16,640]{3,2,1,0:T(8,128)(2,1)S(1)}, u32[]{:S(2)}, u32[]{:S(2)}) collective-permute-start(bf16[3,4,16,640]{3,2,1,0:T(8,128)(2,1)} %get-tuple-element.150), channel_id=1, source_target_pairs={{0,32},{4,36},{8,40},{12,44},{16,48},{20,52},{24,56},{28,60},{32,6... | collective-permute-start | bytes 737288 | tf_op jit(solution)/shard_map/ppermute | solution.py:20
  57.7 16.9 %copy-start.19 = (bf16[3,4,4,640]{3,2,1,0:T(4,128)(2,1)}, bf16[3,4,4,640]{3,2,1,0:T(4,128)(2,1)S(1)}, u32[]{:S(2)}) copy-start(bf16[3,4,4,640]{3,2,1,0:T(4,128)(2,1)S(1)} %collective-permute-done) | copy-start | bytes 184324
  57.7 78.5 %collective-permute-start.6 = (bf16[3,4,16,640]{3,2,1,0:T(8,128)(2,1)}, bf16[3,4,16,640]{3,2,1,0:T(8,128)(2,1)}, u32[]{:S(2)}, u32[]{:S(2)}) collective-permute-start(bf16[3,4,16,640]{3,2,1,0:T(8,128)(2,1)} %get-tuple-element.151), channel_id=1, source_target_pairs={{32,0},{36,4},{40,8},{44,12},{48,16},{52,20},{56,24},{60,28},{64,3... | collective-permute-start | bytes 737288 | tf_op jit(solution)/shard_map/ppermute | solution.py:20
  59.6 15.0 %copy-start.20 = (bf16[3,4,4,640]{3,2,1,0:T(4,128)(2,1)}, bf16[3,4,4,640]{3,2,1,0:T(4,128)(2,1)S(1)}, u32[]{:S(2)}) copy-start(bf16[3,4,4,640]{3,2,1,0:T(4,128)(2,1)S(1)} %collective-permute-done.2) | copy-start | bytes 184324
  59.6 16.9 %collective-permute-start.16 = (bf16[3,4,4,640]{3,2,1,0:T(4,128)(2,1)}, bf16[3,4,4,640]{3,2,1,0:T(4,128)(2,1)}, u32[]{:S(2)}, u32[]{:S(2)}) collective-permute-start(bf16[3,4,4,640]{3,2,1,0:T(4,128)(2,1)} %get-tuple-element.138), channel_id=1, source_target_pairs={{0,36},{4,40},{8,44},{12,48},{16,52},{20,56},{24,60},{28,64},{32,6... | collective-permute-start | bytes 184328 | tf_op jit(solution)/shard_map/ppermute | solution.py:20
  61.7 22.4 %collective-permute-start.18 = (bf16[3,4,4,640]{3,2,1,0:T(4,128)(2,1)}, bf16[3,4,4,640]{3,2,1,0:T(4,128)(2,1)}, u32[]{:S(2)}, u32[]{:S(2)}) collective-permute-start(bf16[3,4,4,640]{3,2,1,0:T(4,128)(2,1)} %get-tuple-element.141), channel_id=1, source_target_pairs={{0,28},{4,32},{8,36},{12,40},{16,44},{20,48},{24,52},{28,56},{32,6... | collective-permute-start | bytes 184328 | tf_op jit(solution)/shard_map/ppermute | solution.py:20
  74.6 52.3 %collective-permute-start.3 = (bf16[3,8,4,640]{3,2,1,0:T(4,128)(2,1)}, bf16[3,8,4,640]{3,2,1,0:T(4,128)(2,1)S(1)}, u32[]{:S(2)}, u32[]{:S(2)}) collective-permute-start(bf16[3,8,4,640]{3,2,1,0:T(4,128)(2,1)} %get-tuple-element.152), channel_id=1, source_target_pairs={{0,4},{4,8},{8,12},{12,16},{16,20},{20,24},{24,28},{28,32},{32,36}... | collective-permute-start | bytes 368648 | tf_op jit(solution)/shard_map/ppermute | solution.py:20
  76.5 52.3 %collective-permute-start.4 = (bf16[3,8,4,640]{3,2,1,0:T(4,128)(2,1)}, bf16[3,8,4,640]{3,2,1,0:T(4,128)(2,1)}, u32[]{:S(2)}, u32[]{:S(2)}) collective-permute-start(bf16[3,8,4,640]{3,2,1,0:T(4,128)(2,1)} %get-tuple-element.153), channel_id=1, source_target_pairs={{4,0},{8,4},{12,8},{16,12},{20,16},{24,20},{28,24},{32,28},{36,32}... | collective-permute-start | bytes 368648 | tf_op jit(solution)/shard_map/ppermute | solution.py:20
  84.1 23.0 %collective-permute-start.21 = (bf16[3,4,4,640]{3,2,1,0:T(4,128)(2,1)}, bf16[3,4,4,640]{3,2,1,0:T(4,128)(2,1)}, u32[]{:S(2)}, u32[]{:S(2)}) collective-permute-start(bf16[3,4,4,640]{3,2,1,0:T(4,128)(2,1)} %get-tuple-element.140), channel_id=1, source_target_pairs={{28,0},{32,4},{36,8},{40,12},{44,16},{48,20},{52,24},{56,28},{60,3... | collective-permute-start | bytes 184328 | tf_op jit(solution)/shard_map/ppermute | solution.py:20
  107.1 10.6 %collective-permute-start.23 = (bf16[3,4,4,640]{3,2,1,0:T(4,128)(2,1)}, bf16[3,4,4,640]{3,2,1,0:T(4,128)(2,1)}, u32[]{:S(2)}, u32[]{:S(2)}) collective-permute-start(bf16[3,4,4,640]{3,2,1,0:T(4,128)(2,1)} %get-tuple-element.139), channel_id=1, source_target_pairs={{36,0},{40,4},{44,8},{48,12},{52,16},{56,20},{60,24},{64,28},{68,3... | collective-permute-start | bytes 184328 | tf_op jit(solution)/shard_map/ppermute | solution.py:20
  117.7 49.5 %copy-start.3 = (bf16[1,3,128,640]{3,2,1,0:T(8,128)(2,1)S(1)}, bf16[1,3,128,640]{3,2,1,0:T(8,128)(2,1)}, u32[]{:S(2)}) copy-start(bf16[1,3,128,640]{3,2,1,0:T(8,128)(2,1)} %param.13) | copy-start | bytes 1474564
  117.7 54.5 %collective-permute-start.8 = (bf16[2,128,640]{2,1,0:T(8,128)(2,1)}, bf16[2,128,640]{2,1,0:T(8,128)(2,1)S(1)}, u32[]{:S(2)}, u32[]{:S(2)}) collective-permute-start(bf16[2,128,640]{2,1,0:T(8,128)(2,1)} %gather_fusion), channel_id=1, source_target_pairs={{0,36},{4,40},{8,44},{12,48},{16,52},{20,56},{24,60},{28,64},{32,6... | collective-permute-start | bytes 983048 | tf_op jit(solution)/shard_map/ppermute | solution.py:20
  126.9 9.3 %copy-start.18 = (bf16[3,8,4,640]{3,2,1,0:T(4,128)(2,1)}, bf16[3,8,4,640]{3,2,1,0:T(4,128)(2,1)S(1)}, u32[]{:S(2)}) copy-start(bf16[3,8,4,640]{3,2,1,0:T(4,128)(2,1)S(1)} %collective-permute-done.3) | copy-start | bytes 368644
  126.9 29.2 %collective-permute-start.17 = (bf16[3,4,16,640]{3,2,1,0:T(8,128)(2,1)}, bf16[3,4,16,640]{3,2,1,0:T(8,128)(2,1)S(1)}, u32[]{:S(2)}, u32[]{:S(2)}) collective-permute-start(bf16[3,4,16,640]{3,2,1,0:T(8,128)(2,1)} %get-tuple-element.142), channel_id=1, source_target_pairs={{0,32},{4,36},{8,40},{12,44},{16,48},{20,52},{24,56},{28,60},{32,6... | collective-permute-start | bytes 737288 | tf_op jit(solution)/shard_map/ppermute | solution.py:20
  128.8 31.2 %collective-permute-start.22 = (bf16[3,4,16,640]{3,2,1,0:T(8,128)(2,1)}, bf16[3,4,16,640]{3,2,1,0:T(8,128)(2,1)S(1)}, u32[]{:S(2)}, u32[]{:S(2)}) collective-permute-start(bf16[3,4,16,640]{3,2,1,0:T(8,128)(2,1)} %get-tuple-element.143), channel_id=1, source_target_pairs={{32,0},{36,4},{40,8},{44,12},{48,16},{52,20},{56,24},{60,28},{64,3... | collective-permute-start | bytes 737288 | tf_op jit(solution)/shard_map/ppermute | solution.py:20
  134.3 13.9 %collective-permute-start.19 = (bf16[3,8,4,640]{3,2,1,0:T(4,128)(2,1)}, bf16[3,8,4,640]{3,2,1,0:T(4,128)(2,1)S(1)}, u32[]{:S(2)}, u32[]{:S(2)}) collective-permute-start(bf16[3,8,4,640]{3,2,1,0:T(4,128)(2,1)} %get-tuple-element.144), channel_id=1, source_target_pairs={{0,4},{4,8},{8,12},{12,16},{16,20},{20,24},{24,28},{28,32},{32,36}... | collective-permute-start | bytes 368648 | tf_op jit(solution)/shard_map/ppermute | solution.py:20
  136.2 36.0 %copy-start.13 = (bf16[2,128,640]{2,1,0:T(8,128)(2,1)S(1)}, bf16[2,128,640]{2,1,0:T(8,128)(2,1)}, u32[]{:S(2)}) copy-start(bf16[2,128,640]{2,1,0:T(8,128)(2,1)} %gather_fusion.6) | copy-start | bytes 983044
  136.2 40.5 %copy-start.11 = (bf16[2,128,640]{2,1,0:T(8,128)(2,1)S(1)}, bf16[2,128,640]{2,1,0:T(8,128)(2,1)}, u32[]{:S(2)}) copy-start(bf16[2,128,640]{2,1,0:T(8,128)(2,1)} %gather_fusion.7) | copy-start | bytes 983044
  136.2 45.9 %copy-start.17 = (bf16[2,128,640]{2,1,0:T(8,128)(2,1)S(1)}, bf16[2,128,640]{2,1,0:T(8,128)(2,1)}, u32[]{:S(2)}) copy-start(bf16[2,128,640]{2,1,0:T(8,128)(2,1)} %gather_fusion.9) | copy-start | bytes 983044
  136.3 16.1 %collective-permute-start.20 = (bf16[3,8,4,640]{3,2,1,0:T(4,128)(2,1)}, bf16[3,8,4,640]{3,2,1,0:T(4,128)(2,1)S(1)}, u32[]{:S(2)}, u32[]{:S(2)}) collective-permute-start(bf16[3,8,4,640]{3,2,1,0:T(4,128)(2,1)} %get-tuple-element.145), channel_id=1, source_target_pairs={{4,0},{8,4},{12,8},{16,12},{20,16},{24,20},{28,24},{32,28},{36,32}... | collective-permute-start | bytes 368648 | tf_op jit(solution)/shard_map/ppermute | solution.py:20
  148.1 43.3 %copy-start.16 = (bf16[2,128,640]{2,1,0:T(8,128)(2,1)S(1)}, bf16[2,128,640]{2,1,0:T(8,128)(2,1)}, u32[]{:S(2)}) copy-start(bf16[2,128,640]{2,1,0:T(8,128)(2,1)} %gather_fusion.10) | copy-start | bytes 983044
  148.1 47.5 %copy-start.6 = (bf16[2,128,640]{2,1,0:T(8,128)(2,1)S(1)}, bf16[2,128,640]{2,1,0:T(8,128)(2,1)}, u32[]{:S(2)}) copy-start(bf16[2,128,640]{2,1,0:T(8,128)(2,1)} %gather_fusion.4) | copy-start | bytes 983044
  148.1 54.3 %copy-start.15 = (bf16[2,128,640]{2,1,0:T(8,128)(2,1)S(1)}, bf16[2,128,640]{2,1,0:T(8,128)(2,1)}, u32[]{:S(2)}) copy-start(bf16[2,128,640]{2,1,0:T(8,128)(2,1)} %gather_fusion.11) | copy-start | bytes 983044
  148.2 72.4 %copy-start.14 = (bf16[2,128,640]{2,1,0:T(8,128)(2,1)S(1)}, bf16[2,128,640]{2,1,0:T(8,128)(2,1)}, u32[]{:S(2)}) copy-start(bf16[2,128,640]{2,1,0:T(8,128)(2,1)} %gather_fusion.12) | copy-start | bytes 983044
  148.2 28.6 %collective-permute-start.9 = (bf16[2,128,640]{2,1,0:T(8,128)(2,1)}, bf16[2,128,640]{2,1,0:T(8,128)(2,1)S(1)}, u32[]{:S(2)}, u32[]{:S(2)}) collective-permute-start(bf16[2,128,640]{2,1,0:T(8,128)(2,1)} %gather_fusion.1), channel_id=1, source_target_pairs={{0,32},{4,36},{8,40},{12,44},{16,48},{20,52},{24,56},{28,60},{32,6... | collective-permute-start | bytes 983048 | tf_op jit(solution)/shard_map/ppermute | solution.py:20
  152.4 29.8 %collective-permute-start.10 = (bf16[2,128,640]{2,1,0:T(8,128)(2,1)}, bf16[2,128,640]{2,1,0:T(8,128)(2,1)S(1)}, u32[]{:S(2)}, u32[]{:S(2)}) collective-permute-start(bf16[2,128,640]{2,1,0:T(8,128)(2,1)} %gather_fusion.2), channel_id=1, source_target_pairs={{0,28},{4,32},{8,36},{12,40},{16,44},{20,48},{24,52},{28,56},{32,6... | collective-permute-start | bytes 983048 | tf_op jit(solution)/shard_map/ppermute | solution.py:20
  156.1 35.3 %collective-permute-start.11 = (bf16[2,128,640]{2,1,0:T(8,128)(2,1)}, bf16[2,128,640]{2,1,0:T(8,128)(2,1)S(1)}, u32[]{:S(2)}, u32[]{:S(2)}) collective-permute-start(bf16[2,128,640]{2,1,0:T(8,128)(2,1)} %gather_fusion.3), channel_id=1, source_target_pairs={{0,4},{4,8},{8,12},{12,16},{16,20},{20,24},{24,28},{28,32},{32,36}... | collective-permute-start | bytes 983048 | tf_op jit(solution)/shard_map/ppermute | solution.py:20
  160.1 87.8 %collective-permute-start.12 = (bf16[2,128,640]{2,1,0:T(8,128)(2,1)}, bf16[2,128,640]{2,1,0:T(8,128)(2,1)S(1)}, u32[]{:S(2)}, u32[]{:S(2)}) collective-permute-start(bf16[2,128,640]{2,1,0:T(8,128)(2,1)} %gather_fusion.5), channel_id=1, source_target_pairs={{4,0},{8,4},{12,8},{16,12},{20,16},{24,20},{28,24},{32,28},{36,32}... | collective-permute-start | bytes 983048 | tf_op jit(solution)/shard_map/ppermute | solution.py:20
  172.2 50.3 %copy-start.12 = (bf16[2,128,640]{2,1,0:T(8,128)(2,1)S(1)}, bf16[2,128,640]{2,1,0:T(8,128)(2,1)}, u32[]{:S(2)}) copy-start(bf16[2,128,640]{2,1,0:T(8,128)(2,1)} %gather_fusion.8) | copy-start | bytes 983044
  172.2 73.6 %copy-start.9 = (bf16[2,128,640]{2,1,0:T(8,128)(2,1)S(1)}, bf16[2,128,640]{2,1,0:T(8,128)(2,1)}, u32[]{:S(2)}) copy-start(bf16[2,128,640]{2,1,0:T(8,128)(2,1)} %gather_fusion.14) | copy-start | bytes 983044
  172.2 75.5 %copy-start.5 = (bf16[2,128,640]{2,1,0:T(8,128)(2,1)S(1)}, bf16[2,128,640]{2,1,0:T(8,128)(2,1)}, u32[]{:S(2)}) copy-start(bf16[2,128,640]{2,1,0:T(8,128)(2,1)} %gather_fusion.13) | copy-start | bytes 983044
  172.2 77.6 %collective-permute-start.13 = (bf16[2,128,640]{2,1,0:T(8,128)(2,1)S(1)}, bf16[2,128,640]{2,1,0:T(8,128)(2,1)S(1)}, u32[]{:S(2)}, u32[]{:S(2)}) collective-permute-start(bf16[2,128,640]{2,1,0:T(8,128)(2,1)S(1)} %copy-done.13), channel_id=1, source_target_pairs={{28,0},{32,4},{36,8},{40,12},{44,16},{48,20},{52,24},{56,28},{60,3... | collective-permute-start | bytes 983048 | tf_op jit(solution)/shard_map/ppermute | solution.py:20
  176.7 71.1 %copy-start.8 = (bf16[2,128,640]{2,1,0:T(8,128)(2,1)S(1)}, bf16[2,128,640]{2,1,0:T(8,128)(2,1)}, u32[]{:S(2)}) copy-start(bf16[2,128,640]{2,1,0:T(8,128)(2,1)} %gather_fusion.15) | copy-start | bytes 983044
  176.8 79.1 %collective-permute-start.14 = (bf16[2,128,640]{2,1,0:T(8,128)(2,1)S(1)}, bf16[2,128,640]{2,1,0:T(8,128)(2,1)S(1)}, u32[]{:S(2)}, u32[]{:S(2)}) collective-permute-start(bf16[2,128,640]{2,1,0:T(8,128)(2,1)S(1)} %copy-done.11), channel_id=1, source_target_pairs={{32,0},{36,4},{40,8},{44,12},{48,16},{52,20},{56,24},{60,28},{64,3... | collective-permute-start | bytes 983048 | tf_op jit(solution)/shard_map/ppermute | solution.py:20
  182.1 67.7 %copy-start.7 = (bf16[2,128,640]{2,1,0:T(8,128)(2,1)S(1)}, bf16[2,128,640]{2,1,0:T(8,128)(2,1)}, u32[]{:S(2)}) copy-start(bf16[2,128,640]{2,1,0:T(8,128)(2,1)} %gather_fusion.16) | copy-start | bytes 983044
  182.1 20.3 %collective-permute-start.24 = (bf16[2,128,640]{2,1,0:T(8,128)(2,1)S(1)}, bf16[2,128,640]{2,1,0:T(8,128)(2,1)S(1)}, u32[]{:S(2)}, u32[]{:S(2)}) collective-permute-start(bf16[2,128,640]{2,1,0:T(8,128)(2,1)S(1)} %copy-done.17), channel_id=1, source_target_pairs={{0,36},{4,40},{8,44},{12,48},{16,52},{20,56},{24,60},{28,64},{32,6... | collective-permute-start | bytes 983048 | tf_op jit(solution)/shard_map/ppermute | solution.py:20
  191.4 64.4 %copy-start.10 = (bf16[2,128,640]{2,1,0:T(8,128)(2,1)S(1)}, bf16[2,128,640]{2,1,0:T(8,128)(2,1)}, u32[]{:S(2)}) copy-start(bf16[2,128,640]{2,1,0:T(8,128)(2,1)} %gather_fusion.17) | copy-start | bytes 983044
  191.4 29.1 %collective-permute-start.25 = (bf16[2,128,640]{2,1,0:T(8,128)(2,1)S(1)}, bf16[2,128,640]{2,1,0:T(8,128)(2,1)S(1)}, u32[]{:S(2)}, u32[]{:S(2)}) collective-permute-start(bf16[2,128,640]{2,1,0:T(8,128)(2,1)S(1)} %copy-done.16), channel_id=1, source_target_pairs={{0,32},{4,36},{8,40},{12,44},{16,48},{20,52},{24,56},{28,60},{32,6... | collective-permute-start | bytes 983048 | tf_op jit(solution)/shard_map/ppermute | solution.py:20
  202.4 20.0 %collective-permute-start.26 = (bf16[2,128,640]{2,1,0:T(8,128)(2,1)S(1)}, bf16[2,128,640]{2,1,0:T(8,128)(2,1)S(1)}, u32[]{:S(2)}, u32[]{:S(2)}) collective-permute-start(bf16[2,128,640]{2,1,0:T(8,128)(2,1)S(1)} %copy-done.15), channel_id=1, source_target_pairs={{0,28},{4,32},{8,36},{12,40},{16,44},{20,48},{24,52},{28,56},{32,6... | collective-permute-start | bytes 983048 | tf_op jit(solution)/shard_map/ppermute | solution.py:20
  220.5 25.3 %collective-permute-start.27 = (bf16[2,128,640]{2,1,0:T(8,128)(2,1)S(1)}, bf16[2,128,640]{2,1,0:T(8,128)(2,1)S(1)}, u32[]{:S(2)}, u32[]{:S(2)}) collective-permute-start(bf16[2,128,640]{2,1,0:T(8,128)(2,1)S(1)} %copy-done.14), channel_id=1, source_target_pairs={{0,4},{4,8},{8,12},{12,16},{16,20},{20,24},{24,28},{28,32},{32,36}... | collective-permute-start | bytes 983048 | tf_op jit(solution)/shard_map/ppermute | solution.py:20
  222.5 39.9 %collective-permute-start.15 = (bf16[2,128,640]{2,1,0:T(8,128)(2,1)S(1)}, bf16[2,128,640]{2,1,0:T(8,128)(2,1)S(1)}, u32[]{:S(2)}, u32[]{:S(2)}) collective-permute-start(bf16[2,128,640]{2,1,0:T(8,128)(2,1)S(1)} %copy-done.12), channel_id=1, source_target_pairs={{36,0},{40,4},{44,8},{48,12},{52,16},{56,20},{60,24},{64,28},{68,3... | collective-permute-start | bytes 983048 | tf_op jit(solution)/shard_map/ppermute | solution.py:20
  245.8 16.7 %collective-permute-start.28 = (bf16[2,128,640]{2,1,0:T(8,128)(2,1)S(1)}, bf16[2,128,640]{2,1,0:T(8,128)(2,1)S(1)}, u32[]{:S(2)}, u32[]{:S(2)}) collective-permute-start(bf16[2,128,640]{2,1,0:T(8,128)(2,1)S(1)} %copy-done.9), channel_id=1, source_target_pairs={{4,0},{8,4},{12,8},{16,12},{20,16},{24,20},{28,24},{32,28},{36,32}... | collective-permute-start | bytes 983048 | tf_op jit(solution)/shard_map/ppermute | solution.py:20
  247.8 23.2 %collective-permute-start.29 = (bf16[2,128,640]{2,1,0:T(8,128)(2,1)S(1)}, bf16[2,128,640]{2,1,0:T(8,128)(2,1)S(1)}, u32[]{:S(2)}, u32[]{:S(2)}) collective-permute-start(bf16[2,128,640]{2,1,0:T(8,128)(2,1)S(1)} %copy-done.8), channel_id=1, source_target_pairs={{28,0},{32,4},{36,8},{40,12},{44,16},{48,20},{52,24},{56,28},{60,3... | collective-permute-start | bytes 983048 | tf_op jit(solution)/shard_map/ppermute | solution.py:20
  249.8 29.4 %collective-permute-start.30 = (bf16[2,128,640]{2,1,0:T(8,128)(2,1)S(1)}, bf16[2,128,640]{2,1,0:T(8,128)(2,1)S(1)}, u32[]{:S(2)}, u32[]{:S(2)}) collective-permute-start(bf16[2,128,640]{2,1,0:T(8,128)(2,1)S(1)} %copy-done.7), channel_id=1, source_target_pairs={{32,0},{36,4},{40,8},{44,12},{48,16},{52,20},{56,24},{60,28},{64,3... | collective-permute-start | bytes 983048 | tf_op jit(solution)/shard_map/ppermute | solution.py:20
  255.9 24.8 %collective-permute-start.31 = (bf16[2,128,640]{2,1,0:T(8,128)(2,1)S(1)}, bf16[2,128,640]{2,1,0:T(8,128)(2,1)S(1)}, u32[]{:S(2)}, u32[]{:S(2)}) collective-permute-start(bf16[2,128,640]{2,1,0:T(8,128)(2,1)S(1)} %copy-done.10), channel_id=1, source_target_pairs={{36,0},{40,4},{44,8},{48,12},{52,16},{56,20},{60,24},{64,28},{68,3... | collective-permute-start | bytes 983048 | tf_op jit(solution)/shard_map/ppermute | solution.py:20
  262.5 18.2 %copy-start.4 = (bf16[9,2,128,640]{3,2,1,0:T(8,128)(2,1)}, bf16[9,2,128,640]{3,2,1,0:T(8,128)(2,1)S(1)}, u32[]{:S(2)}) copy-start(bf16[9,2,128,640]{3,2,1,0:T(8,128)(2,1)S(1)} %bitcast_dynamic-update-slice_fusion.9) | copy-start | bytes 8847364
  280.7 1.7 copy-start.22
  288.8 3.2 copy-start.1
  302.4 3.2 copy-start.1
  316.1 3.2 copy-start.1
  329.7 3.2 copy-start.1
  343.4 3.2 copy-start.1
where the time goes:
time: 356 us; the launch traced here: 353 us
  starting transfers between devices  164 us (46%)
  waiting for transfers between devices  55.4 us (16%)
  matrix products  44.8 us (13%)
  local copies, waits for them, and re-layouts  42 us (12%)
  other arithmetic  30.5 us (9%)
  blocking collectives  9.48 us (3%)
    ppermute x32, starting transfers between devices, shifted(): return lax.ppermute(x, axis, pairs)  164 us
    ppermute x32, waiting for transfers between devices, shifted(): return lax.ppermute(x, axis, pairs)  55.4 us
    gather x18, local copies, waits for them, and re-layouts, blocks_for(): return (own_cache_k[wanted], own_cache_v[wanted])  23.7 us
    dot_general x5, matrix products, attend(): jnp.einsum('qc,kc->qk', head_q, head_ck, preferred_element_type=jnp.float32)  17.8 us
    reduce_sum x10, other arithmetic, attend(): row_total = jnp.sum(window_exp, axis=1) + jnp.sum(cache_exp, axis=1)  16 us
    dot_general x5, matrix products, attend(): jnp.dot(window_probs, head_wv, preferred_element_type=jnp.float32)  10.5 us
    psum x1, blocking collectives, body(): lax.psum((jnp.sum(query_wide * query_wide, axis=-1), jnp.sum(keys_wide *...  9.48 us
    dot_general x5, matrix products, attend(): jnp.dot(cache_probs, head_cv, preferred_element_type=jnp.float32)  9.34 us
  transfers between devices with their start and end apart: 32, of which 6 were waited for; matrix products, arithmetic and copies ran while one was open for 13% of the time, Pallas kernels for 0%

commit v1 on v0

--- a/solution.py
+++ b/solution.py
@@ -2,6 +2,8 @@
 import jax.numpy as jnp
 from jax import lax
 from jax.sharding import PartitionSpec as P
+from jax.experimental import pallas as pl
+from jax.experimental.pallas import tpu as pltpu
 
 HS = 128
 TH = 8
@@ -40,6 +42,36 @@
     wide = tensor.astype(jnp.float32)
     factor = lax.rsqrt(row_total / width_all + EPSILON)
     return (wide * factor[..., None] * gain).astype(jnp.bfloat16)
+
+
+def attend_kernel(wvalid_ref, cvalid_ref, q_ref, wk_ref, ck_ref, wv_ref, cv_ref, o_ref):
+    score_scale = HS ** (-0.5)
+    dims = (((1,), (1,)), ((), ()))
+    head_q = q_ref[...]
+    window_scores = (
+        lax.dot_general(head_q, wk_ref[...], dims, preferred_element_type=jnp.float32)
+        * score_scale
+    )
+    window_scores = jnp.where(wvalid_ref[...] > 0, window_scores, MASKED)
+    cache_scores = (
+        lax.dot_general(head_q, ck_ref[...], dims, preferred_element_type=jnp.float32)
+        * score_scale
+    )
+    cache_scores = jnp.where(cvalid_ref[...] > 0, cache_scores, MASKED)
+    row_top = jnp.maximum(
+        jnp.max(window_scores, axis=1, keepdims=True), jnp.max(cache_scores, axis=1, keepdims=True)
+    )
+    window_exp = jnp.exp(window_scores - row_top)
+    cache_exp = jnp.exp(cache_scores - row_top)
+    row_total = jnp.sum(window_exp, axis=1, keepdims=True) + jnp.sum(
+        cache_exp, axis=1, keepdims=True
+    )
+    window_probs = (window_exp / row_total).astype(jnp.bfloat16)
+    cache_probs = (cache_exp / row_total).astype(jnp.bfloat16)
+    mixed_out = jnp.dot(window_probs, wv_ref[...], preferred_element_type=jnp.float32) + jnp.dot(
+        cache_probs, cv_ref[...], preferred_element_type=jnp.float32
+    )
+    o_ref[...] = mixed_out.astype(jnp.bfloat16)
 
 
 def body(
@@ -138,36 +170,35 @@
     ).reshape(-1)
     score_scale = HS ** (-0.5)
 
-    def attend(head_index):
-        chan_start = head_index * HS
-        head_q = lax.dynamic_slice_in_dim(flat_q, chan_start, HS, 1)
-        head_wk = lax.dynamic_slice_in_dim(flat_wk, chan_start, HS, 1)
-        head_wv = lax.dynamic_slice_in_dim(flat_wv, chan_start, HS, 1)
-        head_ck = lax.dynamic_slice_in_dim(flat_ck, chan_start, HS, 1)
-        head_cv = lax.dynamic_slice_in_dim(flat_cv, chan_start, HS, 1)
-        window_scores = (
-            jnp.einsum("qc,kc->qk", head_q, head_wk, preferred_element_type=jnp.float32)
-            * score_scale
-        )
-        window_scores = jnp.where(window_valid[None, :], window_scores, MASKED)
-        cache_scores = (
-            jnp.einsum("qc,kc->qk", head_q, head_ck, preferred_element_type=jnp.float32)
-            * score_scale
-        )
-        cache_scores = jnp.where(cache_valid[None, :], cache_scores, MASKED)
-        row_top = jnp.maximum(jnp.max(window_scores, axis=1), jnp.max(cache_scores, axis=1))
-        window_exp = jnp.exp(window_scores - row_top[:, None])
-        cache_exp = jnp.exp(cache_scores - row_top[:, None])
-        row_total = jnp.sum(window_exp, axis=1) + jnp.sum(cache_exp, axis=1)
-        window_probs = (window_exp / row_total[:, None]).astype(jnp.bfloat16)
-        cache_probs = (cache_exp / row_total[:, None]).astype(jnp.bfloat16)
-        mixed_out = jnp.dot(window_probs, head_wv, preferred_element_type=jnp.float32) + jnp.dot(
-            cache_probs, head_cv, preferred_element_type=jnp.float32
-        )
-        return mixed_out.astype(jnp.bfloat16)
-
-    heads_out = lax.map(attend, jnp.arange(channels // HS, dtype=jnp.int32))
-    result = jnp.transpose(heads_out, (1, 0, 2)).reshape(1, frames_now, tile_len, channels)
+    head_count = channels // HS
+    query_rows = flat_q.shape[0]
+    window_len = flat_wk.shape[0]
+    cache_len = flat_ck.shape[0]
+    heads_out = pl.pallas_call(
+        attend_kernel,
+        grid=(head_count,),
+        in_specs=[
+            pl.BlockSpec((1, window_len), lambda h: (0, 0)),
+            pl.BlockSpec((1, cache_len), lambda h: (0, 0)),
+            pl.BlockSpec((query_rows, HS), lambda h: (0, h)),
+            pl.BlockSpec((window_len, HS), lambda h: (0, h)),
+            pl.BlockSpec((cache_len, HS), lambda h: (0, h)),
+            pl.BlockSpec((window_len, HS), lambda h: (0, h)),
+            pl.BlockSpec((cache_len, HS), lambda h: (0, h)),
+        ],
+        out_specs=pl.BlockSpec((query_rows, HS), lambda h: (0, h)),
+        out_shape=jax.ShapeDtypeStruct((query_rows, channels), jnp.bfloat16),
+        compiler_params=pltpu.CompilerParams(vmem_limit_bytes=60 * 1024 * 1024),
+    )(
+        window_valid.astype(jnp.int32)[None, :],
+        cache_valid.astype(jnp.int32)[None, :],
+        flat_q,
+        flat_wk,
+        flat_ck,
+        flat_wv,
+        flat_cv,
+    )
+    result = heads_out.reshape(1, frames_now, tile_len, channels)
     return result
 
 

time: 356 us -> 308 us (0.87)
  the two profiles are of different devices: /device:TPU:252 before, /device:TPU:206 now
where the time goes in v1:
time: 308 us; the launch traced here: 306 us
  starting transfers between devices  148 us (48%)
  waiting for transfers between devices  59.5 us (19%)
  local copies, waits for them, and re-layouts  47.3 us (15%)
  Pallas kernels  22 us (7%)
  other arithmetic  17.1 us (6%)
  blocking collectives  9.56 us (3%)
  between operations  3.11 us (1%)
    ppermute x32, starting transfers between devices, shifted(): return lax.ppermute(x, axis, pairs)  148 us
    ppermute x32, waiting for transfers between devices, shifted(): return lax.ppermute(x, axis, pairs)  59.5 us
    gather x18, local copies, waits for them, and re-layouts, blocks_for(): return (own_cache_k[wanted], own_cache_v[wanted])  23 us
    pallas_call x1, Pallas kernels, body(): pl.pallas_call(attend_kernel, grid=(head_count,), in_specs=[pl.BlockSpec(...  22 us
    unnamed x65, local copies, waits for them, and re-layouts  12.4 us
    psum x1, blocking collectives, body(): lax.psum((jnp.sum(query_wide * query_wide, axis=-1), jnp.sum(keys_wide *...  9.56 us
  transfers between devices with their start and end apart: 32, of which 7 were waited for; matrix products, arithmetic and copies ran while one was open for 19% of the time, Pallas kernels for 0%

profile of v1, /device:TPU:206, one launch (start us, length us, event | category | flops | bytes accessed | tf_op | source)
XLA Modules:
  0.0 306.4 jit_solution(5771446754839655454)
XLA Ops:
  0.0 1.5 multiply_reduce_fusion
  1.6 9.6 %all-reduce = (f32[3,128]{1,0:T(4,128)}, f32[3,128]{1,0:T(4,128)S(1)}) all-reduce(f32[3,128]{1,0:T(4,128)S(1)} %get-tuple-element.37, f32[3,128]{1,0:T(4,128)S(1)} %get-tuple-element.36), channel_id=1, replica_groups=mesh['sp'=128,'hd'=4] {'hd'}, use_global_device_ids=true, to_apply=%region_1.0 | all-reduce | flops 768 | bytes 6144 | tf_op jit(solution)/shard_map/psum | solution.py:86
  13.2 4.0 %collective-permute-start = (bf16[3,4,4,640]{3,2,1,0:T(4,128)(2,1)}, bf16[3,4,4,640]{3,2,1,0:T(4,128)(2,1)S(1)}, u32[]{:S(2)}, u32[]{:S(2)}) collective-permute-start(bf16[3,4,4,640]{3,2,1,0:T(4,128)(2,1)} %get-tuple-element.24), channel_id=1, source_target_pairs={{0,36},{4,40},{8,44},{12,48},{16,52},{20,56},{24,60},{28,64},{32,6... | collective-permute-start | bytes 184328 | tf_op jit(solution)/shard_map/ppermute | solution.py:22
  17.2 10.6 %collective-permute-start.2 = (bf16[3,4,4,640]{3,2,1,0:T(4,128)(2,1)}, bf16[3,4,4,640]{3,2,1,0:T(4,128)(2,1)S(1)}, u32[]{:S(2)}, u32[]{:S(2)}) collective-permute-start(bf16[3,4,4,640]{3,2,1,0:T(4,128)(2,1)} %get-tuple-element.27), channel_id=1, source_target_pairs={{0,28},{4,32},{8,36},{12,40},{16,44},{20,48},{24,52},{28,56},{32,6... | collective-permute-start | bytes 184328 | tf_op jit(solution)/shard_map/ppermute | solution.py:22
  27.8 1.9 collective-permute-start.5
  29.7 7.7 %collective-permute-start.7 = (bf16[3,4,4,640]{3,2,1,0:T(4,128)(2,1)S(1)}, bf16[3,4,4,640]{3,2,1,0:T(4,128)(2,1)S(1)}, u32[]{:S(2)}, u32[]{:S(2)}) collective-permute-start(bf16[3,4,4,640]{3,2,1,0:T(4,128)(2,1)S(1)} %get-tuple-element.25), channel_id=1, source_target_pairs={{36,0},{40,4},{44,8},{48,12},{52,16},{56,20},{60,24},{64,28},{68,3... | collective-permute-start | bytes 184328 | tf_op jit(solution)/shard_map/ppermute | solution.py:22
  38.2 5.1 %collective-permute-start.1 = (bf16[3,4,16,640]{3,2,1,0:T(8,128)(2,1)}, bf16[3,4,16,640]{3,2,1,0:T(8,128)(2,1)}, u32[]{:S(2)}, u32[]{:S(2)}) collective-permute-start(bf16[3,4,16,640]{3,2,1,0:T(8,128)(2,1)} %get-tuple-element.28), channel_id=1, source_target_pairs={{0,32},{4,36},{8,40},{12,44},{16,48},{20,52},{24,56},{28,60},{32,6... | collective-permute-start | bytes 737288 | tf_op jit(solution)/shard_map/ppermute | solution.py:22
  44.2 1.9 fusion.21
  46.1 1.9 fusion.22
  48.0 1.9 fusion.23
  54.8 2.0 fusion.1.q_ref
  57.5 2.2 collective-permute-start.6
  59.7 8.5 %collective-permute-start.16 = (bf16[3,4,4,640]{3,2,1,0:T(4,128)(2,1)}, bf16[3,4,4,640]{3,2,1,0:T(4,128)(2,1)}, u32[]{:S(2)}, u32[]{:S(2)}) collective-permute-start(bf16[3,4,4,640]{3,2,1,0:T(4,128)(2,1)} %get-tuple-element.16), channel_id=1, source_target_pairs={{0,36},{4,40},{8,44},{12,48},{16,52},{20,56},{24,60},{28,64},{32,6... | collective-permute-start | bytes 184328 | tf_op jit(solution)/shard_map/ppermute | solution.py:22
  68.2 7.3 %collective-permute-start.18 = (bf16[3,4,4,640]{3,2,1,0:T(4,128)(2,1)}, bf16[3,4,4,640]{3,2,1,0:T(4,128)(2,1)S(1)}, u32[]{:S(2)}, u32[]{:S(2)}) collective-permute-start(bf16[3,4,4,640]{3,2,1,0:T(4,128)(2,1)} %get-tuple-element.19), channel_id=1, source_target_pairs={{0,28},{4,32},{8,36},{12,40},{16,44},{20,48},{24,52},{28,56},{32,6... | collective-permute-start | bytes 184328 | tf_op jit(solution)/shard_map/ppermute | solution.py:22
  75.6 3.4 %collective-permute-start.3 = (bf16[3,8,4,640]{3,2,1,0:T(4,128)(2,1)}, bf16[3,8,4,640]{3,2,1,0:T(4,128)(2,1)}, u32[]{:S(2)}, u32[]{:S(2)}) collective-permute-start(bf16[3,8,4,640]{3,2,1,0:T(4,128)(2,1)} %get-tuple-element.30), channel_id=1, source_target_pairs={{0,4},{4,8},{8,12},{12,16},{16,20},{20,24},{24,28},{28,32},{32,36}... | collective-permute-start | bytes 368648 | tf_op jit(solution)/shard_map/ppermute | solution.py:22
  79.0 7.0 %collective-permute-start.4 = (bf16[3,8,4,640]{3,2,1,0:T(4,128)(2,1)}, bf16[3,8,4,640]{3,2,1,0:T(4,128)(2,1)}, u32[]{:S(2)}, u32[]{:S(2)}) collective-permute-start(bf16[3,8,4,640]{3,2,1,0:T(4,128)(2,1)} %get-tuple-element.31), channel_id=1, source_target_pairs={{4,0},{8,4},{12,8},{16,12},{20,16},{24,20},{28,24},{32,28},{36,32}... | collective-permute-start | bytes 368648 | tf_op jit(solution)/shard_map/ppermute | solution.py:22
  86.0 5.1 %collective-permute-start.21 = (bf16[3,4,4,640]{3,2,1,0:T(4,128)(2,1)}, bf16[3,4,4,640]{3,2,1,0:T(4,128)(2,1)}, u32[]{:S(2)}, u32[]{:S(2)}) collective-permute-start(bf16[3,4,4,640]{3,2,1,0:T(4,128)(2,1)} %get-tuple-element.18), channel_id=1, source_target_pairs={{28,0},{32,4},{36,8},{40,12},{44,16},{48,20},{52,24},{56,28},{60,3... | collective-permute-start | bytes 184328 | tf_op jit(solution)/shard_map/ppermute | solution.py:22
  91.1 1.3 gather_fusion
  92.4 1.3 gather_fusion.1
  93.8 1.3 gather_fusion.9
  95.1 1.3 gather_fusion.10
  96.4 1.3 gather_fusion.2
  97.7 1.3 gather_fusion.11
  99.0 1.3 gather_fusion.3
  100.4 1.3 gather_fusion.12
  103.6 1.3 gather_fusion.5
  104.9 1.3 gather_fusion.14
  106.3 1.3 gather_fusion.6
  107.6 1.3 gather_fusion.15
  108.9 1.3 gather_fusion.7
  110.2 1.3 gather_fusion.16
  111.5 3.2 %collective-permute-start.23 = (bf16[3,4,4,640]{3,2,1,0:T(4,128)(2,1)}, bf16[3,4,4,640]{3,2,1,0:T(4,128)(2,1)}, u32[]{:S(2)}, u32[]{:S(2)}) collective-permute-start(bf16[3,4,4,640]{3,2,1,0:T(4,128)(2,1)} %get-tuple-element.17), channel_id=1, source_target_pairs={{36,0},{40,4},{44,8},{48,12},{52,16},{56,20},{60,24},{64,28},{68,3... | collective-permute-start | bytes 184328 | tf_op jit(solution)/shard_map/ppermute | solution.py:22
  114.7 1.3 gather_fusion.8
  116.0 1.3 gather_fusion.17
  118.2 4.7 %collective-permute-done.23 = bf16[3,4,4,640]{3,2,1,0:T(4,128)(2,1)} collective-permute-done((bf16[3,4,4,640]{3,2,1,0:T(4,128)(2,1)}, bf16[3,4,4,640]{3,2,1,0:T(4,128)(2,1)}, u32[]{:S(2)}, u32[]{:S(2)}) %collective-permute-start.23) | collective-permute-done | bytes 61472 | tf_op jit(solution)/shard_map/ppermute | solution.py:22
  122.9 10.6 %collective-permute-start.8 = (bf16[2,128,640]{2,1,0:T(8,128)(2,1)}, bf16[2,128,640]{2,1,0:T(8,128)(2,1)S(1)}, u32[]{:S(2)}, u32[]{:S(2)}) collective-permute-start(bf16[2,128,640]{2,1,0:T(8,128)(2,1)} %gather_fusion), channel_id=1, source_target_pairs={{0,36},{4,40},{8,44},{12,48},{16,52},{20,56},{24,60},{28,64},{32,6... | collective-permute-start | bytes 983048 | tf_op jit(solution)/shard_map/ppermute | solution.py:22
  133.5 2.7 collective-permute-start.17
  136.2 4.6 %collective-permute-start.22 = (bf16[3,4,16,640]{3,2,1,0:T(8,128)(2,1)}, bf16[3,4,16,640]{3,2,1,0:T(8,128)(2,1)S(1)}, u32[]{:S(2)}, u32[]{:S(2)}) collective-permute-start(bf16[3,4,16,640]{3,2,1,0:T(8,128)(2,1)} %get-tuple-element.21), channel_id=1, source_target_pairs={{32,0},{36,4},{40,8},{44,12},{48,16},{52,20},{56,24},{60,28},{64,3... | collective-permute-start | bytes 737288 | tf_op jit(solution)/shard_map/ppermute | solution.py:22
  140.9 2.5 collective-permute-start.19
  143.4 8.0 %collective-permute-start.20 = (bf16[3,8,4,640]{3,2,1,0:T(4,128)(2,1)}, bf16[3,8,4,640]{3,2,1,0:T(4,128)(2,1)S(1)}, u32[]{:S(2)}, u32[]{:S(2)}) collective-permute-start(bf16[3,8,4,640]{3,2,1,0:T(4,128)(2,1)} %get-tuple-element.23), channel_id=1, source_target_pairs={{4,0},{8,4},{12,8},{16,12},{20,16},{24,20},{28,24},{32,28},{36,32}... | collective-permute-start | bytes 368648 | tf_op jit(solution)/shard_map/ppermute | solution.py:22
  151.4 5.2 %maximum_maximum_fusion = bf16[3,16,24,640]{3,2,1,0:T(8,128)(2,1)} fusion(bf16[3,4,4,640]{3,2,1,0:T(4,128)(2,1)} %copy-done.18, bf16[3,4,16,640]{3,2,1,0:T(8,128)(2,1)} %collective-permute-done.6, bf16[3,4,4,640]{3,2,1,0:T(4,128)(2,1)} %copy-done.17, bf16[3,8,4,640]{3,2,1,0:T(4,128)(2,1)} %collective-permute-done.4, ...), kind=kLoop, calls=%fused_computation.18 | loop fusion | flops 13271040 | bytes 2949120 | tf_op jit(solution)/shard_map/concatenate | solution.py:132
  156.6 4.9 %collective-permute-start.9 = (bf16[2,128,640]{2,1,0:T(8,128)(2,1)}, bf16[2,128,640]{2,1,0:T(8,128)(2,1)S(1)}, u32[]{:S(2)}, u32[]{:S(2)}) collective-permute-start(bf16[2,128,640]{2,1,0:T(8,128)(2,1)} %gather_fusion.1), channel_id=1, source_target_pairs={{0,32},{4,36},{8,40},{12,44},{16,48},{20,52},{24,56},{28,60},{32,6... | collective-permute-start | bytes 983048 | tf_op jit(solution)/shard_map/ppermute | solution.py:22
  161.6 3.3 %collective-permute-start.10 = (bf16[2,128,640]{2,1,0:T(8,128)(2,1)}, bf16[2,128,640]{2,1,0:T(8,128)(2,1)S(1)}, u32[]{:S(2)}, u32[]{:S(2)}) collective-permute-start(bf16[2,128,640]{2,1,0:T(8,128)(2,1)} %gather_fusion.2), channel_id=1, source_target_pairs={{0,28},{4,32},{8,36},{12,40},{16,44},{20,48},{24,52},{28,56},{32,6... | collective-permute-start | bytes 983048 | tf_op jit(solution)/shard_map/ppermute | solution.py:22
  164.9 1.9 collective-permute-start.11
  166.9 8.4 %collective-permute-start.12 = (bf16[2,128,640]{2,1,0:T(8,128)(2,1)S(1)}, bf16[2,128,640]{2,1,0:T(8,128)(2,1)S(1)}, u32[]{:S(2)}, u32[]{:S(2)}) collective-permute-start(bf16[2,128,640]{2,1,0:T(8,128)(2,1)S(1)} %copy-done.11), channel_id=1, source_target_pairs={{4,0},{8,4},{12,8},{16,12},{20,16},{24,20},{28,24},{32,28},{36,32}... | collective-permute-start | bytes 983048 | tf_op jit(solution)/shard_map/ppermute | solution.py:22
  175.3 4.9 %maximum_maximum_fusion.1 = bf16[3,16,24,640]{3,2,1,0:T(8,128)(2,1)} fusion(bf16[3,4,4,640]{3,2,1,0:T(4,128)(2,1)} %collective-permute-done.23, bf16[3,4,16,640]{3,2,1,0:T(8,128)(2,1)S(1)} %collective-permute-done.22, bf16[3,4,4,640]{3,2,1,0:T(4,128)(2,1)} %collective-permute-done.21, bf16[3,8,4,640]{3,2,1,0:T(4,128)(2,1)S(1)} %collective-permute-done.20, ...), kind=kLoop, calls=%fused_computation.19 | loop fusion | flops 13271040 | bytes 2949120 | tf_op jit(solution)/shard_map/concatenate | solution.py:133
  180.3 2.1 collective-permute-start.13
  183.1 2.7 collective-permute-start.14
  186.6 7.1 %collective-permute-start.24 = (bf16[2,128,640]{2,1,0:T(8,128)(2,1)S(1)}, bf16[2,128,640]{2,1,0:T(8,128)(2,1)S(1)}, u32[]{:S(2)}, u32[]{:S(2)}) collective-permute-start(bf16[2,128,640]{2,1,0:T(8,128)(2,1)S(1)} %copy-done.15), channel_id=1, source_target_pairs={{0,36},{4,40},{8,44},{12,48},{16,52},{20,56},{24,60},{28,64},{32,6... | collective-permute-start | bytes 983048 | tf_op jit(solution)/shard_map/ppermute | solution.py:22
  194.5 3.8 %collective-permute-start.25 = (bf16[2,128,640]{2,1,0:T(8,128)(2,1)S(1)}, bf16[2,128,640]{2,1,0:T(8,128)(2,1)S(1)}, u32[]{:S(2)}, u32[]{:S(2)}) collective-permute-start(bf16[2,128,640]{2,1,0:T(8,128)(2,1)S(1)} %copy-done.14), channel_id=1, source_target_pairs={{0,32},{4,36},{8,40},{12,44},{16,48},{20,52},{24,56},{28,60},{32,6... | collective-permute-start | bytes 983048 | tf_op jit(solution)/shard_map/ppermute | solution.py:22
  199.8 8.6 %collective-permute-done.24 = bf16[2,128,640]{2,1,0:T(8,128)(2,1)S(1)} collective-permute-done((bf16[2,128,640]{2,1,0:T(8,128)(2,1)S(1)}, bf16[2,128,640]{2,1,0:T(8,128)(2,1)S(1)}, u32[]{:S(2)}, u32[]{:S(2)}) %collective-permute-start.24) | collective-permute-done | bytes 327712 | tf_op jit(solution)/shard_map/ppermute | solution.py:22
  208.5 2.8 collective-permute-start.26
  212.1 11.2 %collective-permute-done.25 = bf16[2,128,640]{2,1,0:T(8,128)(2,1)S(1)} collective-permute-done((bf16[2,128,640]{2,1,0:T(8,128)(2,1)S(1)}, bf16[2,128,640]{2,1,0:T(8,128)(2,1)S(1)}, u32[]{:S(2)}, u32[]{:S(2)}) %collective-permute-start.25) | collective-permute-done | bytes 327712 | tf_op jit(solution)/shard_map/ppermute | solution.py:22
  223.2 1.9 collective-permute-start.27
  225.9 6.5 %collective-permute-start.15 = (bf16[2,128,640]{2,1,0:T(8,128)(2,1)S(1)}, bf16[2,128,640]{2,1,0:T(8,128)(2,1)S(1)}, u32[]{:S(2)}, u32[]{:S(2)}) collective-permute-start(bf16[2,128,640]{2,1,0:T(8,128)(2,1)S(1)} %copy-done.9), channel_id=1, source_target_pairs={{36,0},{40,4},{44,8},{48,12},{52,16},{56,20},{60,24},{64,28},{68,3... | collective-permute-start | bytes 983048 | tf_op jit(solution)/shard_map/ppermute | solution.py:22
  233.2 16.1 %collective-permute-done.27 = bf16[2,128,640]{2,1,0:T(8,128)(2,1)S(1)} collective-permute-done((bf16[2,128,640]{2,1,0:T(8,128)(2,1)S(1)}, bf16[2,128,640]{2,1,0:T(8,128)(2,1)S(1)}, u32[]{:S(2)}, u32[]{:S(2)}) %collective-permute-start.27) | collective-permute-done | bytes 327712 | tf_op jit(solution)/shard_map/ppermute | solution.py:22
  249.2 1.9 collective-permute-start.28
  252.7 1.9 collective-permute-start.29
  255.4 1.9 collective-permute-start.30
  258.1 2.1 collective-permute-start.31
  262.5 9.7 %collective-permute-done.29 = bf16[2,128,640]{2,1,0:T(8,128)(2,1)S(1)} collective-permute-done((bf16[2,128,640]{2,1,0:T(8,128)(2,1)S(1)}, bf16[2,128,640]{2,1,0:T(8,128)(2,1)S(1)}, u32[]{:S(2)}, u32[]{:S(2)}) %collective-permute-start.29) | collective-permute-done | bytes 327712 | tf_op jit(solution)/shard_map/ppermute | solution.py:22
  272.9 7.9 %collective-permute-done.30 = bf16[2,128,640]{2,1,0:T(8,128)(2,1)S(1)} collective-permute-done((bf16[2,128,640]{2,1,0:T(8,128)(2,1)S(1)}, bf16[2,128,640]{2,1,0:T(8,128)(2,1)S(1)}, u32[]{:S(2)}, u32[]{:S(2)}) %collective-permute-start.30) | collective-permute-done | bytes 327712 | tf_op jit(solution)/shard_map/ppermute | solution.py:22
  281.6 1.4 collective-permute-done.31
  284.4 22.0 %shard_map.91 = bf16[384,640]{1,0:T(8,128)(2,1)} custom-call(s32[1,1152]{1,0:T(1,128)} %convert_element_type.62.wvalid_ref, s32[1,2304]{1,0:T(1,128)} %bitcast.86, bf16[384,640]{1,0:T(8,128)(2,1)} %fusion.1.q_ref, bf16[1152,640]{1,0:T(8,128)(2,1)} %bitcast.79, bf16[2304,640]{1,0:T(8,128)(2,1)} %bitcast.20.ck_ref, bf16[1152,640]{1,0:T(8,128)(2,1)} %bitcast.80, ...), custom_call_target="tpu_custom_call" | custom-call | tf_op jit(solution)/shard_map/pallas_call | solution.py:177
  (121 shorter events, 24.0 us)
Async XLA Ops:
  0.0 91.1 %copy-start = (bf16[1,8,128,640]{3,2,1,0:T(8,128)(2,1)S(1)}, bf16[1,8,128,640]{3,2,1,0:T(8,128)(2,1)}, u32[]{:S(2)}) copy-start(bf16[1,8,128,640]{3,2,1,0:T(8,128)(2,1)} %param.12) | copy-start | bytes 3932164
  0.0 49.9 %copy-start.21 = (s32[128,9,2]{0,2,1:T(2,128)S(1)}, s32[128,9,2]{0,2,1:T(2,128)}, u32[]{:S(2)}) copy-start(s32[128,9,2]{0,2,1:T(2,128)} %param.17) | copy-start | bytes 27652
  0.0 50.7 %copy-start.22 = (s32[1,4]{1,0:T(1,128)S(1)}, s32[1,4]{1,0:T(1,128)}, u32[]{:S(2)}) copy-start(s32[1,4]{1,0:T(1,128)} %param.16) | copy-start | bytes 52
  0.0 54.8 %copy-start.23 = (f32[640]{0:T(1024)S(1)}, f32[640]{0:T(1024)}, u32[]{:S(2)}) copy-start(f32[640]{0:T(1024)} %param.14) | copy-start | bytes 7684
  13.2 44.3 %collective-permute-start = (bf16[3,4,4,640]{3,2,1,0:T(4,128)(2,1)}, bf16[3,4,4,640]{3,2,1,0:T(4,128)(2,1)S(1)}, u32[]{:S(2)}, u32[]{:S(2)}) collective-permute-start(bf16[3,4,4,640]{3,2,1,0:T(4,128)(2,1)} %get-tuple-element.24), channel_id=1, source_target_pairs={{0,36},{4,40},{8,44},{12,48},{16,52},{20,56},{24,60},{28,64},{32,6... | collective-permute-start | bytes 184328 | tf_op jit(solution)/shard_map/ppermute | solution.py:22
  17.2 42.4 %collective-permute-start.2 = (bf16[3,4,4,640]{3,2,1,0:T(4,128)(2,1)}, bf16[3,4,4,640]{3,2,1,0:T(4,128)(2,1)S(1)}, u32[]{:S(2)}, u32[]{:S(2)}) collective-permute-start(bf16[3,4,4,640]{3,2,1,0:T(4,128)(2,1)} %get-tuple-element.27), channel_id=1, source_target_pairs={{0,28},{4,32},{8,36},{12,40},{16,44},{20,48},{24,52},{28,56},{32,6... | collective-permute-start | bytes 184328 | tf_op jit(solution)/shard_map/ppermute | solution.py:22
  27.8 40.4 %collective-permute-start.5 = (bf16[3,4,4,640]{3,2,1,0:T(4,128)(2,1)S(1)}, bf16[3,4,4,640]{3,2,1,0:T(4,128)(2,1)S(1)}, u32[]{:S(2)}, u32[]{:S(2)}) collective-permute-start(bf16[3,4,4,640]{3,2,1,0:T(4,128)(2,1)S(1)} %get-tuple-element.26), channel_id=1, source_target_pairs={{28,0},{32,4},{36,8},{40,12},{44,16},{48,20},{52,24},{56,28},{60,3... | collective-permute-start | bytes 184328 | tf_op jit(solution)/shard_map/ppermute | solution.py:22
  29.7 64.0 %copy-start.1 = (bf16[1,8,128,640]{3,2,1,0:T(8,128)(2,1)S(1)}, bf16[1,8,128,640]{3,2,1,0:T(8,128)(2,1)}, u32[]{:S(2)}) copy-start(bf16[1,8,128,640]{3,2,1,0:T(8,128)(2,1)} %param.13) | copy-start | bytes 3932164
  29.7 45.8 %collective-permute-start.7 = (bf16[3,4,4,640]{3,2,1,0:T(4,128)(2,1)S(1)}, bf16[3,4,4,640]{3,2,1,0:T(4,128)(2,1)S(1)}, u32[]{:S(2)}, u32[]{:S(2)}) collective-permute-start(bf16[3,4,4,640]{3,2,1,0:T(4,128)(2,1)S(1)} %get-tuple-element.25), channel_id=1, source_target_pairs={{36,0},{40,4},{44,8},{48,12},{52,16},{56,20},{60,24},{64,28},{68,3... | collective-permute-start | bytes 184328 | tf_op jit(solution)/shard_map/ppermute | solution.py:22
  38.2 102.6 %collective-permute-start.1 = (bf16[3,4,16,640]{3,2,1,0:T(8,128)(2,1)}, bf16[3,4,16,640]{3,2,1,0:T(8,128)(2,1)}, u32[]{:S(2)}, u32[]{:S(2)}) collective-permute-start(bf16[3,4,16,640]{3,2,1,0:T(8,128)(2,1)} %get-tuple-element.28), channel_id=1, source_target_pairs={{0,32},{4,36},{8,40},{12,44},{16,48},{20,52},{24,56},{28,60},{32,6... | collective-permute-start | bytes 737288 | tf_op jit(solution)/shard_map/ppermute | solution.py:22
  57.5 85.9 %collective-permute-start.6 = (bf16[3,4,16,640]{3,2,1,0:T(8,128)(2,1)}, bf16[3,4,16,640]{3,2,1,0:T(8,128)(2,1)}, u32[]{:S(2)}, u32[]{:S(2)}) collective-permute-start(bf16[3,4,16,640]{3,2,1,0:T(8,128)(2,1)} %get-tuple-element.29), channel_id=1, source_target_pairs={{32,0},{36,4},{40,8},{44,12},{48,16},{52,20},{56,24},{60,28},{64,3... | collective-permute-start | bytes 737288 | tf_op jit(solution)/shard_map/ppermute | solution.py:22
  59.7 42.0 %copy-start.16 = (bf16[3,4,4,640]{3,2,1,0:T(4,128)(2,1)}, bf16[3,4,4,640]{3,2,1,0:T(4,128)(2,1)S(1)}, u32[]{:S(2)}) copy-start(bf16[3,4,4,640]{3,2,1,0:T(4,128)(2,1)S(1)} %collective-permute-done.2) | copy-start | bytes 184324
  59.7 19.3 %collective-permute-start.16 = (bf16[3,4,4,640]{3,2,1,0:T(4,128)(2,1)}, bf16[3,4,4,640]{3,2,1,0:T(4,128)(2,1)}, u32[]{:S(2)}, u32[]{:S(2)}) collective-permute-start(bf16[3,4,4,640]{3,2,1,0:T(4,128)(2,1)} %get-tuple-element.16), channel_id=1, source_target_pairs={{0,36},{4,40},{8,44},{12,48},{16,52},{20,56},{24,60},{28,64},{32,6... | collective-permute-start | bytes 184328 | tf_op jit(solution)/shard_map/ppermute | solution.py:22
  68.2 33.5 %copy-start.17 = (bf16[3,4,4,640]{3,2,1,0:T(4,128)(2,1)}, bf16[3,4,4,640]{3,2,1,0:T(4,128)(2,1)S(1)}, u32[]{:S(2)}) copy-start(bf16[3,4,4,640]{3,2,1,0:T(4,128)(2,1)S(1)} %collective-permute-done.5) | copy-start | bytes 184324
  68.2 17.7 %collective-permute-start.18 = (bf16[3,4,4,640]{3,2,1,0:T(4,128)(2,1)}, bf16[3,4,4,640]{3,2,1,0:T(4,128)(2,1)S(1)}, u32[]{:S(2)}, u32[]{:S(2)}) collective-permute-start(bf16[3,4,4,640]{3,2,1,0:T(4,128)(2,1)} %get-tuple-element.19), channel_id=1, source_target_pairs={{0,28},{4,32},{8,36},{12,40},{16,44},{20,48},{24,52},{28,56},{32,6... | collective-permute-start | bytes 184328 | tf_op jit(solution)/shard_map/ppermute | solution.py:22
  75.6 26.1 %copy-start.18 = (bf16[3,4,4,640]{3,2,1,0:T(4,128)(2,1)}, bf16[3,4,4,640]{3,2,1,0:T(4,128)(2,1)S(1)}, u32[]{:S(2)}) copy-start(bf16[3,4,4,640]{3,2,1,0:T(4,128)(2,1)S(1)} %collective-permute-done.7) | copy-start | bytes 184324
  75.6 57.9 %collective-permute-start.3 = (bf16[3,8,4,640]{3,2,1,0:T(4,128)(2,1)}, bf16[3,8,4,640]{3,2,1,0:T(4,128)(2,1)}, u32[]{:S(2)}, u32[]{:S(2)}) collective-permute-start(bf16[3,8,4,640]{3,2,1,0:T(4,128)(2,1)} %get-tuple-element.30), channel_id=1, source_target_pairs={{0,4},{4,8},{8,12},{12,16},{16,20},{20,24},{24,28},{28,32},{32,36}... | collective-permute-start | bytes 368648 | tf_op jit(solution)/shard_map/ppermute | solution.py:22
  79.0 57.2 %collective-permute-start.4 = (bf16[3,8,4,640]{3,2,1,0:T(4,128)(2,1)}, bf16[3,8,4,640]{3,2,1,0:T(4,128)(2,1)}, u32[]{:S(2)}, u32[]{:S(2)}) collective-permute-start(bf16[3,8,4,640]{3,2,1,0:T(4,128)(2,1)} %get-tuple-element.31), channel_id=1, source_target_pairs={{4,0},{8,4},{12,8},{16,12},{20,16},{24,20},{28,24},{32,28},{36,32}... | collective-permute-start | bytes 368648 | tf_op jit(solution)/shard_map/ppermute | solution.py:22
  86.0 15.7 %copy-start.19 = (bf16[3,4,4,640]{3,2,1,0:T(4,128)(2,1)}, bf16[3,4,4,640]{3,2,1,0:T(4,128)(2,1)S(1)}, u32[]{:S(2)}) copy-start(bf16[3,4,4,640]{3,2,1,0:T(4,128)(2,1)S(1)} %collective-permute-done.18) | copy-start | bytes 184324
  86.0 25.5 %collective-permute-start.21 = (bf16[3,4,4,640]{3,2,1,0:T(4,128)(2,1)}, bf16[3,4,4,640]{3,2,1,0:T(4,128)(2,1)}, u32[]{:S(2)}, u32[]{:S(2)}) collective-permute-start(bf16[3,4,4,640]{3,2,1,0:T(4,128)(2,1)} %get-tuple-element.18), channel_id=1, source_target_pairs={{28,0},{32,4},{36,8},{40,12},{44,16},{48,20},{52,24},{56,28},{60,3... | collective-permute-start | bytes 184328 | tf_op jit(solution)/shard_map/ppermute | solution.py:22
  111.5 11.3 %collective-permute-start.23 = (bf16[3,4,4,640]{3,2,1,0:T(4,128)(2,1)}, bf16[3,4,4,640]{3,2,1,0:T(4,128)(2,1)}, u32[]{:S(2)}, u32[]{:S(2)}) collective-permute-start(bf16[3,4,4,640]{3,2,1,0:T(4,128)(2,1)} %get-tuple-element.17), channel_id=1, source_target_pairs={{36,0},{40,4},{44,8},{48,12},{52,16},{56,20},{60,24},{64,28},{68,3... | collective-permute-start | bytes 184328 | tf_op jit(solution)/shard_map/ppermute | solution.py:22
  117.4 57.9 %copy-start.2 = (bf16[1,3,128,640]{3,2,1,0:T(8,128)(2,1)S(1)}, bf16[1,3,128,640]{3,2,1,0:T(8,128)(2,1)}, u32[]{:S(2)}) copy-start(bf16[1,3,128,640]{3,2,1,0:T(8,128)(2,1)} %param.11) | copy-start | bytes 1474564
  118.2 48.7 %copy-start.11 = (bf16[2,128,640]{2,1,0:T(8,128)(2,1)S(1)}, bf16[2,128,640]{2,1,0:T(8,128)(2,1)}, u32[]{:S(2)}) copy-start(bf16[2,128,640]{2,1,0:T(8,128)(2,1)} %gather_fusion.5) | copy-start | bytes 983044
  118.2 57.2 %copy-start.20 = (bf16[3,4,4,640]{3,2,1,0:T(4,128)(2,1)S(1)}, bf16[3,4,4,640]{3,2,1,0:T(4,128)(2,1)}, u32[]{:S(2)}) copy-start(bf16[3,4,4,640]{3,2,1,0:T(4,128)(2,1)} %copy-done.19) | copy-start | bytes 184324
  122.9 57.4 %collective-permute-start.8 = (bf16[2,128,640]{2,1,0:T(8,128)(2,1)}, bf16[2,128,640]{2,1,0:T(8,128)(2,1)S(1)}, u32[]{:S(2)}, u32[]{:S(2)}) collective-permute-start(bf16[2,128,640]{2,1,0:T(8,128)(2,1)} %gather_fusion), channel_id=1, source_target_pairs={{0,36},{4,40},{8,44},{12,48},{16,52},{20,56},{24,60},{28,64},{32,6... | collective-permute-start | bytes 983048 | tf_op jit(solution)/shard_map/ppermute | solution.py:22
  133.5 31.4 %collective-permute-start.17 = (bf16[3,4,16,640]{3,2,1,0:T(8,128)(2,1)}, bf16[3,4,16,640]{3,2,1,0:T(8,128)(2,1)S(1)}, u32[]{:S(2)}, u32[]{:S(2)}) collective-permute-start(bf16[3,4,16,640]{3,2,1,0:T(8,128)(2,1)} %get-tuple-element.20), channel_id=1, source_target_pairs={{0,32},{4,36},{8,40},{12,44},{16,48},{20,52},{24,56},{28,60},{32,6... | collective-permute-start | bytes 737288 | tf_op jit(solution)/shard_map/ppermute | solution.py:22
  136.2 30.6 %collective-permute-start.22 = (bf16[3,4,16,640]{3,2,1,0:T(8,128)(2,1)}, bf16[3,4,16,640]{3,2,1,0:T(8,128)(2,1)S(1)}, u32[]{:S(2)}, u32[]{:S(2)}) collective-permute-start(bf16[3,4,16,640]{3,2,1,0:T(8,128)(2,1)} %get-tuple-element.21), channel_id=1, source_target_pairs={{32,0},{36,4},{40,8},{44,12},{48,16},{52,20},{56,24},{60,28},{64,3... | collective-permute-start | bytes 737288 | tf_op jit(solution)/shard_map/ppermute | solution.py:22
  140.9 15.8 %collective-permute-start.19 = (bf16[3,8,4,640]{3,2,1,0:T(4,128)(2,1)}, bf16[3,8,4,640]{3,2,1,0:T(4,128)(2,1)S(1)}, u32[]{:S(2)}, u32[]{:S(2)}) collective-permute-start(bf16[3,8,4,640]{3,2,1,0:T(4,128)(2,1)} %get-tuple-element.22), channel_id=1, source_target_pairs={{0,4},{4,8},{8,12},{12,16},{16,20},{20,24},{24,28},{28,32},{32,36}... | collective-permute-start | bytes 368648 | tf_op jit(solution)/shard_map/ppermute | solution.py:22
  143.4 36.9 %copy-start.10 = (bf16[2,128,640]{2,1,0:T(8,128)(2,1)S(1)}, bf16[2,128,640]{2,1,0:T(8,128)(2,1)}, u32[]{:S(2)}) copy-start(bf16[2,128,640]{2,1,0:T(8,128)(2,1)} %gather_fusion.6) | copy-start | bytes 983044
  143.4 39.8 %copy-start.8 = (bf16[2,128,640]{2,1,0:T(8,128)(2,1)S(1)}, bf16[2,128,640]{2,1,0:T(8,128)(2,1)}, u32[]{:S(2)}) copy-start(bf16[2,128,640]{2,1,0:T(8,128)(2,1)} %gather_fusion.7) | copy-start | bytes 983044
  143.4 43.3 %copy-start.15 = (bf16[2,128,640]{2,1,0:T(8,128)(2,1)S(1)}, bf16[2,128,640]{2,1,0:T(8,128)(2,1)}, u32[]{:S(2)}) copy-start(bf16[2,128,640]{2,1,0:T(8,128)(2,1)} %gather_fusion.9) | copy-start | bytes 983044
  143.4 18.2 %collective-permute-start.20 = (bf16[3,8,4,640]{3,2,1,0:T(4,128)(2,1)}, bf16[3,8,4,640]{3,2,1,0:T(4,128)(2,1)S(1)}, u32[]{:S(2)}, u32[]{:S(2)}) collective-permute-start(bf16[3,8,4,640]{3,2,1,0:T(4,128)(2,1)} %get-tuple-element.23), channel_id=1, source_target_pairs={{4,0},{8,4},{12,8},{16,12},{20,16},{24,20},{28,24},{32,28},{36,32}... | collective-permute-start | bytes 368648 | tf_op jit(solution)/shard_map/ppermute | solution.py:22
  156.6 37.9 %copy-start.14 = (bf16[2,128,640]{2,1,0:T(8,128)(2,1)S(1)}, bf16[2,128,640]{2,1,0:T(8,128)(2,1)}, u32[]{:S(2)}) copy-start(bf16[2,128,640]{2,1,0:T(8,128)(2,1)} %gather_fusion.10) | copy-start | bytes 983044
  156.6 42.5 %copy-start.3 = (bf16[2,128,640]{2,1,0:T(8,128)(2,1)S(1)}, bf16[2,128,640]{2,1,0:T(8,128)(2,1)}, u32[]{:S(2)}) copy-start(bf16[2,128,640]{2,1,0:T(8,128)(2,1)} %gather_fusion.4) | copy-start | bytes 983044
  156.6 51.9 %copy-start.13 = (bf16[2,128,640]{2,1,0:T(8,128)(2,1)S(1)}, bf16[2,128,640]{2,1,0:T(8,128)(2,1)}, u32[]{:S(2)}) copy-start(bf16[2,128,640]{2,1,0:T(8,128)(2,1)} %gather_fusion.11) | copy-start | bytes 983044
  156.6 66.6 %copy-start.12 = (bf16[2,128,640]{2,1,0:T(8,128)(2,1)S(1)}, bf16[2,128,640]{2,1,0:T(8,128)(2,1)}, u32[]{:S(2)}) copy-start(bf16[2,128,640]{2,1,0:T(8,128)(2,1)} %gather_fusion.12) | copy-start | bytes 983044
  156.6 26.5 %collective-permute-start.9 = (bf16[2,128,640]{2,1,0:T(8,128)(2,1)}, bf16[2,128,640]{2,1,0:T(8,128)(2,1)S(1)}, u32[]{:S(2)}, u32[]{:S(2)}) collective-permute-start(bf16[2,128,640]{2,1,0:T(8,128)(2,1)} %gather_fusion.1), channel_id=1, source_target_pairs={{0,32},{4,36},{8,40},{12,44},{16,48},{20,52},{24,56},{28,60},{32,6... | collective-permute-start | bytes 983048 | tf_op jit(solution)/shard_map/ppermute | solution.py:22
  161.6 25.1 %collective-permute-start.10 = (bf16[2,128,640]{2,1,0:T(8,128)(2,1)}, bf16[2,128,640]{2,1,0:T(8,128)(2,1)S(1)}, u32[]{:S(2)}, u32[]{:S(2)}) collective-permute-start(bf16[2,128,640]{2,1,0:T(8,128)(2,1)} %gather_fusion.2), channel_id=1, source_target_pairs={{0,28},{4,32},{8,36},{12,40},{16,44},{20,48},{24,52},{28,56},{32,6... | collective-permute-start | bytes 983048 | tf_op jit(solution)/shard_map/ppermute | solution.py:22
  164.9 29.6 %collective-permute-start.11 = (bf16[2,128,640]{2,1,0:T(8,128)(2,1)}, bf16[2,128,640]{2,1,0:T(8,128)(2,1)S(1)}, u32[]{:S(2)}, u32[]{:S(2)}) collective-permute-start(bf16[2,128,640]{2,1,0:T(8,128)(2,1)} %gather_fusion.3), channel_id=1, source_target_pairs={{0,4},{4,8},{8,12},{12,16},{16,20},{20,24},{24,28},{28,32},{32,36}... | collective-permute-start | bytes 983048 | tf_op jit(solution)/shard_map/ppermute | solution.py:22
  166.9 85.8 %collective-permute-start.12 = (bf16[2,128,640]{2,1,0:T(8,128)(2,1)S(1)}, bf16[2,128,640]{2,1,0:T(8,128)(2,1)S(1)}, u32[]{:S(2)}, u32[]{:S(2)}) collective-permute-start(bf16[2,128,640]{2,1,0:T(8,128)(2,1)S(1)} %copy-done.11), channel_id=1, source_target_pairs={{4,0},{8,4},{12,8},{16,12},{20,16},{24,20},{28,24},{32,28},{36,32}... | collective-permute-start | bytes 983048 | tf_op jit(solution)/shard_map/ppermute | solution.py:22
  180.3 45.6 %copy-start.9 = (bf16[2,128,640]{2,1,0:T(8,128)(2,1)S(1)}, bf16[2,128,640]{2,1,0:T(8,128)(2,1)}, u32[]{:S(2)}) copy-start(bf16[2,128,640]{2,1,0:T(8,128)(2,1)} %gather_fusion.8) | copy-start | bytes 983044
  180.3 69.0 %copy-start.6 = (bf16[2,128,640]{2,1,0:T(8,128)(2,1)S(1)}, bf16[2,128,640]{2,1,0:T(8,128)(2,1)}, u32[]{:S(2)}) copy-start(bf16[2,128,640]{2,1,0:T(8,128)(2,1)} %gather_fusion.14) | copy-start | bytes 983044
  180.3 75.1 %collective-permute-start.13 = (bf16[2,128,640]{2,1,0:T(8,128)(2,1)S(1)}, bf16[2,128,640]{2,1,0:T(8,128)(2,1)S(1)}, u32[]{:S(2)}, u32[]{:S(2)}) collective-permute-start(bf16[2,128,640]{2,1,0:T(8,128)(2,1)S(1)} %copy-done.10), channel_id=1, source_target_pairs={{28,0},{32,4},{36,8},{40,12},{44,16},{48,20},{52,24},{56,28},{60,3... | collective-permute-start | bytes 983048 | tf_op jit(solution)/shard_map/ppermute | solution.py:22
  183.1 69.6 %copy-start.5 = (bf16[2,128,640]{2,1,0:T(8,128)(2,1)S(1)}, bf16[2,128,640]{2,1,0:T(8,128)(2,1)}, u32[]{:S(2)}) copy-start(bf16[2,128,640]{2,1,0:T(8,128)(2,1)} %gather_fusion.15) | copy-start | bytes 983044
  183.1 75.0 %collective-permute-start.14 = (bf16[2,128,640]{2,1,0:T(8,128)(2,1)S(1)}, bf16[2,128,640]{2,1,0:T(8,128)(2,1)S(1)}, u32[]{:S(2)}, u32[]{:S(2)}) collective-permute-start(bf16[2,128,640]{2,1,0:T(8,128)(2,1)S(1)} %copy-done.8), channel_id=1, source_target_pairs={{32,0},{36,4},{40,8},{44,12},{48,16},{52,20},{56,24},{60,28},{64,3... | collective-permute-start | bytes 983048 | tf_op jit(solution)/shard_map/ppermute | solution.py:22
  186.6 68.8 %copy-start.4 = (bf16[2,128,640]{2,1,0:T(8,128)(2,1)S(1)}, bf16[2,128,640]{2,1,0:T(8,128)(2,1)}, u32[]{:S(2)}) copy-start(bf16[2,128,640]{2,1,0:T(8,128)(2,1)} %gather_fusion.16) | copy-start | bytes 983044
  186.6 21.8 %collective-permute-start.24 = (bf16[2,128,640]{2,1,0:T(8,128)(2,1)S(1)}, bf16[2,128,640]{2,1,0:T(8,128)(2,1)S(1)}, u32[]{:S(2)}, u32[]{:S(2)}) collective-permute-start(bf16[2,128,640]{2,1,0:T(8,128)(2,1)S(1)} %copy-done.15), channel_id=1, source_target_pairs={{0,36},{4,40},{8,44},{12,48},{16,52},{20,56},{24,60},{28,64},{32,6... | collective-permute-start | bytes 983048 | tf_op jit(solution)/shard_map/ppermute | solution.py:22
  194.5 63.6 %copy-start.7 = (bf16[2,128,640]{2,1,0:T(8,128)(2,1)S(1)}, bf16[2,128,640]{2,1,0:T(8,128)(2,1)}, u32[]{:S(2)}) copy-start(bf16[2,128,640]{2,1,0:T(8,128)(2,1)} %gather_fusion.17) | copy-start | bytes 983044
  194.5 28.7 %collective-permute-start.25 = (bf16[2,128,640]{2,1,0:T(8,128)(2,1)S(1)}, bf16[2,128,640]{2,1,0:T(8,128)(2,1)S(1)}, u32[]{:S(2)}, u32[]{:S(2)}) collective-permute-start(bf16[2,128,640]{2,1,0:T(8,128)(2,1)S(1)} %copy-done.14), channel_id=1, source_target_pairs={{0,32},{4,36},{8,40},{12,44},{16,48},{20,52},{24,56},{28,60},{32,6... | collective-permute-start | bytes 983048 | tf_op jit(solution)/shard_map/ppermute | solution.py:22
  208.5 17.4 %collective-permute-start.26 = (bf16[2,128,640]{2,1,0:T(8,128)(2,1)S(1)}, bf16[2,128,640]{2,1,0:T(8,128)(2,1)S(1)}, u32[]{:S(2)}, u32[]{:S(2)}) collective-permute-start(bf16[2,128,640]{2,1,0:T(8,128)(2,1)S(1)} %copy-done.13), channel_id=1, source_target_pairs={{0,28},{4,32},{8,36},{12,40},{16,44},{20,48},{24,52},{28,56},{32,6... | collective-permute-start | bytes 983048 | tf_op jit(solution)/shard_map/ppermute | solution.py:22
  223.2 26.0 %collective-permute-start.27 = (bf16[2,128,640]{2,1,0:T(8,128)(2,1)S(1)}, bf16[2,128,640]{2,1,0:T(8,128)(2,1)S(1)}, u32[]{:S(2)}, u32[]{:S(2)}) collective-permute-start(bf16[2,128,640]{2,1,0:T(8,128)(2,1)S(1)} %copy-done.12), channel_id=1, source_target_pairs={{0,4},{4,8},{8,12},{12,16},{16,20},{20,24},{24,28},{28,32},{32,36}... | collective-permute-start | bytes 983048 | tf_op jit(solution)/shard_map/ppermute | solution.py:22
  225.9 35.0 %collective-permute-start.15 = (bf16[2,128,640]{2,1,0:T(8,128)(2,1)S(1)}, bf16[2,128,640]{2,1,0:T(8,128)(2,1)S(1)}, u32[]{:S(2)}, u32[]{:S(2)}) collective-permute-start(bf16[2,128,640]{2,1,0:T(8,128)(2,1)S(1)} %copy-done.9), channel_id=1, source_target_pairs={{36,0},{40,4},{44,8},{48,12},{52,16},{56,20},{60,24},{64,28},{68,3... | collective-permute-start | bytes 983048 | tf_op jit(solution)/shard_map/ppermute | solution.py:22
  249.2 12.5 %collective-permute-start.28 = (bf16[2,128,640]{2,1,0:T(8,128)(2,1)S(1)}, bf16[2,128,640]{2,1,0:T(8,128)(2,1)S(1)}, u32[]{:S(2)}, u32[]{:S(2)}) collective-permute-start(bf16[2,128,640]{2,1,0:T(8,128)(2,1)S(1)} %copy-done.6), channel_id=1, source_target_pairs={{4,0},{8,4},{12,8},{16,12},{20,16},{24,20},{28,24},{32,28},{36,32}... | collective-permute-start | bytes 983048 | tf_op jit(solution)/shard_map/ppermute | solution.py:22
  252.7 19.5 %collective-permute-start.29 = (bf16[2,128,640]{2,1,0:T(8,128)(2,1)S(1)}, bf16[2,128,640]{2,1,0:T(8,128)(2,1)S(1)}, u32[]{:S(2)}, u32[]{:S(2)}) collective-permute-start(bf16[2,128,640]{2,1,0:T(8,128)(2,1)S(1)} %copy-done.5), channel_id=1, source_target_pairs={{28,0},{32,4},{36,8},{40,12},{44,16},{48,20},{52,24},{56,28},{60,3... | collective-permute-start | bytes 983048 | tf_op jit(solution)/shard_map/ppermute | solution.py:22
  255.4 25.4 %collective-permute-start.30 = (bf16[2,128,640]{2,1,0:T(8,128)(2,1)S(1)}, bf16[2,128,640]{2,1,0:T(8,128)(2,1)S(1)}, u32[]{:S(2)}, u32[]{:S(2)}) collective-permute-start(bf16[2,128,640]{2,1,0:T(8,128)(2,1)S(1)} %copy-done.4), channel_id=1, source_target_pairs={{32,0},{36,4},{40,8},{44,12},{48,16},{52,20},{56,24},{60,28},{64,3... | collective-permute-start | bytes 983048 | tf_op jit(solution)/shard_map/ppermute | solution.py:22
  258.1 24.9 %collective-permute-start.31 = (bf16[2,128,640]{2,1,0:T(8,128)(2,1)S(1)}, bf16[2,128,640]{2,1,0:T(8,128)(2,1)S(1)}, u32[]{:S(2)}, u32[]{:S(2)}) collective-permute-start(bf16[2,128,640]{2,1,0:T(8,128)(2,1)S(1)} %copy-done.7), channel_id=1, source_target_pairs={{36,0},{40,4},{44,8},{48,12},{52,16},{56,20},{60,24},{64,28},{68,3... | collective-permute-start | bytes 983048 | tf_op jit(solution)/shard_map/ppermute | solution.py:22

commit v2 on v1

--- a/solution.py
+++ b/solution.py
@@ -96,28 +96,46 @@
     own_cache_k = cache_keys[0]
     own_cache_v = cache_values[0]
 
+    cap = cache_frames.shape[2]
+
     def blocks_for(target, slot_index):
         safe_target = jnp.clip(target, 0, tile_count - 1)
         listed = lax.dynamic_index_in_dim(cache_frames, safe_target, 0, keepdims=False)[slot_index]
         wanted = jnp.maximum(listed, 0)
-        return (own_cache_k[wanted], own_cache_v[wanted])
+        picked_k = [
+            lax.dynamic_index_in_dim(own_cache_k, wanted[c], 0, keepdims=False) for c in range(cap)
+        ]
+        picked_v = [
+            lax.dynamic_index_in_dim(own_cache_v, wanted[c], 0, keepdims=False) for c in range(cap)
+        ]
+        return picked_k, picked_v
 
     center_k, center_v = blocks_for(own_place, 4)
+    center_k = jnp.stack(center_k)
+    center_v = jnp.stack(center_v)
     arrived = {}
     for row_step in (-1, 0, 1):
         for col_step in (-1, 0, 1):
             if not (row_step == 0 and col_step == 0):
                 shift_by = -(row_step * GW + col_step)
                 block_k, block_v = blocks_for(own_place + shift_by, slot_of(row_step, col_step))
-                arrived[row_step, col_step] = shifted(
-                    (
-                        edge_part(key_grid, row_step, col_step),
-                        edge_part(value_grid, row_step, col_step),
-                        block_k,
-                        block_v,
-                    ),
-                    "sp",
-                    shift_by,
+                edge_k = edge_part(key_grid, row_step, col_step)
+                edge_v = edge_part(value_grid, row_step, col_step)
+                edge_shape = edge_k.shape
+                edge_rows = edge_k.size // channels
+                packed = jnp.concatenate(
+                    [edge_k.reshape(edge_rows, channels), edge_v.reshape(edge_rows, channels)]
+                    + block_k
+                    + block_v,
+                    axis=0,
+                )
+                got = shifted(packed, "sp", shift_by)
+                cache_rows = cap * tile_len
+                arrived[row_step, col_step] = (
+                    got[:edge_rows].reshape(edge_shape),
+                    got[edge_rows : 2 * edge_rows].reshape(edge_shape),
+                    got[2 * edge_rows : 2 * edge_rows + cache_rows].reshape(cap, tile_len, channels),
+                    got[2 * edge_rows + cache_rows :].reshape(cap, tile_len, channels),
                 )
     arrived[0, 0] = (key_grid, value_grid, center_k, center_v)
     bands_k = []

time: 308 us -> 259 us (0.84)
  the two profiles are of different devices: /device:TPU:206 before, /device:TPU:226 now
where the time goes in v2:
time: 259 us; the launch traced here: 257 us
  local copies, waits for them, and re-layouts  67.1 us (26%)
  waiting for transfers between devices  66.6 us (26%)
  starting transfers between devices  41.7 us (16%)
  between operations  36.3 us (14%)
  Pallas kernels  22 us (8%)
  other arithmetic  14.2 us (5%)
  blocking collectives  9.27 us (4%)
    ppermute x8, waiting for transfers between devices, shifted(): return lax.ppermute(x, axis, pairs)  66.6 us
    ppermute x8, starting transfers between devices, shifted(): return lax.ppermute(x, axis, pairs)  41.7 us
    pallas_call x1, Pallas kernels, body(): pl.pallas_call(attend_kernel, grid=(head_count,), in_specs=[pl.BlockSpec(...  22 us
    unnamed x96, local copies, waits for them, and re-layouts  19.1 us
    slice x8, local copies, waits for them, and re-layouts, body(): got[2 * edge_rows + cache_rows:].reshape(cap, tile_len, channels)  11.9 us
    slice x8, local copies, waits for them, and re-layouts, body(): got[edge_rows:2 * edge_rows].reshape(edge_shape)  10.5 us
    psum x1, blocking collectives, body(): lax.psum((jnp.sum(query_wide * query_wide, axis=-1), jnp.sum(keys_wide *...  9.27 us
    reshape x6, local copies, waits for them, and re-layouts, body(): got[edge_rows:2 * edge_rows].reshape(edge_shape)  5.71 us
  transfers between devices with their start and end apart: 8, of which 4 were waited for; matrix products, arithmetic and copies ran while one was open for 13% of the time, Pallas kernels for 0%

profile of v2, /device:TPU:226, one launch (start us, length us, event | category | flops | bytes accessed | tf_op | source)
XLA Modules:
  0.0 257.2 jit_solution(10947108314945976455)
XLA Ops:
  0.0 0.9 fusion.13
  4.4 1.4 multiply_reduce_fusion
  5.8 9.3 %all-reduce = (f32[3,128]{1,0:T(4,128)S(1)}, f32[3,128]{1,0:T(4,128)S(1)}) all-reduce(f32[3,128]{1,0:T(4,128)S(1)} %get-tuple-element.131, f32[3,128]{1,0:T(4,128)S(1)} %get-tuple-element.130), channel_id=1, replica_groups=mesh['sp'=128,'hd'=4] {'hd'}, use_global_device_ids=true, to_apply=%region_1.0 | all-reduce | flops 768 | bytes 6144 | tf_op jit(solution)/shard_map/psum | solution.py:86
  15.2 1.2 multiply_convert_fusion
  16.4 0.7 fusion.31
  17.2 0.8 fusion.30
  37.9 1.5 constant_dynamic-update-slice_fusion.1
  39.4 1.5 reshape.374
  40.9 1.5 reshape.394
  42.4 1.5 constant_dynamic-update-slice_fusion.15
  43.8 1.5 reshape.395
  45.3 0.7 constant_dynamic-update-slice_fusion.13
  46.7 0.7 constant_dynamic-update-slice_fusion.9
  47.4 0.7 constant_dynamic-update-slice_fusion.7
  48.8 0.7 constant_dynamic-update-slice_fusion.3
  49.5 1.4 constant_dynamic-update-slice_fusion
  51.5 1.5 constant_dynamic-update-slice_fusion.14
  53.6 0.7 constant_dynamic-update-slice_fusion.12
  56.2 0.7 constant_dynamic-update-slice_fusion.8
  60.0 0.7 constant_dynamic-update-slice_fusion.2
  66.3 1.1 bitcast_dynamic-update-slice_fusion.31
  67.4 1.1 bitcast_dynamic-update-slice_fusion.30
  68.5 1.1 bitcast_dynamic-update-slice_fusion.29
  69.6 1.1 bitcast_dynamic-update-slice_fusion.28
  70.7 2.8 %collective-permute-start.7 = (bf16[608,640]{1,0:T(8,128)(2,1)}, bf16[608,640]{1,0:T(8,128)(2,1)}, u32[]{:S(2)}, u32[]{:S(2)}) collective-permute-start(bf16[608,640]{1,0:T(8,128)(2,1)} %get-tuple-element.12), channel_id=1, source_target_pairs={{36,0},{40,4},{44,8},{48,12},{52,16},{56,20},{60,24},{64,28},{68,3... | collective-permute-start | bytes 2334728 | tf_op jit(solution)/shard_map/ppermute | solution.py:22
  73.5 3.3 %collective-permute-start.6 = (bf16[896,640]{1,0:T(8,128)(2,1)}, bf16[896,640]{1,0:T(8,128)(2,1)}, u32[]{:S(2)}, u32[]{:S(2)}) collective-permute-start(bf16[896,640]{1,0:T(8,128)(2,1)} %get-tuple-element.13), channel_id=1, source_target_pairs={{32,0},{36,4},{40,8},{44,12},{48,16},{52,20},{56,24},{60,28},{64,3... | collective-permute-start | bytes 3440648 | tf_op jit(solution)/shard_map/ppermute | solution.py:22
  76.8 2.9 %collective-permute-start.5 = (bf16[608,640]{1,0:T(8,128)(2,1)}, bf16[608,640]{1,0:T(8,128)(2,1)}, u32[]{:S(2)}, u32[]{:S(2)}) collective-permute-start(bf16[608,640]{1,0:T(8,128)(2,1)} %get-tuple-element.14), channel_id=1, source_target_pairs={{28,0},{32,4},{36,8},{40,12},{44,16},{48,20},{52,24},{56,28},{60,3... | collective-permute-start | bytes 2334728 | tf_op jit(solution)/shard_map/ppermute | solution.py:22
  79.7 9.0 %collective-permute-start.2 = (bf16[608,640]{1,0:T(8,128)(2,1)}, bf16[608,640]{1,0:T(8,128)(2,1)}, u32[]{:S(2)}, u32[]{:S(2)}) collective-permute-start(bf16[608,640]{1,0:T(8,128)(2,1)} %get-tuple-element.17), channel_id=1, source_target_pairs={{0,28},{4,32},{8,36},{12,40},{16,44},{20,48},{24,52},{28,56},{32,6... | collective-permute-start | bytes 2334728 | tf_op jit(solution)/shard_map/ppermute | solution.py:22
  88.7 1.9 collective-permute-start
  96.5 0.7 convert_element_type.62.wvalid_ref
  98.5 0.8 dynamic-slice_bitcast_fusion.3
  99.3 2.0 fusion.1.q_ref
  101.3 0.8 dynamic-slice_bitcast_fusion.1
  102.1 21.4 %collective-permute-done.7 = bf16[608,640]{1,0:T(8,128)(2,1)} collective-permute-done((bf16[608,640]{1,0:T(8,128)(2,1)}, bf16[608,640]{1,0:T(8,128)(2,1)}, u32[]{:S(2)}, u32[]{:S(2)}) %collective-permute-start.7) | collective-permute-done | bytes 778272 | tf_op jit(solution)/shard_map/ppermute | solution.py:22
  123.5 8.6 %collective-permute-start.4 = (bf16[704,640]{1,0:T(8,128)(2,1)}, bf16[704,640]{1,0:T(8,128)(2,1)}, u32[]{:S(2)}, u32[]{:S(2)}) collective-permute-start(bf16[704,640]{1,0:T(8,128)(2,1)} %get-tuple-element.15), channel_id=1, source_target_pairs={{4,0},{8,4},{12,8},{16,12},{20,16},{24,20},{28,24},{32,28},{36,32}... | collective-permute-start | bytes 2703368 | tf_op jit(solution)/shard_map/ppermute | solution.py:22
  132.1 0.9 fusion.29
  133.0 6.4 %collective-permute-done.5 = bf16[608,640]{1,0:T(8,128)(2,1)} collective-permute-done((bf16[608,640]{1,0:T(8,128)(2,1)}, bf16[608,640]{1,0:T(8,128)(2,1)}, u32[]{:S(2)}, u32[]{:S(2)}) %collective-permute-start.5) | collective-permute-done | bytes 778272 | tf_op jit(solution)/shard_map/ppermute | solution.py:22
  139.4 11.1 %collective-permute-start.3 = (bf16[704,640]{1,0:T(8,128)(2,1)}, bf16[704,640]{1,0:T(8,128)(2,1)}, u32[]{:S(2)}, u32[]{:S(2)}) collective-permute-start(bf16[704,640]{1,0:T(8,128)(2,1)} %get-tuple-element.16), channel_id=1, source_target_pairs={{0,4},{4,8},{8,12},{12,16},{16,20},{20,24},{24,28},{28,32},{32,36}... | collective-permute-start | bytes 2703368 | tf_op jit(solution)/shard_map/ppermute | solution.py:22
  150.5 0.9 fusion.28
  152.1 2.1 collective-permute-start.1
  154.2 0.9 fusion.27
  156.0 0.9 fusion.26
  160.1 1.1 fusion.25
  161.2 2.0 fusion.24
  163.2 2.0 fusion.23
  165.2 2.0 fusion.22
  167.2 0.7 constant_dynamic-update-slice_fusion.23
  168.0 1.7 fusion.21
  169.6 1.6 reshape.387
  171.2 38.5 %collective-permute-done.3 = bf16[704,640]{1,0:T(8,128)(2,1)} collective-permute-done((bf16[704,640]{1,0:T(8,128)(2,1)}, bf16[704,640]{1,0:T(8,128)(2,1)}, u32[]{:S(2)}, u32[]{:S(2)}) %collective-permute-start.3) | collective-permute-done | bytes 901152 | tf_op jit(solution)/shard_map/ppermute | solution.py:22
  209.7 1.7 fusion.20
  211.4 1.6 reshape.384
  213.0 1.6 reshape.403
  214.6 1.6 reshape.402
  216.2 1.3 fusion.19
  217.4 1.2 fusion.18
  218.6 1.1 fusion.15
  220.2 1.2 fusion.14
  222.4 2.5 fusion.17
  224.9 1.1 fusion.16
  226.1 4.2 %maximum_maximum_fusion = bf16[3,16,24,640]{3,2,1,0:T(8,128)(2,1)} fusion(bf16[3,4,4,640]{3,2,1,0:T(4,128)(2,1)S(1)} %reshape.396, bf16[3,4,16,640]{3,2,1,0:T(8,128)(2,1)S(1)} %bitcast.176, bf16[3,4,4,640]{3,2,1,0:T(4,128)(2,1)S(1)} %copy-done.21, bf16[3,8,4,640]{3,2,1,0:T(4,128)(2,1)S(1)} %copy-done.17, bf16[3,8,16,640]{3,2,1,0:T(8,128)(2,1)S(1)} %multiply_convert_fusion, ...), kind=kLoop, calls=%fused_computation | loop fusion | flops 13271040 | bytes 2949120 | tf_op jit(solution)/shard_map/concatenate | solution.py:150
  230.3 4.2 %maximum_maximum_fusion.1 = bf16[3,16,24,640]{3,2,1,0:T(8,128)(2,1)} fusion(bf16[3,4,4,640]{3,2,1,0:T(4,128)(2,1)S(1)} %copy-done.23, bf16[3,4,16,640]{3,2,1,0:T(8,128)(2,1)S(1)} %bitcast.174, bf16[3,4,4,640]{3,2,1,0:T(4,128)(2,1)S(1)} %copy-done.24, bf16[3,8,4,640]{3,2,1,0:T(4,128)(2,1)S(1)} %copy-done.18, bf16[3,8,16,640]{3,2,1,0:T(8,128)(2,1)S(1)} %bitcast.150, ...), kind=kLoop, calls=%fused_computation.1 | loop fusion | flops 13271040 | bytes 2949120 | tf_op jit(solution)/shard_map/concatenate | solution.py:151
  234.5 0.7 broadcast_in_dim.5
  235.2 22.0 %shard_map.91 = bf16[384,640]{1,0:T(8,128)(2,1)} custom-call(s32[1,1152]{1,0:T(1,128)} %convert_element_type.62.wvalid_ref, s32[1,2304]{1,0:T(1,128)} %bitcast.178, bf16[384,640]{1,0:T(8,128)(2,1)} %fusion.1.q_ref, bf16[1152,640]{1,0:T(8,128)(2,1)} %bitcast.145, bf16[2304,640]{1,0:T(8,128)(2,1)} %bitcast.152, bf16[1152,640]{1,0:T(8,128)(2,1)} %bitcast.146, ...), custom_call_target="tpu_custom_call" | custom-call | tf_op jit(solution)/shard_map/pallas_call | solution.py:195
  (127 shorter events, 14.3 us)
Async XLA Ops:
  0.0 17.2 %copy-start.2 = (bf16[1,3,128,640]{3,2,1,0:T(8,128)(2,1)S(1)}, bf16[1,3,128,640]{3,2,1,0:T(8,128)(2,1)}, u32[]{:S(2)}) copy-start(bf16[1,3,128,640]{3,2,1,0:T(8,128)(2,1)} %param.11) | copy-start | bytes 1474564
  37.9 28.4 %copy-start = (bf16[1,8,128,640]{3,2,1,0:T(8,128)(2,1)S(1)}, bf16[1,8,128,640]{3,2,1,0:T(8,128)(2,1)}, u32[]{:S(2)}) copy-start(bf16[1,8,128,640]{3,2,1,0:T(8,128)(2,1)} %param.12) | copy-start | bytes 3932164
  58.7 9.8 %copy-start.1 = (bf16[1,8,128,640]{3,2,1,0:T(8,128)(2,1)S(1)}, bf16[1,8,128,640]{3,2,1,0:T(8,128)(2,1)}, u32[]{:S(2)}) copy-start(bf16[1,8,128,640]{3,2,1,0:T(8,128)(2,1)} %param.13) | copy-start | bytes 3932164
  68.5 22.1 %copy-start.29 = (s32[1,4]{1,0:T(1,128)S(1)}, s32[1,4]{1,0:T(1,128)}, u32[]{:S(2)}) copy-start(s32[1,4]{1,0:T(1,128)} %param.16) | copy-start | bytes 52
  68.5 24.1 %copy-start.28 = (s32[128,9,2]{0,2,1:T(2,128)S(1)}, s32[128,9,2]{0,2,1:T(2,128)}, u32[]{:S(2)}) copy-start(s32[128,9,2]{0,2,1:T(2,128)} %param.17) | copy-start | bytes 27652
  68.5 30.8 %copy-start.30 = (f32[640]{0:T(1024)S(1)}, f32[640]{0:T(1024)}, u32[]{:S(2)}) copy-start(f32[640]{0:T(1024)} %param.14) | copy-start | bytes 7684
  70.7 52.8 %collective-permute-start.7 = (bf16[608,640]{1,0:T(8,128)(2,1)}, bf16[608,640]{1,0:T(8,128)(2,1)}, u32[]{:S(2)}, u32[]{:S(2)}) collective-permute-start(bf16[608,640]{1,0:T(8,128)(2,1)} %get-tuple-element.12), channel_id=1, source_target_pairs={{36,0},{40,4},{44,8},{48,12},{52,16},{56,20},{60,24},{64,28},{68,3... | collective-permute-start | bytes 2334728 | tf_op jit(solution)/shard_map/ppermute | solution.py:22
  73.5 146.7 %collective-permute-start.6 = (bf16[896,640]{1,0:T(8,128)(2,1)}, bf16[896,640]{1,0:T(8,128)(2,1)}, u32[]{:S(2)}, u32[]{:S(2)}) collective-permute-start(bf16[896,640]{1,0:T(8,128)(2,1)} %get-tuple-element.13), channel_id=1, source_target_pairs={{32,0},{36,4},{40,8},{44,12},{48,16},{52,20},{56,24},{60,28},{64,3... | collective-permute-start | bytes 3440648 | tf_op jit(solution)/shard_map/ppermute | solution.py:22
  76.8 62.6 %collective-permute-start.5 = (bf16[608,640]{1,0:T(8,128)(2,1)}, bf16[608,640]{1,0:T(8,128)(2,1)}, u32[]{:S(2)}, u32[]{:S(2)}) collective-permute-start(bf16[608,640]{1,0:T(8,128)(2,1)} %get-tuple-element.14), channel_id=1, source_target_pairs={{28,0},{32,4},{36,8},{40,12},{44,16},{48,20},{52,24},{56,28},{60,3... | collective-permute-start | bytes 2334728 | tf_op jit(solution)/shard_map/ppermute | solution.py:22
  79.7 72.3 %collective-permute-start.2 = (bf16[608,640]{1,0:T(8,128)(2,1)}, bf16[608,640]{1,0:T(8,128)(2,1)}, u32[]{:S(2)}, u32[]{:S(2)}) collective-permute-start(bf16[608,640]{1,0:T(8,128)(2,1)} %get-tuple-element.17), channel_id=1, source_target_pairs={{0,28},{4,32},{8,36},{12,40},{16,44},{20,48},{24,52},{28,56},{32,6... | collective-permute-start | bytes 2334728 | tf_op jit(solution)/shard_map/ppermute | solution.py:22
  88.7 67.3 %collective-permute-start = (bf16[608,640]{1,0:T(8,128)(2,1)}, bf16[608,640]{1,0:T(8,128)(2,1)}, u32[]{:S(2)}, u32[]{:S(2)}) collective-permute-start(bf16[608,640]{1,0:T(8,128)(2,1)} %get-tuple-element.11), channel_id=1, source_target_pairs={{0,36},{4,40},{8,44},{12,48},{16,52},{20,56},{24,60},{28,64},{32,6... | collective-permute-start | bytes 2334728 | tf_op jit(solution)/shard_map/ppermute | solution.py:22
  123.5 44.5 %collective-permute-start.4 = (bf16[704,640]{1,0:T(8,128)(2,1)}, bf16[704,640]{1,0:T(8,128)(2,1)}, u32[]{:S(2)}, u32[]{:S(2)}) collective-permute-start(bf16[704,640]{1,0:T(8,128)(2,1)} %get-tuple-element.15), channel_id=1, source_target_pairs={{4,0},{8,4},{12,8},{16,12},{20,16},{24,20},{28,24},{32,28},{36,32}... | collective-permute-start | bytes 2703368 | tf_op jit(solution)/shard_map/ppermute | solution.py:22
  139.4 70.3 %collective-permute-start.3 = (bf16[704,640]{1,0:T(8,128)(2,1)}, bf16[704,640]{1,0:T(8,128)(2,1)}, u32[]{:S(2)}, u32[]{:S(2)}) collective-permute-start(bf16[704,640]{1,0:T(8,128)(2,1)} %get-tuple-element.16), channel_id=1, source_target_pairs={{0,4},{4,8},{8,12},{12,16},{16,20},{20,24},{24,28},{28,32},{32,36}... | collective-permute-start | bytes 2703368 | tf_op jit(solution)/shard_map/ppermute | solution.py:22
  152.1 66.6 %collective-permute-start.1 = (bf16[896,640]{1,0:T(8,128)(2,1)}, bf16[896,640]{1,0:T(8,128)(2,1)}, u32[]{:S(2)}, u32[]{:S(2)}) collective-permute-start(bf16[896,640]{1,0:T(8,128)(2,1)} %get-tuple-element.18), channel_id=1, source_target_pairs={{0,32},{4,36},{8,40},{12,44},{16,48},{20,52},{24,56},{28,60},{32,6... | collective-permute-start | bytes 3440648 | tf_op jit(solution)/shard_map/ppermute | solution.py:22
  216.1 3.6 %copy-start.5 = (bf16[9,2,128,640]{3,2,1,0:T(8,128)(2,1)S(1)}, bf16[9,2,128,640]{3,2,1,0:T(8,128)(2,1)}, u32[]{:S(2)}) copy-start(bf16[9,2,128,640]{3,2,1,0:T(8,128)(2,1)} %constant_dynamic-update-slice_fusion.23) | copy-start | bytes 8847364
  216.1 3.7 %copy-start.12 = (bf16[256,640]{1,0:T(8,128)(2,1)S(1)}, bf16[256,640]{1,0:T(8,128)(2,1)}, u32[]{:S(2)}) copy-start(bf16[256,640]{1,0:T(8,128)(2,1)} %get-tuple-element.64) | copy-start | bytes 983044
  216.1 3.8 %copy-start.15 = (bf16[1,128,640]{2,1,0:T(8,128)(2,1)S(1)}, bf16[1,128,640]{2,1,0:T(8,128)(2,1)}, u32[]{:S(2)}) copy-start(bf16[1,128,640]{2,1,0:T(8,128)(2,1)} %get-tuple-element.9) | copy-start | bytes 491524
  216.1 3.8 %copy-start.16 = (bf16[1,128,640]{2,1,0:T(8,128)(2,1)S(1)}, bf16[1,128,640]{2,1,0:T(8,128)(2,1)}, u32[]{:S(2)}) copy-start(bf16[1,128,640]{2,1,0:T(8,128)(2,1)} %get-tuple-element.10) | copy-start | bytes 491524
  217.4 2.7 %copy-start.11 = (bf16[256,640]{1,0:T(8,128)(2,1)S(1)}, bf16[256,640]{1,0:T(8,128)(2,1)}, u32[]{:S(2)}) copy-start(bf16[256,640]{1,0:T(8,128)(2,1)} %get-tuple-element.62) | copy-start | bytes 983044
  219.8 1.6 copy-start.10
  219.9 1.6 copy-start.9
  220.0 1.7 copy-start.13
  220.0 1.7 copy-start.14
  220.2 1.7 copy-start.8
  221.4 1.0 copy-start.7
  221.5 3.5 %copy-start.6 = (bf16[9,2,128,640]{3,2,1,0:T(8,128)(2,1)}, bf16[9,2,128,640]{3,2,1,0:T(8,128)(2,1)S(1)}, u32[]{:S(2)}) copy-start(bf16[9,2,128,640]{3,2,1,0:T(8,128)(2,1)S(1)} %constant_dynamic-update-slice_fusion.16) | copy-start | bytes 8847364
  221.6 4.5 %copy-start.17 = (bf16[3,8,4,640]{3,2,1,0:T(4,128)(2,1)S(1)}, bf16[3,8,4,640]{3,2,1,0:T(4,128)(2,1)}, u32[]{:S(2)}) copy-start(bf16[3,8,4,640]{3,2,1,0:T(4,128)(2,1)} %reshape.387) | copy-start | bytes 368644
  221.6 4.5 %copy-start.20 = (bf16[3,8,4,640]{3,2,1,0:T(4,128)(2,1)S(1)}, bf16[3,8,4,640]{3,2,1,0:T(4,128)(2,1)}, u32[]{:S(2)}) copy-start(bf16[3,8,4,640]{3,2,1,0:T(4,128)(2,1)} %reshape.384) | copy-start | bytes 368644
  221.6 4.5 %copy-start.21 = (bf16[3,4,4,640]{3,2,1,0:T(4,128)(2,1)S(1)}, bf16[3,4,4,640]{3,2,1,0:T(4,128)(2,1)}, u32[]{:S(2)}) copy-start(bf16[3,4,4,640]{3,2,1,0:T(4,128)(2,1)} %reshape.390) | copy-start | bytes 184324
  221.6 4.5 %copy-start.22 = (bf16[3,4,4,640]{3,2,1,0:T(4,128)(2,1)S(1)}, bf16[3,4,4,640]{3,2,1,0:T(4,128)(2,1)}, u32[]{:S(2)}) copy-start(bf16[3,4,4,640]{3,2,1,0:T(4,128)(2,1)} %reshape.381) | copy-start | bytes 184324
  221.6 4.5 %copy-start.26 = (bf16[3,4,4,640]{3,2,1,0:T(4,128)(2,1)S(1)}, bf16[3,4,4,640]{3,2,1,0:T(4,128)(2,1)}, u32[]{:S(2)}) copy-start(bf16[3,4,4,640]{3,2,1,0:T(4,128)(2,1)} %reshape.375) | copy-start | bytes 184324
  221.9 8.4 %copy-start.3 = (bf16[1,3,128,640]{3,2,1,0:T(8,128)(2,1)S(1)}, bf16[1,3,128,640]{3,2,1,0:T(8,128)(2,1)}, u32[]{:S(2)}) copy-start(bf16[1,3,128,640]{3,2,1,0:T(8,128)(2,1)} %param.11) | copy-start | bytes 1474564
  221.9 8.4 %copy-start.18 = (bf16[3,8,4,640]{3,2,1,0:T(4,128)(2,1)S(1)}, bf16[3,8,4,640]{3,2,1,0:T(4,128)(2,1)}, u32[]{:S(2)}) copy-start(bf16[3,8,4,640]{3,2,1,0:T(4,128)(2,1)} %reshape.403) | copy-start | bytes 368644
  221.9 8.4 %copy-start.19 = (bf16[3,8,4,640]{3,2,1,0:T(4,128)(2,1)S(1)}, bf16[3,8,4,640]{3,2,1,0:T(4,128)(2,1)}, u32[]{:S(2)}) copy-start(bf16[3,8,4,640]{3,2,1,0:T(4,128)(2,1)} %reshape.402) | copy-start | bytes 368644
  222.0 8.4 %copy-start.23 = (bf16[3,4,4,640]{3,2,1,0:T(4,128)(2,1)S(1)}, bf16[3,4,4,640]{3,2,1,0:T(4,128)(2,1)}, u32[]{:S(2)}) copy-start(bf16[3,4,4,640]{3,2,1,0:T(4,128)(2,1)} %reshape.406) | copy-start | bytes 184324
  222.0 8.4 %copy-start.24 = (bf16[3,4,4,640]{3,2,1,0:T(4,128)(2,1)S(1)}, bf16[3,4,4,640]{3,2,1,0:T(4,128)(2,1)}, u32[]{:S(2)}) copy-start(bf16[3,4,4,640]{3,2,1,0:T(4,128)(2,1)} %reshape.404) | copy-start | bytes 184324
  222.0 8.4 %copy-start.25 = (bf16[3,4,4,640]{3,2,1,0:T(4,128)(2,1)S(1)}, bf16[3,4,4,640]{3,2,1,0:T(4,128)(2,1)}, u32[]{:S(2)}) copy-start(bf16[3,4,4,640]{3,2,1,0:T(4,128)(2,1)} %reshape.401) | copy-start | bytes 184324
  222.0 8.4 %copy-start.27 = (bf16[3,4,4,640]{3,2,1,0:T(4,128)(2,1)S(1)}, bf16[3,4,4,640]{3,2,1,0:T(4,128)(2,1)}, u32[]{:S(2)}) copy-start(bf16[3,4,4,640]{3,2,1,0:T(4,128)(2,1)} %reshape.399) | copy-start | bytes 184324
  222.4 12.1 %copy-start.4 = (bf16[9,2,128,640]{3,2,1,0:T(8,128)(2,1)}, bf16[9,2,128,640]{3,2,1,0:T(8,128)(2,1)S(1)}, u32[]{:S(2)}) copy-start(bf16[9,2,128,640]{3,2,1,0:T(8,128)(2,1)S(1)} %constant_dynamic-update-slice_fusion.24) | copy-start | bytes 8847364

commit v3 on v1

v3 whole, which is shorter than its diff:
```python
import jax
import jax.numpy as jnp
from jax import lax
from jax.sharding import PartitionSpec as P
from jax.experimental import pallas as pl
from jax.experimental.pallas import tpu as pltpu

HS = 128
TH = 8
TW = 16
GW = 8
HALO = 4


EPSILON = 1e-06
MASKED = -1e30
STEPS = [(r, c) for r in (-1, 0, 1) for c in (-1, 0, 1)]


def shifted(x, axis, by):
    size = lax.axis_size(axis)
    pairs = [(i, i + by) for i in range(size) if 0 <= i + by < size]
    return lax.ppermute(x, axis, pairs)


def edge_part(grid, row_step, col_step):
    if row_step == -1:
        grid = grid[:, :, TH - HALO :]
    elif row_step == 1:
        grid = grid[:, :, :HALO]
    if col_step == -1:
        grid = grid[:, :, :, TW - HALO :]
    elif col_step == 1:
        grid = grid[:, :, :, :HALO]
    return grid


def slot_of(row_step, col_step):
    return 3 * (row_step + 1) + (col_step + 1)


def normalize(tensor, gain, row_total, width_all):
    wide = tensor.astype(jnp.float32)
    factor = lax.rsqrt(row_total / width_all + EPSILON)
    return (wide * factor[..., None] * gain).astype(jnp.bfloat16)


def attend_kernel(wvalid_ref, cvalid_ref, q_ref, wk_ref, wv_ref, *rest):
    cache_refs = rest[:-1]
    o_ref = rest[-1]
    cap_rows = cache_refs[0].shape[0] // 2
    tile_len = cache_refs[0].shape[1]
    score_scale = HS ** (-0.5)
    dims = (((1,), (1,)), ((), ()))
    head_q = q_ref[...]
    cache_k = jnp.concatenate(
        [ref[:cap_rows].reshape(cap_rows * tile_len, HS) for ref in cache_refs], axis=0
    )
    cache_v = jnp.concatenate(
        [ref[cap_rows:].reshape(cap_rows * tile_len, HS) for ref in cache_refs], axis=0
    )
    window_scores = (
        lax.dot_general(head_q, wk_ref[...], dims, preferred_element_type=jnp.float32)
        * score_scale
    )
    window_scores = jnp.where(wvalid_ref[...] > 0, window_scores, MASKED)
    cache_scores = (
        lax.dot_general(head_q, cache_k, dims, preferred_element_type=jnp.float32) * score_scale
    )
    cache_scores = jnp.where(cvalid_ref[...] > 0, cache_scores, MASKED)
    row_top = jnp.maximum(
        jnp.max(window_scores, axis=1, keepdims=True), jnp.max(cache_scores, axis=1, keepdims=True)
    )
    window_exp = jnp.exp(window_scores - row_top)
    cache_exp = jnp.exp(cache_scores - row_top)
    row_total = jnp.sum(window_exp, axis=1, keepdims=True) + jnp.sum(
        cache_exp, axis=1, keepdims=True
    )
    window_probs = (window_exp / row_total).astype(jnp.bfloat16)
    cache_probs = (cache_exp / row_total).astype(jnp.bfloat16)
    mixed_out = jnp.dot(window_probs, wv_ref[...], preferred_element_type=jnp.float32) + jnp.dot(
        cache_probs, cache_v, preferred_element_type=jnp.float32
    )
    o_ref[...] = mixed_out.astype(jnp.bfloat16)


def body(
    query, keys, values, cache_keys, cache_values, q_gain, k_gain, window_margins, cache_frames
):
    frames_now = query.shape[1]
    tile_len = query.shape[2]
    channels = query.shape[3]
    width_all = channels * lax.axis_size("hd")
    own_place = lax.axis_index("sp")
    tile_count = lax.axis_size("sp")
    grid_rows = tile_count // GW
    own_cache_k = cache_keys[0]
    own_cache_v = cache_values[0]
    cap = cache_frames.shape[2]

    def blocks_for(target, slot_index):
        safe_target = jnp.clip(target, 0, tile_count - 1)
        listed = lax.dynamic_index_in_dim(cache_frames, safe_target, 0, keepdims=False)[slot_index]
        wanted = jnp.maximum(listed, 0)
        picked = [
            lax.dynamic_index_in_dim(own_cache_k, wanted[c], 0, keepdims=False) for c in range(cap)
        ] + [
            lax.dynamic_index_in_dim(own_cache_v, wanted[c], 0, keepdims=False) for c in range(cap)
        ]
        return jnp.stack(picked)

    cache_in = {}
    for row_step, col_step in STEPS:
        if (row_step, col_step) != (0, 0):
            shift_by = -(row_step * GW + col_step)
            packed = blocks_for(own_place + shift_by, slot_of(row_step, col_step))
            cache_in[row_step, col_step] = shifted(packed, "sp", shift_by)
    cache_in[0, 0] = blocks_for(own_place, 4)

    query_wide = query[0].astype(jnp.float32)
    keys_wide = keys[0].astype(jnp.float32)
    query_total, keys_total = lax.psum(
        (jnp.sum(query_wide * query_wide, axis=-1), jnp.sum(keys_wide * keys_wide, axis=-1)),
        "hd",
    )
    query_normed = normalize(query[0], q_gain, query_total, width_all)
    keys_normed = normalize(keys[0], k_gain, keys_total, width_all)
    key_grid = keys_normed.reshape(frames_now, TH, TW, channels)
    value_grid = values[0].reshape(frames_now, TH, TW, channels)
    both_grid = jnp.stack([key_grid, value_grid])

    edge_in = {}
    for row_step, col_step in STEPS:
        if (row_step, col_step) != (0, 0):
            shift_by = -(row_step * GW + col_step)
            edge_in[row_step, col_step] = shifted(
                edge_part(both_grid, row_step, col_step), "sp", shift_by
            )
    edge_in[0, 0] = both_grid
    bands = []
    for row_step in (-1, 0, 1):
        bands.append(
            jnp.concatenate([edge_in[row_step, col_step] for col_step in (-1, 0, 1)], axis=3)
        )
    window = jnp.concatenate(bands, axis=2)
    flat_wk = window[0].reshape(-1, channels)
    flat_wv = window[1].reshape(-1, channels)
    flat_q = query_normed.reshape(-1, channels)
    margins = window_margins[0]
    tile_row = own_place // GW
    tile_col = own_place % GW
    row_pos = jnp.arange(TH + 2 * HALO, dtype=jnp.int32)
    row_global = tile_row * TH - HALO + row_pos
    row_valid = (
        (row_global >= 0)
        & (row_global < grid_rows * TH)
        & (row_pos >= HALO - margins[0])
        & (row_pos < HALO + TH + margins[1])
    )
    col_pos = jnp.arange(TW + 2 * HALO, dtype=jnp.int32)
    col_global = tile_col * TW - HALO + col_pos
    col_valid = (
        (col_global >= 0)
        & (col_global < GW * TW)
        & (col_pos >= HALO - margins[2])
        & (col_pos < HALO + TW + margins[3])
    )
    window_valid = jnp.broadcast_to(
        (row_valid[:, None] & col_valid[None, :])[None], (frames_now, TH + 2 * HALO, TW + 2 * HALO)
    ).reshape(-1)
    own_listed = lax.dynamic_index_in_dim(cache_frames, own_place, 0, keepdims=False)
    cache_valid = jnp.broadcast_to(
        (own_listed >= 0)[:, :, None], (9, own_listed.shape[1], tile_len)
    ).reshape(-1)

    head_count = channels // HS
    query_rows = flat_q.shape[0]
    window_len = flat_wk.shape[0]
    cache_len = cache_valid.shape[0]
    cache_list = [cache_in[step] for step in STEPS]
    heads_out = pl.pallas_call(
        attend_kernel,
        grid=(head_count,),
        in_specs=[
            pl.BlockSpec((1, window_len), lambda h: (0, 0)),
            pl.BlockSpec((1, cache_len), lambda h: (0, 0)),
            pl.BlockSpec((query_rows, HS), lambda h: (0, h)),
            pl.BlockSpec((window_len, HS), lambda h: (0, h)),
            pl.BlockSpec((window_len, HS), lambda h: (0, h)),
        ]
        + [pl.BlockSpec((2 * cap, tile_len, HS), lambda h: (0, 0, h)) for _ in cache_list],
        out_specs=pl.BlockSpec((query_rows, HS), lambda h: (0, h)),
        out_shape=jax.ShapeDtypeStruct((query_rows, channels), jnp.bfloat16),
        compiler_params=pltpu.CompilerParams(vmem_limit_bytes=60 * 1024 * 1024),
    )(
        window_valid.astype(jnp.int32)[None, :],
        cache_valid.astype(jnp.int32)[None, :],
        flat_q,
        flat_wk,
        flat_wv,
        *cache_list,
    )
    result = heads_out.reshape(1, frames_now, tile_len, channels)
    return result


def solution(mesh):
    return jax.shard_map(
        body,
        mesh=mesh,
        in_specs=(
            P("sp", None, None, "hd"),
            P("sp", None, None, "hd"),
            P("sp", None, None, "hd"),
            P("sp", None, None, "hd"),
            P("sp", None, None, "hd"),
            P("hd"),
            P("hd"),
            P("sp", None),
            P(),
        ),
        out_specs=P("sp", None, None, "hd"),
        check_vma=False,
    )
```

time: 308 us -> 263 us (0.85)
  starting transfers between devices: 148 us -> 87.6 us
  local copies, waits for them, and re-layouts: 47.3 us -> 13.2 us
  between operations: 3.11 us -> 36.8 us
  waiting for transfers between devices: 59.5 us -> 72.9 us
    ppermute x32 -> x16, starting transfers between devices: 148 us -> 87.6 us  [shifted(): return lax.ppermute(x, axis, pairs)]
    gather x18 -> x0, local copies, waits for them, and re-layouts: 23 us -> none  [blocks_for(): return (own_cache_k[wanted], own_cache_v[wanted])]
    ppermute x32 -> x16, waiting for transfers between devices: 59.5 us -> 72.9 us  [shifted(): return lax.ppermute(x, axis, pairs)]
    another operation x0 -> x12, other arithmetic: none -> 12.1 us  [the longest x9 8.65 us: blocks_for(): return jnp.stack(picked)]
    unnamed x65 -> x35, local copies, waits for them, and re-layouts: 12.4 us -> 5.27 us
    concatenate x2 -> x1, other arithmetic: 10.1 us -> 3.63 us  [body(): window = jnp.concatenate(bands, axis=2)]
    slice x6, local copies, waits for them, and re-layouts: 8.06 us -> 4.82 us  [the longest x5 2.93 us: blocks_for(): wanted[c]]
  transfers between devices with their start and end apart: 32 -> 16, of which waited for: 7 -> 3; matrix products, arithmetic and copies ran while one was open for 19% -> 9% of each run, Pallas kernels for 0% -> 0%
where the time goes in v3:
time: 263 us; the launch traced here: 261 us
  starting transfers between devices  87.6 us (33%)
  waiting for transfers between devices  72.9 us (28%)
  between operations  36.8 us (14%)
  Pallas kernels  22.1 us (8%)
  other arithmetic  19.7 us (7%)
  local copies, waits for them, and re-layouts  13.2 us (5%)
  blocking collectives  8.99 us (3%)
    ppermute x16, starting transfers between devices, shifted(): return lax.ppermute(x, axis, pairs)  87.6 us
    ppermute x16, waiting for transfers between devices, shifted(): return lax.ppermute(x, axis, pairs)  72.9 us
    pallas_call x1, Pallas kernels, body(): pl.pallas_call(attend_kernel, grid=(head_count,), in_specs=[pl.BlockSpec(...  22.1 us
    psum x1, blocking collectives, body(): lax.psum((jnp.sum(query_wide * query_wide, axis=-1), jnp.sum(keys_wide *...  8.99 us
    another operation x9, other arithmetic, blocks_for(): return jnp.stack(picked)  8.65 us
    unnamed x35, local copies, waits for them, and re-layouts  5.27 us
  transfers between devices with their start and end apart: 16, of which 3 were waited for; matrix products, arithmetic and copies ran while one was open for 9% of the time, Pallas kernels for 0%

profile of v3, /device:TPU:206, one launch (start us, length us, event | category | flops | bytes accessed | tf_op | source)
XLA Modules:
  0.0 261.4 jit_solution(13808714179063026835)
XLA Ops:
  0.0 1.5 multiply_reduce_fusion
  1.5 9.0 %all-reduce = (f32[3,128]{1,0:T(4,128)S(1)}, f32[3,128]{1,0:T(4,128)S(1)}) all-reduce(f32[3,128]{1,0:T(4,128)S(1)} %get-tuple-element.93, f32[3,128]{1,0:T(4,128)S(1)} %get-tuple-element.92), channel_id=1, replica_groups=mesh['sp'=128,'hd'=4] {'hd'}, use_global_device_ids=true, to_apply=%region_1.2 | all-reduce | flops 768 | bytes 6144 | tf_op jit(solution)/shard_map/psum | solution.py:122
  10.5 0.1 mul.75
  10.6 1.3 multiply_convert_fusion
  11.9 1.3 fusion.6
  13.2 4.0 %collective-permute-start = (bf16[2,3,4,4,640]{4,3,2,1,0:T(4,128)(2,1)S(1)}, bf16[2,3,4,4,640]{4,3,2,1,0:T(4,128)(2,1)S(1)}, u32[]{:S(2)}, u32[]{:S(2)}) collective-permute-start(bf16[2,3,4,4,640]{4,3,2,1,0:T(4,128)(2,1)S(1)} %get-tuple-element.45), channel_id=1, source_target_pairs={{0,36},{4,40},{8,44},{12,48},{16,52},{20,56},{24,60},{28,64},{32,6... | collective-permute-start | bytes 368648 | tf_op jit(solution)/shard_map/ppermute | solution.py:23
  17.3 10.6 %collective-permute-start.2 = (bf16[2,3,4,4,640]{4,3,2,1,0:T(4,128)(2,1)S(1)}, bf16[2,3,4,4,640]{4,3,2,1,0:T(4,128)(2,1)S(1)}, u32[]{:S(2)}, u32[]{:S(2)}) collective-permute-start(bf16[2,3,4,4,640]{4,3,2,1,0:T(4,128)(2,1)S(1)} %get-tuple-element.46), channel_id=1, source_target_pairs={{0,28},{4,32},{8,36},{12,40},{16,44},{20,48},{24,52},{28,56},{32,6... | collective-permute-start | bytes 368648 | tf_op jit(solution)/shard_map/ppermute | solution.py:23
  27.8 1.9 collective-permute-start.5
  29.8 7.5 %collective-permute-start.7 = (bf16[2,3,4,4,640]{4,3,2,1,0:T(4,128)(2,1)S(1)}, bf16[2,3,4,4,640]{4,3,2,1,0:T(4,128)(2,1)}, u32[]{:S(2)}, u32[]{:S(2)}) collective-permute-start(bf16[2,3,4,4,640]{4,3,2,1,0:T(4,128)(2,1)S(1)} %get-tuple-element.48), channel_id=1, source_target_pairs={{36,0},{40,4},{44,8},{48,12},{52,16},{56,20},{60,24},{64,28},{68,3... | collective-permute-start | bytes 368648 | tf_op jit(solution)/shard_map/ppermute | solution.py:23
  37.3 1.1 fusion.4
  38.4 3.1 %collective-permute-start.3 = (bf16[2,3,8,4,640]{4,3,2,1,0:T(4,128)(2,1)}, bf16[2,3,8,4,640]{4,3,2,1,0:T(4,128)(2,1)}, u32[]{:S(2)}, u32[]{:S(2)}) collective-permute-start(bf16[2,3,8,4,640]{4,3,2,1,0:T(4,128)(2,1)} %get-tuple-element.51), channel_id=1, source_target_pairs={{0,4},{4,8},{8,12},{12,16},{16,20},{20,24},{24,28},{28,32},{32,36}... | collective-permute-start | bytes 737288 | tf_op jit(solution)/shard_map/ppermute | solution.py:23
  41.6 0.1 fusion.18
  41.7 0.6 fusion.20
  47.3 0.6 fusion.28
  50.3 0.6 fusion.22
  56.0 0.6 fusion.24
  61.6 0.6 fusion.26
  67.2 1.0 fusion.3
  68.3 0.6 fusion.29
  70.2 0.1 constant_dynamic-slice_fusion.9
  70.2 0.1 copy.14
  81.7 0.0 copy-start.2
  81.7 0.5 dynamic-slice_bitcast_fusion.1
  82.2 0.8 copy-done.2
  83.0 0.5 dynamic-slice_bitcast_fusion.3
  84.7 0.1 and_convert_fusion
  84.8 1.0 pad_maximum_fusion.8
  85.8 0.9 pad_maximum_fusion.7
  86.7 0.9 pad_maximum_fusion.6
  87.7 0.9 pad_maximum_fusion.5
  88.6 1.0 pad_maximum_fusion.2
  89.6 0.9 pad_maximum_fusion.1
  90.5 0.0 collective-permute-done
  90.6 7.2 %collective-permute-start.4 = (bf16[2,3,8,4,640]{4,3,2,1,0:T(4,128)(2,1)}, bf16[2,3,8,4,640]{4,3,2,1,0:T(4,128)(2,1)}, u32[]{:S(2)}, u32[]{:S(2)}) collective-permute-start(bf16[2,3,8,4,640]{4,3,2,1,0:T(4,128)(2,1)} %get-tuple-element.52), channel_id=1, source_target_pairs={{4,0},{8,4},{12,8},{16,12},{20,16},{24,20},{28,24},{32,28},{36,32}... | collective-permute-start | bytes 737288 | tf_op jit(solution)/shard_map/ppermute | solution.py:23
  97.8 0.9 pad_maximum_fusion
  98.7 6.9 %collective-permute-start.8 = (bf16[4,128,640]{2,1,0:T(8,128)(2,1)}, bf16[4,128,640]{2,1,0:T(8,128)(2,1)S(1)}, u32[]{:S(2)}, u32[]{:S(2)}) collective-permute-start(bf16[4,128,640]{2,1,0:T(8,128)(2,1)} %pad_maximum_fusion), channel_id=1, source_target_pairs={{0,36},{4,40},{8,44},{12,48},{16,52},{20,56},{24,60},{28,64},{32,6... | collective-permute-start | bytes 1966088 | tf_op jit(solution)/shard_map/ppermute | solution.py:23
  105.7 0.0 collective-permute-done.5
  105.7 4.0 %collective-permute-start.9 = (bf16[4,128,640]{2,1,0:T(8,128)(2,1)}, bf16[4,128,640]{2,1,0:T(8,128)(2,1)S(1)}, u32[]{:S(2)}, u32[]{:S(2)}) collective-permute-start(bf16[4,128,640]{2,1,0:T(8,128)(2,1)} %pad_maximum_fusion.1), channel_id=1, source_target_pairs={{0,32},{4,36},{8,40},{12,44},{16,48},{20,52},{24,56},{28,60},{32,6... | collective-permute-start | bytes 1966088 | tf_op jit(solution)/shard_map/ppermute | solution.py:23
  109.7 6.8 %collective-permute-start.10 = (bf16[4,128,640]{2,1,0:T(8,128)(2,1)}, bf16[4,128,640]{2,1,0:T(8,128)(2,1)S(1)}, u32[]{:S(2)}, u32[]{:S(2)}) collective-permute-start(bf16[4,128,640]{2,1,0:T(8,128)(2,1)} %pad_maximum_fusion.2), channel_id=1, source_target_pairs={{0,28},{4,32},{8,36},{12,40},{16,44},{20,48},{24,52},{28,56},{32,6... | collective-permute-start | bytes 1966088 | tf_op jit(solution)/shard_map/ppermute | solution.py:23
  116.5 1.0 pad_maximum_fusion.4.rest_4_
  117.5 0.0 collective-permute-done.3
  117.5 4.2 %collective-permute-start.1 = (bf16[2,3,4,16,640]{4,3,2,1,0:T(8,128)(2,1)}, bf16[2,3,4,16,640]{4,3,2,1,0:T(8,128)(2,1)}, u32[]{:S(2)}, u32[]{:S(2)}) collective-permute-start(bf16[2,3,4,16,640]{4,3,2,1,0:T(8,128)(2,1)} %get-tuple-element.49), channel_id=1, source_target_pairs={{0,32},{4,36},{8,40},{12,44},{16,48},{20,52},{24,56},{28,60},{32,6... | collective-permute-start | bytes 1474568 | tf_op jit(solution)/shard_map/ppermute | solution.py:23
  121.7 3.1 %collective-permute-start.6 = (bf16[2,3,4,16,640]{4,3,2,1,0:T(8,128)(2,1)}, bf16[2,3,4,16,640]{4,3,2,1,0:T(8,128)(2,1)}, u32[]{:S(2)}, u32[]{:S(2)}) collective-permute-start(bf16[2,3,4,16,640]{4,3,2,1,0:T(8,128)(2,1)} %get-tuple-element.50), channel_id=1, source_target_pairs={{32,0},{36,4},{40,8},{44,12},{48,16},{52,20},{56,24},{60,28},{64,3... | collective-permute-start | bytes 1474568 | tf_op jit(solution)/shard_map/ppermute | solution.py:23
  124.9 1.0 pad_maximum_fusion.3
  125.9 0.1 copy.13
  126.0 0.7 convert_element_type.74.wvalid_ref
  126.7 1.0 fusion.1.q_ref
  127.6 33.0 %collective-permute-done.1 = bf16[2,3,4,16,640]{4,3,2,1,0:T(8,128)(2,1)} collective-permute-done((bf16[2,3,4,16,640]{4,3,2,1,0:T(8,128)(2,1)}, bf16[2,3,4,16,640]{4,3,2,1,0:T(8,128)(2,1)}, u32[]{:S(2)}, u32[]{:S(2)}) %collective-permute-start.1) | collective-permute-done | bytes 491552 | tf_op jit(solution)/shard_map/ppermute | solution.py:23
  160.7 10.9 %collective-permute-start.11 = (bf16[4,128,640]{2,1,0:T(8,128)(2,1)}, bf16[4,128,640]{2,1,0:T(8,128)(2,1)S(1)}, u32[]{:S(2)}, u32[]{:S(2)}) collective-permute-start(bf16[4,128,640]{2,1,0:T(8,128)(2,1)} %pad_maximum_fusion.3), channel_id=1, source_target_pairs={{0,4},{4,8},{8,12},{12,16},{16,20},{20,24},{24,28},{28,32},{32,36}... | collective-permute-start | bytes 1966088 | tf_op jit(solution)/shard_map/ppermute | solution.py:23
  171.6 6.0 %collective-permute-start.12 = (bf16[4,128,640]{2,1,0:T(8,128)(2,1)}, bf16[4,128,640]{2,1,0:T(8,128)(2,1)S(1)}, u32[]{:S(2)}, u32[]{:S(2)}) collective-permute-start(bf16[4,128,640]{2,1,0:T(8,128)(2,1)} %pad_maximum_fusion.5), channel_id=1, source_target_pairs={{4,0},{8,4},{12,8},{16,12},{20,16},{24,20},{28,24},{32,28},{36,32}... | collective-permute-start | bytes 1966088 | tf_op jit(solution)/shard_map/ppermute | solution.py:23
  177.6 1.9 collective-permute-start.13
  179.6 2.3 collective-permute-start.14
  181.9 7.0 %collective-permute-start.15 = (bf16[4,128,640]{2,1,0:T(8,128)(2,1)}, bf16[4,128,640]{2,1,0:T(8,128)(2,1)S(1)}, u32[]{:S(2)}, u32[]{:S(2)}) collective-permute-start(bf16[4,128,640]{2,1,0:T(8,128)(2,1)} %pad_maximum_fusion.8), channel_id=1, source_target_pairs={{36,0},{40,4},{44,8},{48,12},{52,16},{56,20},{60,24},{64,28},{68,3... | collective-permute-start | bytes 1966088 | tf_op jit(solution)/shard_map/ppermute | solution.py:23
  188.9 3.6 %maximum_maximum_fusion = bf16[2,3,16,24,640]{4,3,2,1,0:T(8,128)(2,1)S(1)} fusion(bf16[2,3,4,4,640]{4,3,2,1,0:T(4,128)(2,1)} %collective-permute-done.7, bf16[2,3,4,16,640]{4,3,2,1,0:T(8,128)(2,1)} %collective-permute-done.6, bf16[2,3,4,4,640]{4,3,2,1,0:T(4,128)(2,1)} %collective-permute-done.5, bf16[2,3,8,4,640]{4,3,2,1,0:T(4,128)(2,1)} %collective-permute-done.4, ...), kind=kLoop, calls=%fused_computation | loop fusion | flops 29491200 | bytes 5898240 | tf_op jit(solution)/shard_map/concatenate | solution.py:145
  192.6 1.9 fusion.19
  194.4 21.7 %collective-permute-done.11.rest_3_ = bf16[4,128,640]{2,1,0:T(8,128)(2,1)S(1)} collective-permute-done((bf16[4,128,640]{2,1,0:T(8,128)(2,1)}, bf16[4,128,640]{2,1,0:T(8,128)(2,1)S(1)}, u32[]{:S(2)}, u32[]{:S(2)}) %collective-permute-start.11) | collective-permute-done | bytes 655392 | tf_op jit(solution)/shard_map/ppermute | solution.py:23
  216.1 0.9 copy-done.7
  217.1 0.8 copy-done.8
  217.9 18.1 %collective-permute-done.13.rest_6_ = bf16[4,128,640]{2,1,0:T(8,128)(2,1)S(1)} collective-permute-done((bf16[4,128,640]{2,1,0:T(8,128)(2,1)}, bf16[4,128,640]{2,1,0:T(8,128)(2,1)S(1)}, u32[]{:S(2)}, u32[]{:S(2)}) %collective-permute-start.13) | collective-permute-done | bytes 655392 | tf_op jit(solution)/shard_map/ppermute | solution.py:23
  236.0 0.8 copy-done.9
  236.9 0.8 copy-done.10
  237.7 0.8 copy-done.11
  238.6 0.7 broadcast_in_dim.5
  239.2 22.1 %shard_map.91 = bf16[384,640]{1,0:T(8,128)(2,1)} custom-call(s32[1,1152]{1,0:T(1,128)} %convert_element_type.74.wvalid_ref, s32[1,2304]{1,0:T(1,128)} %bitcast.118, bf16[384,640]{1,0:T(8,128)(2,1)} %fusion.1.q_ref, bf16[1152,640]{1,0:T(8,128)(2,1)} %bitcast.116, bf16[1152,640]{1,0:T(8,128)(2,1)} %bitcast.115, bf16[4,128,640]{2,1,0:T(8,128)(2,1)} %copy-done.4, ...), custom_call_target="tpu_custom_call" | custom-call | tf_op jit(solution)/shard_map/pallas_call | solution.py:181
  (43 shorter events, 0.1 us)
Async XLA Ops:
  0.0 37.3 %copy-start = (bf16[1,3,128,640]{3,2,1,0:T(8,128)(2,1)S(1)}, bf16[1,3,128,640]{3,2,1,0:T(8,128)(2,1)}, u32[]{:S(2)}) copy-start(bf16[1,3,128,640]{3,2,1,0:T(8,128)(2,1)} %param.11) | copy-start | bytes 1474564
  0.0 41.6 %copy-start.14 = (s32[128,9,2]{0,2,1:T(2,128)S(1)}, s32[128,9,2]{0,2,1:T(2,128)}, u32[]{:S(2)}) copy-start(s32[128,9,2]{0,2,1:T(2,128)} %param.17) | copy-start | bytes 27652
  10.6 57.7 %copy-start.15 = (s32[1,4]{1,0:T(1,128)S(1)}, s32[1,4]{1,0:T(1,128)}, u32[]{:S(2)}) copy-start(s32[1,4]{1,0:T(1,128)} %param.16) | copy-start | bytes 52
  10.6 71.1 %copy-start.1 = (bf16[1,8,128,640]{3,2,1,0:T(8,128)(2,1)S(1)}, bf16[1,8,128,640]{3,2,1,0:T(8,128)(2,1)}, u32[]{:S(2)}) copy-start(bf16[1,8,128,640]{3,2,1,0:T(8,128)(2,1)} %param.13) | copy-start | bytes 3932164
  13.2 77.3 %collective-permute-start = (bf16[2,3,4,4,640]{4,3,2,1,0:T(4,128)(2,1)S(1)}, bf16[2,3,4,4,640]{4,3,2,1,0:T(4,128)(2,1)S(1)}, u32[]{:S(2)}, u32[]{:S(2)}) collective-permute-start(bf16[2,3,4,4,640]{4,3,2,1,0:T(4,128)(2,1)S(1)} %get-tuple-element.45), channel_id=1, source_target_pairs={{0,36},{4,40},{8,44},{12,48},{16,52},{20,56},{24,60},{28,64},{32,6... | collective-permute-start | bytes 368648 | tf_op jit(solution)/shard_map/ppermute | solution.py:23
  17.3 81.5 %collective-permute-start.2 = (bf16[2,3,4,4,640]{4,3,2,1,0:T(4,128)(2,1)S(1)}, bf16[2,3,4,4,640]{4,3,2,1,0:T(4,128)(2,1)S(1)}, u32[]{:S(2)}, u32[]{:S(2)}) collective-permute-start(bf16[2,3,4,4,640]{4,3,2,1,0:T(4,128)(2,1)S(1)} %get-tuple-element.46), channel_id=1, source_target_pairs={{0,28},{4,32},{8,36},{12,40},{16,44},{20,48},{24,52},{28,56},{32,6... | collective-permute-start | bytes 368648 | tf_op jit(solution)/shard_map/ppermute | solution.py:23
  27.8 77.8 %collective-permute-start.5 = (bf16[2,3,4,4,640]{4,3,2,1,0:T(4,128)(2,1)S(1)}, bf16[2,3,4,4,640]{4,3,2,1,0:T(4,128)(2,1)}, u32[]{:S(2)}, u32[]{:S(2)}) collective-permute-start(bf16[2,3,4,4,640]{4,3,2,1,0:T(4,128)(2,1)S(1)} %get-tuple-element.47), channel_id=1, source_target_pairs={{28,0},{32,4},{36,8},{40,12},{44,16},{48,20},{52,24},{56,28},{60,3... | collective-permute-start | bytes 368648 | tf_op jit(solution)/shard_map/ppermute | solution.py:23
  29.8 79.9 %collective-permute-start.7 = (bf16[2,3,4,4,640]{4,3,2,1,0:T(4,128)(2,1)S(1)}, bf16[2,3,4,4,640]{4,3,2,1,0:T(4,128)(2,1)}, u32[]{:S(2)}, u32[]{:S(2)}) collective-permute-start(bf16[2,3,4,4,640]{4,3,2,1,0:T(4,128)(2,1)S(1)} %get-tuple-element.48), channel_id=1, source_target_pairs={{36,0},{40,4},{44,8},{48,12},{52,16},{56,20},{60,24},{64,28},{68,3... | collective-permute-start | bytes 368648 | tf_op jit(solution)/shard_map/ppermute | solution.py:23
  38.4 79.1 %collective-permute-start.3 = (bf16[2,3,8,4,640]{4,3,2,1,0:T(4,128)(2,1)}, bf16[2,3,8,4,640]{4,3,2,1,0:T(4,128)(2,1)}, u32[]{:S(2)}, u32[]{:S(2)}) collective-permute-start(bf16[2,3,8,4,640]{4,3,2,1,0:T(4,128)(2,1)} %get-tuple-element.51), channel_id=1, source_target_pairs={{0,4},{4,8},{8,12},{12,16},{16,20},{20,24},{24,28},{28,32},{32,36}... | collective-permute-start | bytes 737288 | tf_op jit(solution)/shard_map/ppermute | solution.py:23
  81.7 1.3 copy-start.2
  89.6 37.1 %copy-start.3 = (bf16[1,3,128,640]{3,2,1,0:T(8,128)(2,1)S(1)}, bf16[1,3,128,640]{3,2,1,0:T(8,128)(2,1)}, u32[]{:S(2)}) copy-start(bf16[1,3,128,640]{3,2,1,0:T(8,128)(2,1)} %param.9) | copy-start | bytes 1474564
  89.6 37.1 %copy-start.16 = (f32[640]{0:T(1024)S(1)}, f32[640]{0:T(1024)}, u32[]{:S(2)}) copy-start(f32[640]{0:T(1024)} %param.14) | copy-start | bytes 7684
  90.6 15.1 %copy-start.12 = (bf16[2,3,4,4,640]{4,3,2,1,0:T(4,128)(2,1)}, bf16[2,3,4,4,640]{4,3,2,1,0:T(4,128)(2,1)S(1)}, u32[]{:S(2)}) copy-start(bf16[2,3,4,4,640]{4,3,2,1,0:T(4,128)(2,1)S(1)} %collective-permute-done) | copy-start | bytes 368644
  90.6 31.2 %collective-permute-start.4 = (bf16[2,3,8,4,640]{4,3,2,1,0:T(4,128)(2,1)}, bf16[2,3,8,4,640]{4,3,2,1,0:T(4,128)(2,1)}, u32[]{:S(2)}, u32[]{:S(2)}) collective-permute-start(bf16[2,3,8,4,640]{4,3,2,1,0:T(4,128)(2,1)} %get-tuple-element.52), channel_id=1, source_target_pairs={{4,0},{8,4},{12,8},{16,12},{20,16},{24,20},{28,24},{32,28},{36,32}... | collective-permute-start | bytes 737288 | tf_op jit(solution)/shard_map/ppermute | solution.py:23
  98.7 6.9 %copy-start.13 = (bf16[2,3,4,4,640]{4,3,2,1,0:T(4,128)(2,1)}, bf16[2,3,4,4,640]{4,3,2,1,0:T(4,128)(2,1)S(1)}, u32[]{:S(2)}) copy-start(bf16[2,3,4,4,640]{4,3,2,1,0:T(4,128)(2,1)S(1)} %collective-permute-done.2) | copy-start | bytes 368644
  98.7 78.9 %collective-permute-start.8 = (bf16[4,128,640]{2,1,0:T(8,128)(2,1)}, bf16[4,128,640]{2,1,0:T(8,128)(2,1)S(1)}, u32[]{:S(2)}, u32[]{:S(2)}) collective-permute-start(bf16[4,128,640]{2,1,0:T(8,128)(2,1)} %pad_maximum_fusion), channel_id=1, source_target_pairs={{0,36},{4,40},{8,44},{12,48},{16,52},{20,56},{24,60},{28,64},{32,6... | collective-permute-start | bytes 1966088 | tf_op jit(solution)/shard_map/ppermute | solution.py:23
  105.7 73.9 %collective-permute-start.9 = (bf16[4,128,640]{2,1,0:T(8,128)(2,1)}, bf16[4,128,640]{2,1,0:T(8,128)(2,1)S(1)}, u32[]{:S(2)}, u32[]{:S(2)}) collective-permute-start(bf16[4,128,640]{2,1,0:T(8,128)(2,1)} %pad_maximum_fusion.1), channel_id=1, source_target_pairs={{0,32},{4,36},{8,40},{12,44},{16,48},{20,52},{24,56},{28,60},{32,6... | collective-permute-start | bytes 1966088 | tf_op jit(solution)/shard_map/ppermute | solution.py:23
  109.7 72.2 %collective-permute-start.10 = (bf16[4,128,640]{2,1,0:T(8,128)(2,1)}, bf16[4,128,640]{2,1,0:T(8,128)(2,1)S(1)}, u32[]{:S(2)}, u32[]{:S(2)}) collective-permute-start(bf16[4,128,640]{2,1,0:T(8,128)(2,1)} %pad_maximum_fusion.2), channel_id=1, source_target_pairs={{0,28},{4,32},{8,36},{12,40},{16,44},{20,48},{24,52},{28,56},{32,6... | collective-permute-start | bytes 1966088 | tf_op jit(solution)/shard_map/ppermute | solution.py:23
  117.5 43.2 %collective-permute-start.1 = (bf16[2,3,4,16,640]{4,3,2,1,0:T(8,128)(2,1)}, bf16[2,3,4,16,640]{4,3,2,1,0:T(8,128)(2,1)}, u32[]{:S(2)}, u32[]{:S(2)}) collective-permute-start(bf16[2,3,4,16,640]{4,3,2,1,0:T(8,128)(2,1)} %get-tuple-element.49), channel_id=1, source_target_pairs={{0,32},{4,36},{8,40},{12,44},{16,48},{20,52},{24,56},{28,60},{32,6... | collective-permute-start | bytes 1474568 | tf_op jit(solution)/shard_map/ppermute | solution.py:23
  121.7 49.9 %collective-permute-start.6 = (bf16[2,3,4,16,640]{4,3,2,1,0:T(8,128)(2,1)}, bf16[2,3,4,16,640]{4,3,2,1,0:T(8,128)(2,1)}, u32[]{:S(2)}, u32[]{:S(2)}) collective-permute-start(bf16[2,3,4,16,640]{4,3,2,1,0:T(8,128)(2,1)} %get-tuple-element.50), channel_id=1, source_target_pairs={{32,0},{36,4},{40,8},{44,12},{48,16},{52,20},{56,24},{60,28},{64,3... | collective-permute-start | bytes 1474568 | tf_op jit(solution)/shard_map/ppermute | solution.py:23
  160.7 55.5 %collective-permute-start.11 = (bf16[4,128,640]{2,1,0:T(8,128)(2,1)}, bf16[4,128,640]{2,1,0:T(8,128)(2,1)S(1)}, u32[]{:S(2)}, u32[]{:S(2)}) collective-permute-start(bf16[4,128,640]{2,1,0:T(8,128)(2,1)} %pad_maximum_fusion.3), channel_id=1, source_target_pairs={{0,4},{4,8},{8,12},{12,16},{16,20},{20,24},{24,28},{28,32},{32,36}... | collective-permute-start | bytes 1966088 | tf_op jit(solution)/shard_map/ppermute | solution.py:23
  171.6 45.4 %collective-permute-start.12 = (bf16[4,128,640]{2,1,0:T(8,128)(2,1)}, bf16[4,128,640]{2,1,0:T(8,128)(2,1)S(1)}, u32[]{:S(2)}, u32[]{:S(2)}) collective-permute-start(bf16[4,128,640]{2,1,0:T(8,128)(2,1)} %pad_maximum_fusion.5), channel_id=1, source_target_pairs={{4,0},{8,4},{12,8},{16,12},{20,16},{24,20},{28,24},{32,28},{36,32}... | collective-permute-start | bytes 1966088 | tf_op jit(solution)/shard_map/ppermute | solution.py:23
  177.6 16.8 %copy-start.4 = (bf16[4,128,640]{2,1,0:T(8,128)(2,1)}, bf16[4,128,640]{2,1,0:T(8,128)(2,1)S(1)}, u32[]{:S(2)}) copy-start(bf16[4,128,640]{2,1,0:T(8,128)(2,1)S(1)} %collective-permute-done.8.rest_0_) | copy-start | bytes 1966084
  177.6 58.4 %collective-permute-start.13 = (bf16[4,128,640]{2,1,0:T(8,128)(2,1)}, bf16[4,128,640]{2,1,0:T(8,128)(2,1)S(1)}, u32[]{:S(2)}, u32[]{:S(2)}) collective-permute-start(bf16[4,128,640]{2,1,0:T(8,128)(2,1)} %pad_maximum_fusion.6), channel_id=1, source_target_pairs={{28,0},{32,4},{36,8},{40,12},{44,16},{48,20},{52,24},{56,28},{60,3... | collective-permute-start | bytes 1966088 | tf_op jit(solution)/shard_map/ppermute | solution.py:23
  179.6 14.9 %copy-start.5 = (bf16[4,128,640]{2,1,0:T(8,128)(2,1)}, bf16[4,128,640]{2,1,0:T(8,128)(2,1)S(1)}, u32[]{:S(2)}) copy-start(bf16[4,128,640]{2,1,0:T(8,128)(2,1)S(1)} %collective-permute-done.9.rest_1_) | copy-start | bytes 1966084
  179.6 57.3 %collective-permute-start.14 = (bf16[4,128,640]{2,1,0:T(8,128)(2,1)}, bf16[4,128,640]{2,1,0:T(8,128)(2,1)S(1)}, u32[]{:S(2)}, u32[]{:S(2)}) collective-permute-start(bf16[4,128,640]{2,1,0:T(8,128)(2,1)} %pad_maximum_fusion.7), channel_id=1, source_target_pairs={{32,0},{36,4},{40,8},{44,12},{48,16},{52,20},{56,24},{60,28},{64,3... | collective-permute-start | bytes 1966088 | tf_op jit(solution)/shard_map/ppermute | solution.py:23
  181.9 12.5 %copy-start.6 = (bf16[4,128,640]{2,1,0:T(8,128)(2,1)}, bf16[4,128,640]{2,1,0:T(8,128)(2,1)S(1)}, u32[]{:S(2)}) copy-start(bf16[4,128,640]{2,1,0:T(8,128)(2,1)S(1)} %collective-permute-done.10.rest_2_) | copy-start | bytes 1966084
  181.9 55.8 %collective-permute-start.15 = (bf16[4,128,640]{2,1,0:T(8,128)(2,1)}, bf16[4,128,640]{2,1,0:T(8,128)(2,1)S(1)}, u32[]{:S(2)}, u32[]{:S(2)}) collective-permute-start(bf16[4,128,640]{2,1,0:T(8,128)(2,1)} %pad_maximum_fusion.8), channel_id=1, source_target_pairs={{36,0},{40,4},{44,8},{48,12},{52,16},{56,20},{60,24},{64,28},{68,3... | collective-permute-start | bytes 1966088 | tf_op jit(solution)/shard_map/ppermute | solution.py:23
  216.1 0.9 copy-start.7
  217.1 0.8 copy-start.8
  236.0 0.8 copy-start.9
  236.9 0.8 copy-start.10
  237.7 0.8 copy-start.11

commit v4 on v3

--- a/solution.py
+++ b/solution.py
@@ -82,6 +82,13 @@
         cache_probs, cache_v, preferred_element_type=jnp.float32
     )
     o_ref[...] = mixed_out.astype(jnp.bfloat16)
+
+
+def pick_kernel(idx_ref, k0_ref, k1_ref, v0_ref, v1_ref, o_ref):
+    o_ref[0, 0] = k0_ref[0]
+    o_ref[0, 1] = k1_ref[0]
+    o_ref[0, 2] = v0_ref[0]
+    o_ref[0, 3] = v1_ref[0]
 
 
 def body(
@@ -98,24 +105,37 @@
     own_cache_v = cache_values[0]
     cap = cache_frames.shape[2]
 
-    def blocks_for(target, slot_index):
-        safe_target = jnp.clip(target, 0, tile_count - 1)
-        listed = lax.dynamic_index_in_dim(cache_frames, safe_target, 0, keepdims=False)[slot_index]
-        wanted = jnp.maximum(listed, 0)
-        picked = [
-            lax.dynamic_index_in_dim(own_cache_k, wanted[c], 0, keepdims=False) for c in range(cap)
-        ] + [
-            lax.dynamic_index_in_dim(own_cache_v, wanted[c], 0, keepdims=False) for c in range(cap)
-        ]
-        return jnp.stack(picked)
+    slot_ids = jnp.arange(9, dtype=jnp.int32)
+    targets = jnp.clip(
+        own_place - ((slot_ids // 3 - 1) * GW + (slot_ids % 3 - 1)), 0, tile_count - 1
+    )
+    listed = cache_frames[targets, slot_ids]
+    wanted = jnp.clip(listed, 0, own_cache_k.shape[0] - 1).reshape(-1).astype(jnp.int32)
+    block_shape = (1,) + own_cache_k.shape[1:]
+    picked = pl.pallas_call(
+        pick_kernel,
+        grid_spec=pltpu.PrefetchScalarGridSpec(
+            num_scalar_prefetch=1,
+            grid=(9,),
+            in_specs=[
+                pl.BlockSpec(block_shape, lambda d, idx: (idx[2 * d], 0, 0)),
+                pl.BlockSpec(block_shape, lambda d, idx: (idx[2 * d + 1], 0, 0)),
+                pl.BlockSpec(block_shape, lambda d, idx: (idx[2 * d], 0, 0)),
+                pl.BlockSpec(block_shape, lambda d, idx: (idx[2 * d + 1], 0, 0)),
+            ],
+            out_specs=pl.BlockSpec((1, 2 * cap) + own_cache_k.shape[1:], lambda d, idx: (d, 0, 0, 0)),
+        ),
+        out_shape=jax.ShapeDtypeStruct((9, 2 * cap) + own_cache_k.shape[1:], own_cache_k.dtype),
+    )(wanted, own_cache_k, own_cache_k, own_cache_v, own_cache_v)
 
     cache_in = {}
     for row_step, col_step in STEPS:
+        slot = slot_of(row_step, col_step)
         if (row_step, col_step) != (0, 0):
             shift_by = -(row_step * GW + col_step)
-            packed = blocks_for(own_place + shift_by, slot_of(row_step, col_step))
-            cache_in[row_step, col_step] = shifted(packed, "sp", shift_by)
-    cache_in[0, 0] = blocks_for(own_place, 4)
+            cache_in[row_step, col_step] = shifted(picked[slot], "sp", shift_by)
+        else:
+            cache_in[row_step, col_step] = picked[slot]
 
     query_wide = query[0].astype(jnp.float32)
     keys_wide = keys[0].astype(jnp.float32)

time: 263 us -> 230 us (0.87)
  the two profiles are of different devices: /device:TPU:206 before, /device:TPU:198 now
where the time goes in v4:
time: 230 us; the launch traced here: 229 us
  waiting for transfers between devices  80.9 us (35%)
  starting transfers between devices  76.7 us (33%)
  Pallas kernels  30.5 us (13%)
  local copies, waits for them, and re-layouts  13.1 us (6%)
  other arithmetic  12.6 us (5%)
  blocking collectives  12 us (5%)
  between operations  2.96 us (1%)
    ppermute x16, waiting for transfers between devices, shifted(): return lax.ppermute(x, axis, pairs)  80.9 us
    ppermute x16, starting transfers between devices, shifted(): return lax.ppermute(x, axis, pairs)  76.7 us
    pallas_call x1, Pallas kernels, body(): pl.pallas_call(attend_kernel, grid=(head_count,), in_specs=[pl.BlockSpec(...  22.1 us
    psum x1, blocking collectives, body(): lax.psum((jnp.sum(query_wide * query_wide, axis=-1), jnp.sum(keys_wide *...  12 us
    pallas_call x1, Pallas kernels, body(): pl.pallas_call(pick_kernel, grid_spec=pltpu.PrefetchScalarGridSpec(num_sc...  8.35 us
    another operation x3, other arithmetic, body(): both_grid = jnp.stack([key_grid, value_grid])  5.21 us
    squeeze x1, local copies, waits for them, and re-layouts, body(): cache_in[row_step, col_step] = shifted(picked[slot], 'sp', shift_by)  4.99 us
  transfers between devices with their start and end apart: 16, of which 6 were waited for; matrix products, arithmetic and copies ran while one was open for 8% of the time, Pallas kernels for 4%

profile of v4, /device:TPU:198, one launch (start us, length us, event | category | flops | bytes accessed | tf_op | source)
XLA Modules:
  0.0 228.8 jit_solution(8565145493600871808)
XLA Ops:
  0.0 1.4 multiply_reduce_fusion
  1.4 12.0 %all-reduce = (f32[3,128]{1,0:T(4,128)S(1)}, f32[3,128]{1,0:T(4,128)S(1)}) all-reduce(f32[3,128]{1,0:T(4,128)S(1)} %get-tuple-element.31, f32[3,128]{1,0:T(4,128)S(1)} %get-tuple-element.30), channel_id=1, replica_groups=mesh['sp'=128,'hd'=4] {'hd'}, use_global_device_ids=true, to_apply=%region_1.2 | all-reduce | flops 768 | bytes 6144 | tf_op jit(solution)/shard_map/psum | solution.py:142
  13.5 0.1 mul.85
  13.5 1.2 multiply_convert_fusion
  14.8 2.0 fusion.6
  16.8 3.7 %collective-permute-start = (bf16[2,3,4,4,640]{4,3,2,1,0:T(4,128)(2,1)}, bf16[2,3,4,4,640]{4,3,2,1,0:T(4,128)(2,1)}, u32[]{:S(2)}, u32[]{:S(2)}) collective-permute-start(bf16[2,3,4,4,640]{4,3,2,1,0:T(4,128)(2,1)} %get-tuple-element.18), channel_id=1, source_target_pairs={{0,36},{4,40},{8,44},{12,48},{16,52},{20,56},{24,60},{28,64},{32,6... | collective-permute-start | bytes 368648 | tf_op jit(solution)/shard_map/ppermute | solution.py:23
  20.5 10.9 %collective-permute-start.2 = (bf16[2,3,4,4,640]{4,3,2,1,0:T(4,128)(2,1)}, bf16[2,3,4,4,640]{4,3,2,1,0:T(4,128)(2,1)}, u32[]{:S(2)}, u32[]{:S(2)}) collective-permute-start(bf16[2,3,4,4,640]{4,3,2,1,0:T(4,128)(2,1)} %get-tuple-element.19), channel_id=1, source_target_pairs={{0,28},{4,32},{8,36},{12,40},{16,44},{20,48},{24,52},{28,56},{32,6... | collective-permute-start | bytes 368648 | tf_op jit(solution)/shard_map/ppermute | solution.py:23
  31.4 1.9 collective-permute-start.5
  33.3 2.1 fusion.4
  35.5 6.2 %collective-permute-start.3 = (bf16[2,3,8,4,640]{4,3,2,1,0:T(4,128)(2,1)}, bf16[2,3,8,4,640]{4,3,2,1,0:T(4,128)(2,1)}, u32[]{:S(2)}, u32[]{:S(2)}) collective-permute-start(bf16[2,3,8,4,640]{4,3,2,1,0:T(4,128)(2,1)} %get-tuple-element.24), channel_id=1, source_target_pairs={{0,4},{4,8},{8,12},{12,16},{16,20},{20,24},{24,28},{28,32},{32,36}... | collective-permute-start | bytes 737288 | tf_op jit(solution)/shard_map/ppermute | solution.py:23
  41.7 4.1 %collective-permute-start.4 = (bf16[2,3,8,4,640]{4,3,2,1,0:T(4,128)(2,1)}, bf16[2,3,8,4,640]{4,3,2,1,0:T(4,128)(2,1)}, u32[]{:S(2)}, u32[]{:S(2)}) collective-permute-start(bf16[2,3,8,4,640]{4,3,2,1,0:T(4,128)(2,1)} %get-tuple-element.25), channel_id=1, source_target_pairs={{4,0},{8,4},{12,8},{16,12},{20,16},{24,20},{28,24},{32,28},{36,32}... | collective-permute-start | bytes 737288 | tf_op jit(solution)/shard_map/ppermute | solution.py:23
  45.9 1.5 fusion.21
  48.7 0.9 copy.18
  49.6 0.7 gather_fusion
  50.3 0.6 min.22.idx_ref
  50.9 8.4 %shard_map.91 = bf16[9,4,128,640]{3,2,1,0:T(8,128)(2,1)} custom-call(s32[18]{0:T(128)} %min.22.idx_ref, bf16[8,128,640]{2,1,0:T(8,128)(2,1)} %bitcast.49, bf16[8,128,640]{2,1,0:T(8,128)(2,1)} %bitcast.50, bf16[8,128,640]{2,1,0:T(8,128)(2,1)} %bitcast.51, bf16[8,128,640]{2,1,0:T(8,128)(2,1)} %bitcast.52), custom_call_target="tpu_custom_call" | custom-call | tf_op jit(solution)/shard_map/pallas_call | solution.py:115
  59.3 0.0 copy-start.8
  59.3 5.0 %slice_bitcast_fusion = (bf16[4,128,640]{2,1,0:T(8,128)(2,1)S(1)}, bf16[4,128,640]{2,1,0:T(8,128)(2,1)}, bf16[4,128,640]{2,1,0:T(8,128)(2,1)}, bf16[4,128,640]{2...) fusion(bf16[9,4,128,640]{3,2,1,0:T(8,128)(2,1)} %shard_map.91), kind=kLoop, calls=%fused_computation.22 | loop fusion | bytes 11796480 | tf_op jit(solution)/shard_map/squeeze | solution.py:136
  65.6 0.1 and_convert_fusion
  65.7 0.0 copy-done.7
  65.7 0.1 constant_dynamic-slice_fusion
  65.8 0.1 copy.19
  65.9 0.0 collective-permute-done
  65.9 1.9 collective-permute-start.7
  67.8 0.0 copy-done
  67.8 1.1 fusion.3
  68.9 0.0 collective-permute-done.2
  68.9 6.6 %collective-permute-start.1 = (bf16[2,3,4,16,640]{4,3,2,1,0:T(8,128)(2,1)}, bf16[2,3,4,16,640]{4,3,2,1,0:T(8,128)(2,1)}, u32[]{:S(2)}, u32[]{:S(2)}) collective-permute-start(bf16[2,3,4,16,640]{4,3,2,1,0:T(8,128)(2,1)} %get-tuple-element.22), channel_id=1, source_target_pairs={{0,32},{4,36},{8,40},{12,44},{16,48},{20,52},{24,56},{28,60},{32,6... | collective-permute-start | bytes 1474568 | tf_op jit(solution)/shard_map/ppermute | solution.py:23
  75.5 0.0 collective-permute-done.5
  75.6 1.9 collective-permute-start.6
  77.5 0.0 collective-permute-done.7
  77.5 10.0 %collective-permute-start.10 = (bf16[4,128,640]{2,1,0:T(8,128)(2,1)}, bf16[4,128,640]{2,1,0:T(8,128)(2,1)}, u32[]{:S(2)}, u32[]{:S(2)}) collective-permute-start(bf16[4,128,640]{2,1,0:T(8,128)(2,1)} %get-tuple-element.13), channel_id=1, source_target_pairs={{0,28},{4,32},{8,36},{12,40},{16,44},{20,48},{24,52},{28,56},{32,6... | collective-permute-start | bytes 1966088 | tf_op jit(solution)/shard_map/ppermute | solution.py:23
  87.5 0.0 collective-permute-done.3
  87.5 1.9 collective-permute-start.11
  89.4 0.0 collective-permute-done.4
  89.4 8.4 %collective-permute-start.12 = (bf16[4,128,640]{2,1,0:T(8,128)(2,1)}, bf16[4,128,640]{2,1,0:T(8,128)(2,1)}, u32[]{:S(2)}, u32[]{:S(2)}) collective-permute-start(bf16[4,128,640]{2,1,0:T(8,128)(2,1)} %get-tuple-element.10), channel_id=1, source_target_pairs={{4,0},{8,4},{12,8},{16,12},{20,16},{24,20},{28,24},{32,28},{36,32}... | collective-permute-start | bytes 1966088 | tf_op jit(solution)/shard_map/ppermute | solution.py:23
  97.9 0.7 convert_element_type.74.wvalid_ref
  98.6 0.1 copy.17
  98.7 0.0 copy-done.1
  98.7 0.0 copy-done.8
  98.7 1.0 fusion.1.q_ref
  99.7 1.2 collective-permute-done.1
  100.9 1.9 collective-permute-start.13
  102.8 2.3 %collective-permute-done.6 = bf16[2,3,4,16,640]{4,3,2,1,0:T(8,128)(2,1)} collective-permute-done((bf16[2,3,4,16,640]{4,3,2,1,0:T(8,128)(2,1)}, bf16[2,3,4,16,640]{4,3,2,1,0:T(8,128)(2,1)}, u32[]{:S(2)}, u32[]{:S(2)}) %collective-permute-start.6) | collective-permute-done | bytes 491552 | tf_op jit(solution)/shard_map/ppermute | solution.py:23
  105.1 6.0 %collective-permute-start.14 = (bf16[4,128,640]{2,1,0:T(8,128)(2,1)}, bf16[4,128,640]{2,1,0:T(8,128)(2,1)S(1)}, u32[]{:S(2)}, u32[]{:S(2)}) collective-permute-start(bf16[4,128,640]{2,1,0:T(8,128)(2,1)} %get-tuple-element.8), channel_id=1, source_target_pairs={{32,0},{36,4},{40,8},{44,12},{48,16},{52,20},{56,24},{60,28},{64,3... | collective-permute-start | bytes 1966088 | tf_op jit(solution)/shard_map/ppermute | solution.py:23
  111.1 44.1 %collective-permute-done.10.rest_2_ = bf16[4,128,640]{2,1,0:T(8,128)(2,1)} collective-permute-done((bf16[4,128,640]{2,1,0:T(8,128)(2,1)}, bf16[4,128,640]{2,1,0:T(8,128)(2,1)}, u32[]{:S(2)}, u32[]{:S(2)}) %collective-permute-start.10) | collective-permute-done | bytes 655392 | tf_op jit(solution)/shard_map/ppermute | solution.py:23
  155.2 1.9 collective-permute-start.15
  157.1 0.0 collective-permute-done.11.rest_3_
  157.2 7.3 %collective-permute-start.8 = (bf16[4,128,640]{2,1,0:T(8,128)(2,1)S(1)}, bf16[4,128,640]{2,1,0:T(8,128)(2,1)S(1)}, u32[]{:S(2)}, u32[]{:S(2)}) collective-permute-start(bf16[4,128,640]{2,1,0:T(8,128)(2,1)S(1)} %get-tuple-element.15), channel_id=1, source_target_pairs={{0,36},{4,40},{8,44},{12,48},{16,52},{20,56},{24,60},{28,64},{32,6... | collective-permute-start | bytes 1966088 | tf_op jit(solution)/shard_map/ppermute | solution.py:23
  164.4 9.7 %collective-permute-done.12.rest_5_ = bf16[4,128,640]{2,1,0:T(8,128)(2,1)} collective-permute-done((bf16[4,128,640]{2,1,0:T(8,128)(2,1)}, bf16[4,128,640]{2,1,0:T(8,128)(2,1)}, u32[]{:S(2)}, u32[]{:S(2)}) %collective-permute-start.12) | collective-permute-done | bytes 655392 | tf_op jit(solution)/shard_map/ppermute | solution.py:23
  174.1 1.9 collective-permute-start.9
  176.0 3.6 %maximum_maximum_fusion = bf16[2,3,16,24,640]{4,3,2,1,0:T(8,128)(2,1)S(1)} fusion(bf16[2,3,4,4,640]{4,3,2,1,0:T(4,128)(2,1)} %collective-permute-done.7, bf16[2,3,4,16,640]{4,3,2,1,0:T(8,128)(2,1)} %collective-permute-done.6, bf16[2,3,4,4,640]{4,3,2,1,0:T(4,128)(2,1)} %collective-permute-done.5, bf16[2,3,8,4,640]{4,3,2,1,0:T(4,128)(2,1)} %collective-permute-done.4, ...), kind=kLoop, calls=%fused_computation.1 | loop fusion | flops 29491200 | bytes 5898240 | tf_op jit(solution)/shard_map/concatenate | solution.py:165
  179.7 1.9 fusion.20
  181.5 0.0 collective-permute-done.13.rest_6_
  181.5 0.0 collective-permute-done.14.rest_7_
  181.5 0.0 copy-start.3
  181.6 9.0 %collective-permute-done.15.rest_8_ = bf16[4,128,640]{2,1,0:T(8,128)(2,1)S(1)} collective-permute-done((bf16[4,128,640]{2,1,0:T(8,128)(2,1)S(1)}, bf16[4,128,640]{2,1,0:T(8,128)(2,1)S(1)}, u32[]{:S(2)}, u32[]{:S(2)}) %collective-permute-start.15) | collective-permute-done | bytes 655392 | tf_op jit(solution)/shard_map/ppermute | solution.py:23
  190.6 0.0 collective-permute-done.8.rest_0_
  190.6 14.5 %collective-permute-done.9.rest_1_ = bf16[4,128,640]{2,1,0:T(8,128)(2,1)S(1)} collective-permute-done((bf16[4,128,640]{2,1,0:T(8,128)(2,1)S(1)}, bf16[4,128,640]{2,1,0:T(8,128)(2,1)S(1)}, u32[]{:S(2)}, u32[]{:S(2)}) %collective-permute-start.9) | collective-permute-done | bytes 655392 | tf_op jit(solution)/shard_map/ppermute | solution.py:23
  205.1 0.0 copy-done.2
  205.1 0.0 copy-done.3
  205.2 0.8 copy-done.6
  206.0 0.7 broadcast_in_dim.5
  206.6 22.1 %shard_map.92 = bf16[384,640]{1,0:T(8,128)(2,1)} custom-call(s32[1,1152]{1,0:T(1,128)} %convert_element_type.74.wvalid_ref, s32[1,2304]{1,0:T(1,128)} %bitcast.54, bf16[384,640]{1,0:T(8,128)(2,1)} %fusion.1.q_ref, bf16[1152,640]{1,0:T(8,128)(2,1)} %bitcast.48, bf16[1152,640]{1,0:T(8,128)(2,1)} %bitcast.47, bf16[4,128,640]{2,1,0:T(8,128)(2,1)} %copy-done.5, ...), custom_call_target="tpu_custom_call" | custom-call | tf_op jit(solution)/shard_map/pallas_call | solution.py:201
  (17 shorter events, 0.1 us)
Async XLA Ops:
  16.8 49.1 %collective-permute-start = (bf16[2,3,4,4,640]{4,3,2,1,0:T(4,128)(2,1)}, bf16[2,3,4,4,640]{4,3,2,1,0:T(4,128)(2,1)}, u32[]{:S(2)}, u32[]{:S(2)}) collective-permute-start(bf16[2,3,4,4,640]{4,3,2,1,0:T(4,128)(2,1)} %get-tuple-element.18), channel_id=1, source_target_pairs={{0,36},{4,40},{8,44},{12,48},{16,52},{20,56},{24,60},{28,64},{32,6... | collective-permute-start | bytes 368648 | tf_op jit(solution)/shard_map/ppermute | solution.py:23
  20.5 48.4 %collective-permute-start.2 = (bf16[2,3,4,4,640]{4,3,2,1,0:T(4,128)(2,1)}, bf16[2,3,4,4,640]{4,3,2,1,0:T(4,128)(2,1)}, u32[]{:S(2)}, u32[]{:S(2)}) collective-permute-start(bf16[2,3,4,4,640]{4,3,2,1,0:T(4,128)(2,1)} %get-tuple-element.19), channel_id=1, source_target_pairs={{0,28},{4,32},{8,36},{12,40},{16,44},{20,48},{24,52},{28,56},{32,6... | collective-permute-start | bytes 368648 | tf_op jit(solution)/shard_map/ppermute | solution.py:23
  31.4 44.1 %collective-permute-start.5 = (bf16[2,3,4,4,640]{4,3,2,1,0:T(4,128)(2,1)}, bf16[2,3,4,4,640]{4,3,2,1,0:T(4,128)(2,1)}, u32[]{:S(2)}, u32[]{:S(2)}) collective-permute-start(bf16[2,3,4,4,640]{4,3,2,1,0:T(4,128)(2,1)} %get-tuple-element.20), channel_id=1, source_target_pairs={{28,0},{32,4},{36,8},{40,12},{44,16},{48,20},{52,24},{56,28},{60,3... | collective-permute-start | bytes 368648 | tf_op jit(solution)/shard_map/ppermute | solution.py:23
  35.5 52.0 %collective-permute-start.3 = (bf16[2,3,8,4,640]{4,3,2,1,0:T(4,128)(2,1)}, bf16[2,3,8,4,640]{4,3,2,1,0:T(4,128)(2,1)}, u32[]{:S(2)}, u32[]{:S(2)}) collective-permute-start(bf16[2,3,8,4,640]{4,3,2,1,0:T(4,128)(2,1)} %get-tuple-element.24), channel_id=1, source_target_pairs={{0,4},{4,8},{8,12},{12,16},{16,20},{20,24},{24,28},{28,32},{32,36}... | collective-permute-start | bytes 737288 | tf_op jit(solution)/shard_map/ppermute | solution.py:23
  41.7 47.7 %collective-permute-start.4 = (bf16[2,3,8,4,640]{4,3,2,1,0:T(4,128)(2,1)}, bf16[2,3,8,4,640]{4,3,2,1,0:T(4,128)(2,1)}, u32[]{:S(2)}, u32[]{:S(2)}) collective-permute-start(bf16[2,3,8,4,640]{4,3,2,1,0:T(4,128)(2,1)} %get-tuple-element.25), channel_id=1, source_target_pairs={{4,0},{8,4},{12,8},{16,12},{20,16},{24,20},{28,24},{32,28},{36,32}... | collective-permute-start | bytes 737288 | tf_op jit(solution)/shard_map/ppermute | solution.py:23
  59.3 6.4 %copy-start.7 = (s32[128,9,2]{0,2,1:T(2,128)S(1)}, s32[128,9,2]{0,2,1:T(2,128)}, u32[]{:S(2)}) copy-start(s32[128,9,2]{0,2,1:T(2,128)} %param.17) | copy-start | bytes 27652
  59.3 8.5 %copy-start = (bf16[1,3,128,640]{3,2,1,0:T(8,128)(2,1)S(1)}, bf16[1,3,128,640]{3,2,1,0:T(8,128)(2,1)}, u32[]{:S(2)}) copy-start(bf16[1,3,128,640]{3,2,1,0:T(8,128)(2,1)} %param.11) | copy-start | bytes 1474564
  59.3 39.4 %copy-start.1 = (bf16[1,3,128,640]{3,2,1,0:T(8,128)(2,1)S(1)}, bf16[1,3,128,640]{3,2,1,0:T(8,128)(2,1)}, u32[]{:S(2)}) copy-start(bf16[1,3,128,640]{3,2,1,0:T(8,128)(2,1)} %param.9) | copy-start | bytes 1474564
  59.3 39.4 %copy-start.8 = (f32[640]{0:T(1024)S(1)}, f32[640]{0:T(1024)}, u32[]{:S(2)}) copy-start(f32[640]{0:T(1024)} %param.14) | copy-start | bytes 7684
  65.9 11.6 %collective-permute-start.7 = (bf16[2,3,4,4,640]{4,3,2,1,0:T(4,128)(2,1)}, bf16[2,3,4,4,640]{4,3,2,1,0:T(4,128)(2,1)}, u32[]{:S(2)}, u32[]{:S(2)}) collective-permute-start(bf16[2,3,4,4,640]{4,3,2,1,0:T(4,128)(2,1)} %get-tuple-element.21), channel_id=1, source_target_pairs={{36,0},{40,4},{44,8},{48,12},{52,16},{56,20},{60,24},{64,28},{68,3... | collective-permute-start | bytes 368648 | tf_op jit(solution)/shard_map/ppermute | solution.py:23
  68.9 32.0 %collective-permute-start.1 = (bf16[2,3,4,16,640]{4,3,2,1,0:T(8,128)(2,1)}, bf16[2,3,4,16,640]{4,3,2,1,0:T(8,128)(2,1)}, u32[]{:S(2)}, u32[]{:S(2)}) collective-permute-start(bf16[2,3,4,16,640]{4,3,2,1,0:T(8,128)(2,1)} %get-tuple-element.22), channel_id=1, source_target_pairs={{0,32},{4,36},{8,40},{12,44},{16,48},{20,52},{24,56},{28,60},{32,6... | collective-permute-start | bytes 1474568 | tf_op jit(solution)/shard_map/ppermute | solution.py:23
  75.6 29.6 %collective-permute-start.6 = (bf16[2,3,4,16,640]{4,3,2,1,0:T(8,128)(2,1)}, bf16[2,3,4,16,640]{4,3,2,1,0:T(8,128)(2,1)}, u32[]{:S(2)}, u32[]{:S(2)}) collective-permute-start(bf16[2,3,4,16,640]{4,3,2,1,0:T(8,128)(2,1)} %get-tuple-element.23), channel_id=1, source_target_pairs={{32,0},{36,4},{40,8},{44,12},{48,16},{52,20},{56,24},{60,28},{64,3... | collective-permute-start | bytes 1474568 | tf_op jit(solution)/shard_map/ppermute | solution.py:23
  77.5 77.7 %collective-permute-start.10 = (bf16[4,128,640]{2,1,0:T(8,128)(2,1)}, bf16[4,128,640]{2,1,0:T(8,128)(2,1)}, u32[]{:S(2)}, u32[]{:S(2)}) collective-permute-start(bf16[4,128,640]{2,1,0:T(8,128)(2,1)} %get-tuple-element.13), channel_id=1, source_target_pairs={{0,28},{4,32},{8,36},{12,40},{16,44},{20,48},{24,52},{28,56},{32,6... | collective-permute-start | bytes 1966088 | tf_op jit(solution)/shard_map/ppermute | solution.py:23
  87.5 69.7 %collective-permute-start.11 = (bf16[4,128,640]{2,1,0:T(8,128)(2,1)}, bf16[4,128,640]{2,1,0:T(8,128)(2,1)}, u32[]{:S(2)}, u32[]{:S(2)}) collective-permute-start(bf16[4,128,640]{2,1,0:T(8,128)(2,1)} %get-tuple-element.12), channel_id=1, source_target_pairs={{0,4},{4,8},{8,12},{12,16},{16,20},{20,24},{24,28},{28,32},{32,36}... | collective-permute-start | bytes 1966088 | tf_op jit(solution)/shard_map/ppermute | solution.py:23
  89.4 84.7 %collective-permute-start.12 = (bf16[4,128,640]{2,1,0:T(8,128)(2,1)}, bf16[4,128,640]{2,1,0:T(8,128)(2,1)}, u32[]{:S(2)}, u32[]{:S(2)}) collective-permute-start(bf16[4,128,640]{2,1,0:T(8,128)(2,1)} %get-tuple-element.10), channel_id=1, source_target_pairs={{4,0},{8,4},{12,8},{16,12},{20,16},{24,20},{28,24},{32,28},{36,32}... | collective-permute-start | bytes 1966088 | tf_op jit(solution)/shard_map/ppermute | solution.py:23
  100.9 80.7 %collective-permute-start.13 = (bf16[4,128,640]{2,1,0:T(8,128)(2,1)}, bf16[4,128,640]{2,1,0:T(8,128)(2,1)S(1)}, u32[]{:S(2)}, u32[]{:S(2)}) collective-permute-start(bf16[4,128,640]{2,1,0:T(8,128)(2,1)} %get-tuple-element.9), channel_id=1, source_target_pairs={{28,0},{32,4},{36,8},{40,12},{44,16},{48,20},{52,24},{56,28},{60,3... | collective-permute-start | bytes 1966088 | tf_op jit(solution)/shard_map/ppermute | solution.py:23
  105.1 76.4 %collective-permute-start.14 = (bf16[4,128,640]{2,1,0:T(8,128)(2,1)}, bf16[4,128,640]{2,1,0:T(8,128)(2,1)S(1)}, u32[]{:S(2)}, u32[]{:S(2)}) collective-permute-start(bf16[4,128,640]{2,1,0:T(8,128)(2,1)} %get-tuple-element.8), channel_id=1, source_target_pairs={{32,0},{36,4},{40,8},{44,12},{48,16},{52,20},{56,24},{60,28},{64,3... | collective-permute-start | bytes 1966088 | tf_op jit(solution)/shard_map/ppermute | solution.py:23
  155.2 35.4 %collective-permute-start.15 = (bf16[4,128,640]{2,1,0:T(8,128)(2,1)S(1)}, bf16[4,128,640]{2,1,0:T(8,128)(2,1)S(1)}, u32[]{:S(2)}, u32[]{:S(2)}) collective-permute-start(bf16[4,128,640]{2,1,0:T(8,128)(2,1)S(1)} %get-tuple-element.7), channel_id=1, source_target_pairs={{36,0},{40,4},{44,8},{48,12},{52,16},{56,20},{60,24},{64,28},{68,3... | collective-permute-start | bytes 1966088 | tf_op jit(solution)/shard_map/ppermute | solution.py:23
  157.2 33.4 %collective-permute-start.8 = (bf16[4,128,640]{2,1,0:T(8,128)(2,1)S(1)}, bf16[4,128,640]{2,1,0:T(8,128)(2,1)S(1)}, u32[]{:S(2)}, u32[]{:S(2)}) collective-permute-start(bf16[4,128,640]{2,1,0:T(8,128)(2,1)S(1)} %get-tuple-element.15), channel_id=1, source_target_pairs={{0,36},{4,40},{8,44},{12,48},{16,52},{20,56},{24,60},{28,64},{32,6... | collective-permute-start | bytes 1966088 | tf_op jit(solution)/shard_map/ppermute | solution.py:23
  174.1 31.0 %collective-permute-start.9 = (bf16[4,128,640]{2,1,0:T(8,128)(2,1)S(1)}, bf16[4,128,640]{2,1,0:T(8,128)(2,1)S(1)}, u32[]{:S(2)}, u32[]{:S(2)}) collective-permute-start(bf16[4,128,640]{2,1,0:T(8,128)(2,1)S(1)} %get-tuple-element.14), channel_id=1, source_target_pairs={{0,32},{4,36},{8,40},{12,44},{16,48},{20,52},{24,56},{28,60},{32,6... | collective-permute-start | bytes 1966088 | tf_op jit(solution)/shard_map/ppermute | solution.py:23
  181.5 23.6 %copy-start.2 = (bf16[4,128,640]{2,1,0:T(8,128)(2,1)}, bf16[4,128,640]{2,1,0:T(8,128)(2,1)S(1)}, u32[]{:S(2)}) copy-start(bf16[4,128,640]{2,1,0:T(8,128)(2,1)S(1)} %collective-permute-done.13.rest_6_) | copy-start | bytes 1966084
  181.5 23.6 %copy-start.3 = (bf16[4,128,640]{2,1,0:T(8,128)(2,1)}, bf16[4,128,640]{2,1,0:T(8,128)(2,1)S(1)}, u32[]{:S(2)}) copy-start(bf16[4,128,640]{2,1,0:T(8,128)(2,1)S(1)} %collective-permute-done.14.rest_7_) | copy-start | bytes 1966084
  190.6 14.6 %copy-start.4 = (bf16[4,128,640]{2,1,0:T(8,128)(2,1)}, bf16[4,128,640]{2,1,0:T(8,128)(2,1)S(1)}, u32[]{:S(2)}) copy-start(bf16[4,128,640]{2,1,0:T(8,128)(2,1)S(1)} %collective-permute-done.15.rest_8_) | copy-start | bytes 1966084
  190.6 14.6 %copy-start.5 = (bf16[4,128,640]{2,1,0:T(8,128)(2,1)}, bf16[4,128,640]{2,1,0:T(8,128)(2,1)S(1)}, u32[]{:S(2)}) copy-start(bf16[4,128,640]{2,1,0:T(8,128)(2,1)S(1)} %collective-permute-done.8.rest_0_) | copy-start | bytes 1966084
  205.1 0.8 copy-start.6

commit v5 on v4

--- a/solution.py
+++ b/solution.py
@@ -35,6 +35,16 @@
     return grid
 
 
+def hd_sum(x):
+    size = lax.axis_size("hd")
+    step = 1
+    while step < size:
+        pairs = [(i, i ^ step) for i in range(size)]
+        x = x + lax.ppermute(x, "hd", pairs)
+        step *= 2
+    return x
+
+
 def slot_of(row_step, col_step):
     return 3 * (row_step + 1) + (col_step + 1)
 
@@ -76,19 +86,21 @@
     row_total = jnp.sum(window_exp, axis=1, keepdims=True) + jnp.sum(
         cache_exp, axis=1, keepdims=True
     )
-    window_probs = (window_exp / row_total).astype(jnp.bfloat16)
-    cache_probs = (cache_exp / row_total).astype(jnp.bfloat16)
+    row_scale = 1.0 / row_total
+    window_probs = (window_exp * row_scale).astype(jnp.bfloat16)
+    cache_probs = (cache_exp * row_scale).astype(jnp.bfloat16)
     mixed_out = jnp.dot(window_probs, wv_ref[...], preferred_element_type=jnp.float32) + jnp.dot(
         cache_probs, cache_v, preferred_element_type=jnp.float32
     )
     o_ref[...] = mixed_out.astype(jnp.bfloat16)
 
 
-def pick_kernel(idx_ref, k0_ref, k1_ref, v0_ref, v1_ref, o_ref):
-    o_ref[0, 0] = k0_ref[0]
-    o_ref[0, 1] = k1_ref[0]
-    o_ref[0, 2] = v0_ref[0]
-    o_ref[0, 3] = v1_ref[0]
+def pick_kernel(idx_ref, k_ref, v_ref, *o_refs):
+    cap = o_refs[0].shape[0] // 2
+    for d, o_ref in enumerate(o_refs):
+        for c in range(cap):
+            o_ref[c] = k_ref[idx_ref[cap * d + c]]
+            o_ref[cap + c] = v_ref[idx_ref[cap * d + c]]
 
 
 def body(
@@ -111,22 +123,18 @@
     )
     listed = cache_frames[targets, slot_ids]
     wanted = jnp.clip(listed, 0, own_cache_k.shape[0] - 1).reshape(-1).astype(jnp.int32)
-    block_shape = (1,) + own_cache_k.shape[1:]
+    full_spec = pl.BlockSpec(own_cache_k.shape, lambda i, idx: (0, 0, 0))
+    out_block = (2 * cap,) + own_cache_k.shape[1:]
     picked = pl.pallas_call(
         pick_kernel,
         grid_spec=pltpu.PrefetchScalarGridSpec(
             num_scalar_prefetch=1,
-            grid=(9,),
-            in_specs=[
-                pl.BlockSpec(block_shape, lambda d, idx: (idx[2 * d], 0, 0)),
-                pl.BlockSpec(block_shape, lambda d, idx: (idx[2 * d + 1], 0, 0)),
-                pl.BlockSpec(block_shape, lambda d, idx: (idx[2 * d], 0, 0)),
-                pl.BlockSpec(block_shape, lambda d, idx: (idx[2 * d + 1], 0, 0)),
-            ],
-            out_specs=pl.BlockSpec((1, 2 * cap) + own_cache_k.shape[1:], lambda d, idx: (d, 0, 0, 0)),
+            grid=(1,),
+            in_specs=[full_spec, full_spec],
+            out_specs=[pl.BlockSpec(out_block, lambda i, idx: (0, 0, 0)) for _ in range(9)],
         ),
-        out_shape=jax.ShapeDtypeStruct((9, 2 * cap) + own_cache_k.shape[1:], own_cache_k.dtype),
-    )(wanted, own_cache_k, own_cache_k, own_cache_v, own_cache_v)
+        out_shape=[jax.ShapeDtypeStruct(out_block, own_cache_k.dtype) for _ in range(9)],
+    )(wanted, own_cache_k, own_cache_v)
 
     cache_in = {}
     for row_step, col_step in STEPS:
@@ -139,9 +147,10 @@
 
     query_wide = query[0].astype(jnp.float32)
     keys_wide = keys[0].astype(jnp.float32)
-    query_total, keys_total = lax.psum(
-        (jnp.sum(query_wide * query_wide, axis=-1), jnp.sum(keys_wide * keys_wide, axis=-1)),
-        "hd",
+    query_total, keys_total = hd_sum(
+        jnp.stack(
+            [jnp.sum(query_wide * query_wide, axis=-1), jnp.sum(keys_wide * keys_wide, axis=-1)]
+        )
     )
     query_normed = normalize(query[0], q_gain, query_total, width_all)
     keys_normed = normalize(keys[0], k_gain, keys_total, width_all)

time: 230 us -> 221 us (0.961)
  the two profiles are of different devices: /device:TPU:198 before, /device:TPU:228 now
where the time goes in v5:
time: 221 us; the launch traced here: 220 us
  starting transfers between devices  88.6 us (40%)
  waiting for transfers between devices  81.7 us (37%)
  Pallas kernels  27.4 us (12%)
  other arithmetic  10.2 us (5%)
  local copies, waits for them, and re-layouts  8.8 us (4%)
  between operations  3.02 us (1%)
    ppermute x16, starting transfers between devices, shifted(): return lax.ppermute(x, axis, pairs)  83.4 us
    ppermute x16, waiting for transfers between devices, shifted(): return lax.ppermute(x, axis, pairs)  81.4 us
    pallas_call x1, Pallas kernels, body(): pl.pallas_call(attend_kernel, grid=(head_count,), in_specs=[pl.BlockSpec(...  22.1 us
    pallas_call x1, Pallas kernels, body(): pl.pallas_call(pick_kernel, grid_spec=pltpu.PrefetchScalarGridSpec(num_sc...  5.29 us
    ppermute x2, starting transfers between devices, hd_sum(): x = x + lax.ppermute(x, 'hd', pairs)  5.27 us
  transfers between devices with their start and end apart: 18, of which 6 were waited for; matrix products, arithmetic and copies ran while one was open for 6% of the time, Pallas kernels for 2%

profile of v5, /device:TPU:228, one launch (start us, length us, event | category | flops | bytes accessed | tf_op | source)
XLA Modules:
  0.0 219.8 jit_solution(12918316244099399250)
XLA Ops:
  0.0 1.3 multiply_reduce_fusion.1
  1.3 1.2 multiply_reduce_fusion
  2.5 2.6 %collective-permute-start = (f32[2,3,128]{2,1,0:T(4,128)S(1)}, f32[2,3,128]{2,1,0:T(4,128)S(1)}, u32[]{:S(2)}, u32[]{:S(2)}) collective-permute-start(f32[2,3,128]{2,1,0:T(4,128)S(1)} %pad_maximum_fusion.1), channel_id=1, source_target_pairs={{0,1},{1,0},{2,3},{3,2},{4,5},{5,4},{6,7},{7,6},{8,9},{9,8},{10,11... | collective-permute-start | bytes 9224 | tf_op jit(solution)/shard_map/ppermute | solution.py:43
  5.1 0.9 copy.18
  6.1 0.8 constant_dynamic-slice_fusion
  6.9 0.1 copy.19
  7.0 0.7 gather_fusion
  7.7 0.4 collective-permute-done
  8.0 2.7 %collective-permute-start.1 = (f32[2,3,128]{2,1,0:T(4,128)S(1)}, f32[2,3,128]{2,1,0:T(4,128)S(1)}, u32[]{:S(2)}, u32[]{:S(2)}) collective-permute-start(f32[2,3,128]{2,1,0:T(4,128)S(1)} %fusion.25), channel_id=1, source_target_pairs={{0,2},{1,3},{2,0},{3,1},{4,6},{5,7},{6,4},{7,5},{8,10},{9,11},{10,... | collective-permute-start | bytes 9224 | tf_op jit(solution)/shard_map/ppermute | solution.py:43
  10.7 1.5 fusion.27
  13.5 0.6 min.22.idx_ref
  15.5 5.3 %shard_map.91 = (bf16[4,128,640]{2,1,0:T(8,128)(2,1)}, bf16[4,128,640]{2,1,0:T(8,128)(2,1)}, bf16[4,128,640]{2,1,0:T(8,128)(2,1)}, bf16[4,128,640]{2,1,0:T(8,128...) custom-call(s32[18]{0:T(128)} %min.22.idx_ref, ...), custom_call_target="tpu_custom_call" | custom-call | tf_op jit(solution)/shard_map/pallas_call | solution.py:128
  20.8 0.0 collective-permute-done.1
  20.8 0.6 fusion.10
  21.4 0.1 rsqrt.23
  21.4 0.0 copy-done.1
  21.4 0.0 copy-done.7
  21.5 0.2 multiply_convert_fusion
  21.7 0.2 fusion.6
  21.9 4.0 %collective-permute-start.2 = (bf16[2,3,4,4,640]{4,3,2,1,0:T(4,128)(2,1)S(1)}, bf16[2,3,4,4,640]{4,3,2,1,0:T(4,128)(2,1)}, u32[]{:S(2)}, u32[]{:S(2)}) collective-permute-start(bf16[2,3,4,4,640]{4,3,2,1,0:T(4,128)(2,1)S(1)} %get-tuple-element.25), channel_id=1, source_target_pairs={{0,36},{4,40},{8,44},{12,48},{16,52},{20,56},{24,60},{28,64},{32,6... | collective-permute-start | bytes 368648 | tf_op jit(solution)/shard_map/ppermute | solution.py:23
  25.9 10.9 %collective-permute-start.4 = (bf16[2,3,4,4,640]{4,3,2,1,0:T(4,128)(2,1)S(1)}, bf16[2,3,4,4,640]{4,3,2,1,0:T(4,128)(2,1)}, u32[]{:S(2)}, u32[]{:S(2)}) collective-permute-start(bf16[2,3,4,4,640]{4,3,2,1,0:T(4,128)(2,1)S(1)} %get-tuple-element.26), channel_id=1, source_target_pairs={{0,28},{4,32},{8,36},{12,40},{16,44},{20,48},{24,52},{28,56},{32,6... | collective-permute-start | bytes 368648 | tf_op jit(solution)/shard_map/ppermute | solution.py:23
  36.8 1.9 collective-permute-start.7
  38.7 7.8 %collective-permute-start.9 = (bf16[2,3,4,4,640]{4,3,2,1,0:T(4,128)(2,1)S(1)}, bf16[2,3,4,4,640]{4,3,2,1,0:T(4,128)(2,1)}, u32[]{:S(2)}, u32[]{:S(2)}) collective-permute-start(bf16[2,3,4,4,640]{4,3,2,1,0:T(4,128)(2,1)S(1)} %get-tuple-element.28), channel_id=1, source_target_pairs={{36,0},{40,4},{44,8},{48,12},{52,16},{56,20},{60,24},{64,28},{68,3... | collective-permute-start | bytes 368648 | tf_op jit(solution)/shard_map/ppermute | solution.py:23
  46.5 0.3 fusion.4
  46.8 1.9 collective-permute-start.5
  48.8 0.0 collective-permute-done.2
  48.8 7.6 %collective-permute-start.6 = (bf16[2,3,8,4,640]{4,3,2,1,0:T(4,128)(2,1)S(1)}, bf16[2,3,8,4,640]{4,3,2,1,0:T(4,128)(2,1)}, u32[]{:S(2)}, u32[]{:S(2)}) collective-permute-start(bf16[2,3,8,4,640]{4,3,2,1,0:T(4,128)(2,1)S(1)} %get-tuple-element.32), channel_id=1, source_target_pairs={{4,0},{8,4},{12,8},{16,12},{20,16},{24,20},{28,24},{32,28},{36,32}... | collective-permute-start | bytes 737288 | tf_op jit(solution)/shard_map/ppermute | solution.py:23
  56.4 0.0 collective-permute-done.4
  56.4 1.9 collective-permute-start.10
  58.3 0.0 collective-permute-done.7
  58.3 6.6 %collective-permute-start.11 = (bf16[4,128,640]{2,1,0:T(8,128)(2,1)}, bf16[4,128,640]{2,1,0:T(8,128)(2,1)S(1)}, u32[]{:S(2)}, u32[]{:S(2)}) collective-permute-start(bf16[4,128,640]{2,1,0:T(8,128)(2,1)} %get-tuple-element.15), channel_id=1, source_target_pairs={{0,32},{4,36},{8,40},{12,44},{16,48},{20,52},{24,56},{28,60},{32,6... | collective-permute-start | bytes 1966088 | tf_op jit(solution)/shard_map/ppermute | solution.py:23
  65.0 0.0 collective-permute-done.9
  65.0 9.5 %collective-permute-start.12 = (bf16[4,128,640]{2,1,0:T(8,128)(2,1)}, bf16[4,128,640]{2,1,0:T(8,128)(2,1)}, u32[]{:S(2)}, u32[]{:S(2)}) collective-permute-start(bf16[4,128,640]{2,1,0:T(8,128)(2,1)} %get-tuple-element.16), channel_id=1, source_target_pairs={{0,28},{4,32},{8,36},{12,40},{16,44},{20,48},{24,52},{28,56},{32,6... | collective-permute-start | bytes 1966088 | tf_op jit(solution)/shard_map/ppermute | solution.py:23
  74.4 1.1 fusion.3
  75.5 0.0 collective-permute-done.5
  75.5 4.8 %collective-permute-start.3 = (bf16[2,3,4,16,640]{4,3,2,1,0:T(8,128)(2,1)}, bf16[2,3,4,16,640]{4,3,2,1,0:T(8,128)(2,1)S(1)}, u32[]{:S(2)}, u32[]{:S(2)}) collective-permute-start(bf16[2,3,4,16,640]{4,3,2,1,0:T(8,128)(2,1)} %get-tuple-element.29), channel_id=1, source_target_pairs={{0,32},{4,36},{8,40},{12,44},{16,48},{20,52},{24,56},{28,60},{32,6... | collective-permute-start | bytes 1474568 | tf_op jit(solution)/shard_map/ppermute | solution.py:23
  80.3 0.0 collective-permute-done.6
  80.4 2.5 %collective-permute-start.8 = (bf16[2,3,4,16,640]{4,3,2,1,0:T(8,128)(2,1)}, bf16[2,3,4,16,640]{4,3,2,1,0:T(8,128)(2,1)}, u32[]{:S(2)}, u32[]{:S(2)}) collective-permute-start(bf16[2,3,4,16,640]{4,3,2,1,0:T(8,128)(2,1)} %get-tuple-element.30), channel_id=1, source_target_pairs={{32,0},{36,4},{40,8},{44,12},{48,16},{52,20},{56,24},{60,28},{64,3... | collective-permute-start | bytes 1474568 | tf_op jit(solution)/shard_map/ppermute | solution.py:23
  82.9 0.1 copy.17
  83.0 0.1 and_convert_fusion
  83.1 0.7 convert_element_type.74.wvalid_ref
  83.8 1.7 fusion.1.q_ref
  85.4 35.0 %collective-permute-done.3 = bf16[2,3,4,16,640]{4,3,2,1,0:T(8,128)(2,1)S(1)} collective-permute-done((bf16[2,3,4,16,640]{4,3,2,1,0:T(8,128)(2,1)}, bf16[2,3,4,16,640]{4,3,2,1,0:T(8,128)(2,1)S(1)}, u32[]{:S(2)}, u32[]{:S(2)}) %collective-permute-start.3) | collective-permute-done | bytes 491552 | tf_op jit(solution)/shard_map/ppermute | solution.py:23
  120.4 0.8 copy-done.6
  121.2 9.9 %collective-permute-start.13 = (bf16[4,128,640]{2,1,0:T(8,128)(2,1)}, bf16[4,128,640]{2,1,0:T(8,128)(2,1)S(1)}, u32[]{:S(2)}, u32[]{:S(2)}) collective-permute-start(bf16[4,128,640]{2,1,0:T(8,128)(2,1)} %get-tuple-element.17), channel_id=1, source_target_pairs={{0,4},{4,8},{8,12},{12,16},{16,20},{20,24},{24,28},{28,32},{32,36}... | collective-permute-start | bytes 1966088 | tf_op jit(solution)/shard_map/ppermute | solution.py:23
  131.1 0.0 collective-permute-done.8
  131.1 1.9 collective-permute-start.14
  133.0 0.0 collective-permute-done.10.rest_0_
  133.1 1.9 collective-permute-start.15
  135.0 0.0 collective-permute-done.11.rest_1_
  135.0 3.8 %collective-permute-start.16 = (bf16[4,128,640]{2,1,0:T(8,128)(2,1)}, bf16[4,128,640]{2,1,0:T(8,128)(2,1)}, u32[]{:S(2)}, u32[]{:S(2)}) collective-permute-start(bf16[4,128,640]{2,1,0:T(8,128)(2,1)} %get-tuple-element.21), channel_id=1, source_target_pairs={{32,0},{36,4},{40,8},{44,12},{48,16},{52,20},{56,24},{60,28},{64,3... | collective-permute-start | bytes 1966088 | tf_op jit(solution)/shard_map/ppermute | solution.py:23
  138.8 0.0 collective-permute-done.12.rest_2_
  138.8 6.3 %collective-permute-start.17 = (bf16[4,128,640]{2,1,0:T(8,128)(2,1)}, bf16[4,128,640]{2,1,0:T(8,128)(2,1)}, u32[]{:S(2)}, u32[]{:S(2)}) collective-permute-start(bf16[4,128,640]{2,1,0:T(8,128)(2,1)} %get-tuple-element.22), channel_id=1, source_target_pairs={{36,0},{40,4},{44,8},{48,12},{52,16},{56,20},{60,24},{64,28},{68,3... | collective-permute-start | bytes 1966088 | tf_op jit(solution)/shard_map/ppermute | solution.py:23
  145.2 3.5 %maximum_maximum_fusion = bf16[2,3,16,24,640]{4,3,2,1,0:T(8,128)(2,1)S(1)} fusion(bf16[2,3,4,4,640]{4,3,2,1,0:T(4,128)(2,1)} %collective-permute-done.9, bf16[2,3,4,16,640]{4,3,2,1,0:T(8,128)(2,1)} %collective-permute-done.8, bf16[2,3,4,4,640]{4,3,2,1,0:T(4,128)(2,1)} %collective-permute-done.7, bf16[2,3,8,4,640]{4,3,2,1,0:T(4,128)(2,1)} %collective-permute-done.6, ...), kind=kLoop, calls=%fused_computation.1 | loop fusion | flops 29491200 | bytes 5898240 | tf_op jit(solution)/shard_map/concatenate | solution.py:174
  148.7 0.0 copy-done.3
  148.7 0.0 copy-done.4
  148.7 1.9 fusion.26
  150.6 0.0 collective-permute-done.13.rest_3_
  150.6 4.5 %collective-permute-done.14.rest_5_ = bf16[4,128,640]{2,1,0:T(8,128)(2,1)} collective-permute-done((bf16[4,128,640]{2,1,0:T(8,128)(2,1)}, bf16[4,128,640]{2,1,0:T(8,128)(2,1)}, u32[]{:S(2)}, u32[]{:S(2)}) %collective-permute-start.14) | collective-permute-done | bytes 655392 | tf_op jit(solution)/shard_map/ppermute | solution.py:23
  155.1 13.2 %collective-permute-done.15.rest_6_ = bf16[4,128,640]{2,1,0:T(8,128)(2,1)} collective-permute-done((bf16[4,128,640]{2,1,0:T(8,128)(2,1)}, bf16[4,128,640]{2,1,0:T(8,128)(2,1)}, u32[]{:S(2)}, u32[]{:S(2)}) %collective-permute-start.15) | collective-permute-done | bytes 655392 | tf_op jit(solution)/shard_map/ppermute | solution.py:23
  168.3 21.3 %collective-permute-done.16.rest_7_ = bf16[4,128,640]{2,1,0:T(8,128)(2,1)} collective-permute-done((bf16[4,128,640]{2,1,0:T(8,128)(2,1)}, bf16[4,128,640]{2,1,0:T(8,128)(2,1)}, u32[]{:S(2)}, u32[]{:S(2)}) %collective-permute-start.16) | collective-permute-done | bytes 655392 | tf_op jit(solution)/shard_map/ppermute | solution.py:23
  189.7 7.3 %collective-permute-done.17.rest_8_ = bf16[4,128,640]{2,1,0:T(8,128)(2,1)} collective-permute-done((bf16[4,128,640]{2,1,0:T(8,128)(2,1)}, bf16[4,128,640]{2,1,0:T(8,128)(2,1)}, u32[]{:S(2)}, u32[]{:S(2)}) %collective-permute-start.17) | collective-permute-done | bytes 655392 | tf_op jit(solution)/shard_map/ppermute | solution.py:23
  197.0 0.7 broadcast_in_dim.5
  197.7 22.1 %shard_map.92 = bf16[384,640]{1,0:T(8,128)(2,1)} custom-call(s32[1,1152]{1,0:T(1,128)} %convert_element_type.74.wvalid_ref, s32[1,2304]{1,0:T(1,128)} %bitcast.36, bf16[384,640]{1,0:T(8,128)(2,1)} %fusion.1.q_ref, bf16[1152,640]{1,0:T(8,128)(2,1)} %bitcast.32, bf16[1152,640]{1,0:T(8,128)(2,1)} %bitcast.31, bf16[4,128,640]{2,1,0:T(8,128)(2,1)} %copy-done.3, ...), custom_call_target="tpu_custom_call" | custom-call | tf_op jit(solution)/shard_map/pallas_call | solution.py:210
  (20 shorter events, 0.1 us)
Async XLA Ops:
  0.0 21.4 %copy-start.1 = (bf16[1,3,128,640]{3,2,1,0:T(8,128)(2,1)S(1)}, bf16[1,3,128,640]{3,2,1,0:T(8,128)(2,1)}, u32[]{:S(2)}) copy-start(bf16[1,3,128,640]{3,2,1,0:T(8,128)(2,1)} %param.10) | copy-start | bytes 1474564
  0.0 21.4 %copy-start.7 = (f32[640]{0:T(1024)S(1)}, f32[640]{0:T(1024)}, u32[]{:S(2)}) copy-start(f32[640]{0:T(1024)} %param.15) | copy-start | bytes 7684
  0.0 21.6 %copy-start = (bf16[1,3,128,640]{3,2,1,0:T(8,128)(2,1)S(1)}, bf16[1,3,128,640]{3,2,1,0:T(8,128)(2,1)}, u32[]{:S(2)}) copy-start(bf16[1,3,128,640]{3,2,1,0:T(8,128)(2,1)} %param.11) | copy-start | bytes 1474564
  2.5 5.5 %collective-permute-start = (f32[2,3,128]{2,1,0:T(4,128)S(1)}, f32[2,3,128]{2,1,0:T(4,128)S(1)}, u32[]{:S(2)}, u32[]{:S(2)}) collective-permute-start(f32[2,3,128]{2,1,0:T(4,128)S(1)} %pad_maximum_fusion.1), channel_id=1, source_target_pairs={{0,1},{1,0},{2,3},{3,2},{4,5},{5,4},{6,7},{7,6},{8,9},{9,8},{10,11... | collective-permute-start | bytes 9224 | tf_op jit(solution)/shard_map/ppermute | solution.py:43
  8.0 12.7 %collective-permute-start.1 = (f32[2,3,128]{2,1,0:T(4,128)S(1)}, f32[2,3,128]{2,1,0:T(4,128)S(1)}, u32[]{:S(2)}, u32[]{:S(2)}) collective-permute-start(f32[2,3,128]{2,1,0:T(4,128)S(1)} %fusion.25), channel_id=1, source_target_pairs={{0,2},{1,3},{2,0},{3,1},{4,6},{5,7},{6,4},{7,5},{8,10},{9,11},{10,... | collective-permute-start | bytes 9224 | tf_op jit(solution)/shard_map/ppermute | solution.py:43
  21.5 62.3 %copy-start.2 = (bf16[1,3,128,640]{3,2,1,0:T(8,128)(2,1)S(1)}, bf16[1,3,128,640]{3,2,1,0:T(8,128)(2,1)}, u32[]{:S(2)}) copy-start(bf16[1,3,128,640]{3,2,1,0:T(8,128)(2,1)} %param.9) | copy-start | bytes 1474564
  21.9 26.9 %collective-permute-start.2 = (bf16[2,3,4,4,640]{4,3,2,1,0:T(4,128)(2,1)S(1)}, bf16[2,3,4,4,640]{4,3,2,1,0:T(4,128)(2,1)}, u32[]{:S(2)}, u32[]{:S(2)}) collective-permute-start(bf16[2,3,4,4,640]{4,3,2,1,0:T(4,128)(2,1)S(1)} %get-tuple-element.25), channel_id=1, source_target_pairs={{0,36},{4,40},{8,44},{12,48},{16,52},{20,56},{24,60},{28,64},{32,6... | collective-permute-start | bytes 368648 | tf_op jit(solution)/shard_map/ppermute | solution.py:23
  25.9 30.5 %collective-permute-start.4 = (bf16[2,3,4,4,640]{4,3,2,1,0:T(4,128)(2,1)S(1)}, bf16[2,3,4,4,640]{4,3,2,1,0:T(4,128)(2,1)}, u32[]{:S(2)}, u32[]{:S(2)}) collective-permute-start(bf16[2,3,4,4,640]{4,3,2,1,0:T(4,128)(2,1)S(1)} %get-tuple-element.26), channel_id=1, source_target_pairs={{0,28},{4,32},{8,36},{12,40},{16,44},{20,48},{24,52},{28,56},{32,6... | collective-permute-start | bytes 368648 | tf_op jit(solution)/shard_map/ppermute | solution.py:23
  36.8 21.5 %collective-permute-start.7 = (bf16[2,3,4,4,640]{4,3,2,1,0:T(4,128)(2,1)S(1)}, bf16[2,3,4,4,640]{4,3,2,1,0:T(4,128)(2,1)}, u32[]{:S(2)}, u32[]{:S(2)}) collective-permute-start(bf16[2,3,4,4,640]{4,3,2,1,0:T(4,128)(2,1)S(1)} %get-tuple-element.27), channel_id=1, source_target_pairs={{28,0},{32,4},{36,8},{40,12},{44,16},{48,20},{52,24},{56,28},{60,3... | collective-permute-start | bytes 368648 | tf_op jit(solution)/shard_map/ppermute | solution.py:23
  38.7 26.3 %collective-permute-start.9 = (bf16[2,3,4,4,640]{4,3,2,1,0:T(4,128)(2,1)S(1)}, bf16[2,3,4,4,640]{4,3,2,1,0:T(4,128)(2,1)}, u32[]{:S(2)}, u32[]{:S(2)}) collective-permute-start(bf16[2,3,4,4,640]{4,3,2,1,0:T(4,128)(2,1)S(1)} %get-tuple-element.28), channel_id=1, source_target_pairs={{36,0},{40,4},{44,8},{48,12},{52,16},{56,20},{60,24},{64,28},{68,3... | collective-permute-start | bytes 368648 | tf_op jit(solution)/shard_map/ppermute | solution.py:23
  46.8 28.7 %collective-permute-start.5 = (bf16[2,3,8,4,640]{4,3,2,1,0:T(4,128)(2,1)S(1)}, bf16[2,3,8,4,640]{4,3,2,1,0:T(4,128)(2,1)S(1)}, u32[]{:S(2)}, u32[]{:S(2)}) collective-permute-start(bf16[2,3,8,4,640]{4,3,2,1,0:T(4,128)(2,1)S(1)} %get-tuple-element.31), channel_id=1, source_target_pairs={{0,4},{4,8},{8,12},{12,16},{16,20},{20,24},{24,28},{28,32},{32,36}... | collective-permute-start | bytes 737288 | tf_op jit(solution)/shard_map/ppermute | solution.py:23
  48.8 31.6 %collective-permute-start.6 = (bf16[2,3,8,4,640]{4,3,2,1,0:T(4,128)(2,1)S(1)}, bf16[2,3,8,4,640]{4,3,2,1,0:T(4,128)(2,1)}, u32[]{:S(2)}, u32[]{:S(2)}) collective-permute-start(bf16[2,3,8,4,640]{4,3,2,1,0:T(4,128)(2,1)S(1)} %get-tuple-element.32), channel_id=1, source_target_pairs={{4,0},{8,4},{12,8},{16,12},{20,16},{24,20},{28,24},{32,28},{36,32}... | collective-permute-start | bytes 737288 | tf_op jit(solution)/shard_map/ppermute | solution.py:23
  56.4 76.7 %collective-permute-start.10 = (bf16[4,128,640]{2,1,0:T(8,128)(2,1)}, bf16[4,128,640]{2,1,0:T(8,128)(2,1)S(1)}, u32[]{:S(2)}, u32[]{:S(2)}) collective-permute-start(bf16[4,128,640]{2,1,0:T(8,128)(2,1)} %get-tuple-element.14), channel_id=1, source_target_pairs={{0,36},{4,40},{8,44},{12,48},{16,52},{20,56},{24,60},{28,64},{32,6... | collective-permute-start | bytes 1966088 | tf_op jit(solution)/shard_map/ppermute | solution.py:23
  58.3 76.7 %collective-permute-start.11 = (bf16[4,128,640]{2,1,0:T(8,128)(2,1)}, bf16[4,128,640]{2,1,0:T(8,128)(2,1)S(1)}, u32[]{:S(2)}, u32[]{:S(2)}) collective-permute-start(bf16[4,128,640]{2,1,0:T(8,128)(2,1)} %get-tuple-element.15), channel_id=1, source_target_pairs={{0,32},{4,36},{8,40},{12,44},{16,48},{20,52},{24,56},{28,60},{32,6... | collective-permute-start | bytes 1966088 | tf_op jit(solution)/shard_map/ppermute | solution.py:23
  65.0 73.8 %collective-permute-start.12 = (bf16[4,128,640]{2,1,0:T(8,128)(2,1)}, bf16[4,128,640]{2,1,0:T(8,128)(2,1)}, u32[]{:S(2)}, u32[]{:S(2)}) collective-permute-start(bf16[4,128,640]{2,1,0:T(8,128)(2,1)} %get-tuple-element.16), channel_id=1, source_target_pairs={{0,28},{4,32},{8,36},{12,40},{16,44},{20,48},{24,52},{28,56},{32,6... | collective-permute-start | bytes 1966088 | tf_op jit(solution)/shard_map/ppermute | solution.py:23
  75.5 44.9 %collective-permute-start.3 = (bf16[2,3,4,16,640]{4,3,2,1,0:T(8,128)(2,1)}, bf16[2,3,4,16,640]{4,3,2,1,0:T(8,128)(2,1)S(1)}, u32[]{:S(2)}, u32[]{:S(2)}) collective-permute-start(bf16[2,3,4,16,640]{4,3,2,1,0:T(8,128)(2,1)} %get-tuple-element.29), channel_id=1, source_target_pairs={{0,32},{4,36},{8,40},{12,44},{16,48},{20,52},{24,56},{28,60},{32,6... | collective-permute-start | bytes 1474568 | tf_op jit(solution)/shard_map/ppermute | solution.py:23
  80.4 50.7 %collective-permute-start.8 = (bf16[2,3,4,16,640]{4,3,2,1,0:T(8,128)(2,1)}, bf16[2,3,4,16,640]{4,3,2,1,0:T(8,128)(2,1)}, u32[]{:S(2)}, u32[]{:S(2)}) collective-permute-start(bf16[2,3,4,16,640]{4,3,2,1,0:T(8,128)(2,1)} %get-tuple-element.30), channel_id=1, source_target_pairs={{32,0},{36,4},{40,8},{44,12},{48,16},{52,20},{56,24},{60,28},{64,3... | collective-permute-start | bytes 1474568 | tf_op jit(solution)/shard_map/ppermute | solution.py:23
  120.4 0.8 copy-start.6
  121.2 29.4 %collective-permute-start.13 = (bf16[4,128,640]{2,1,0:T(8,128)(2,1)}, bf16[4,128,640]{2,1,0:T(8,128)(2,1)S(1)}, u32[]{:S(2)}, u32[]{:S(2)}) collective-permute-start(bf16[4,128,640]{2,1,0:T(8,128)(2,1)} %get-tuple-element.17), channel_id=1, source_target_pairs={{0,4},{4,8},{8,12},{12,16},{16,20},{20,24},{24,28},{28,32},{32,36}... | collective-permute-start | bytes 1966088 | tf_op jit(solution)/shard_map/ppermute | solution.py:23
  131.1 24.0 %collective-permute-start.14 = (bf16[4,128,640]{2,1,0:T(8,128)(2,1)}, bf16[4,128,640]{2,1,0:T(8,128)(2,1)}, u32[]{:S(2)}, u32[]{:S(2)}) collective-permute-start(bf16[4,128,640]{2,1,0:T(8,128)(2,1)} %get-tuple-element.19), channel_id=1, source_target_pairs={{4,0},{8,4},{12,8},{16,12},{20,16},{24,20},{28,24},{32,28},{36,32}... | collective-permute-start | bytes 1966088 | tf_op jit(solution)/shard_map/ppermute | solution.py:23
  133.0 15.7 %copy-start.3 = (bf16[4,128,640]{2,1,0:T(8,128)(2,1)}, bf16[4,128,640]{2,1,0:T(8,128)(2,1)S(1)}, u32[]{:S(2)}) copy-start(bf16[4,128,640]{2,1,0:T(8,128)(2,1)S(1)} %collective-permute-done.10.rest_0_) | copy-start | bytes 1966084
  133.1 35.3 %collective-permute-start.15 = (bf16[4,128,640]{2,1,0:T(8,128)(2,1)}, bf16[4,128,640]{2,1,0:T(8,128)(2,1)}, u32[]{:S(2)}, u32[]{:S(2)}) collective-permute-start(bf16[4,128,640]{2,1,0:T(8,128)(2,1)} %get-tuple-element.20), channel_id=1, source_target_pairs={{28,0},{32,4},{36,8},{40,12},{44,16},{48,20},{52,24},{56,28},{60,3... | collective-permute-start | bytes 1966088 | tf_op jit(solution)/shard_map/ppermute | solution.py:23
  135.0 13.7 %copy-start.4 = (bf16[4,128,640]{2,1,0:T(8,128)(2,1)}, bf16[4,128,640]{2,1,0:T(8,128)(2,1)S(1)}, u32[]{:S(2)}) copy-start(bf16[4,128,640]{2,1,0:T(8,128)(2,1)S(1)} %collective-permute-done.11.rest_1_) | copy-start | bytes 1966084
  135.0 54.7 %collective-permute-start.16 = (bf16[4,128,640]{2,1,0:T(8,128)(2,1)}, bf16[4,128,640]{2,1,0:T(8,128)(2,1)}, u32[]{:S(2)}, u32[]{:S(2)}) collective-permute-start(bf16[4,128,640]{2,1,0:T(8,128)(2,1)} %get-tuple-element.21), channel_id=1, source_target_pairs={{32,0},{36,4},{40,8},{44,12},{48,16},{52,20},{56,24},{60,28},{64,3... | collective-permute-start | bytes 1966088 | tf_op jit(solution)/shard_map/ppermute | solution.py:23
  138.8 58.1 %collective-permute-start.17 = (bf16[4,128,640]{2,1,0:T(8,128)(2,1)}, bf16[4,128,640]{2,1,0:T(8,128)(2,1)}, u32[]{:S(2)}, u32[]{:S(2)}) collective-permute-start(bf16[4,128,640]{2,1,0:T(8,128)(2,1)} %get-tuple-element.22), channel_id=1, source_target_pairs={{36,0},{40,4},{44,8},{48,12},{52,16},{56,20},{60,24},{64,28},{68,3... | collective-permute-start | bytes 1966088 | tf_op jit(solution)/shard_map/ppermute | solution.py:23
  150.6 47.1 %copy-start.5 = (bf16[4,128,640]{2,1,0:T(8,128)(2,1)}, bf16[4,128,640]{2,1,0:T(8,128)(2,1)S(1)}, u32[]{:S(2)}) copy-start(bf16[4,128,640]{2,1,0:T(8,128)(2,1)S(1)} %collective-permute-done.13.rest_3_) | copy-start | bytes 1966084

commit v6 on v5

--- a/solution.py
+++ b/solution.py
@@ -55,7 +55,39 @@
     return (wide * factor[..., None] * gain).astype(jnp.bfloat16)
 
 
-def attend_kernel(wvalid_ref, cvalid_ref, q_ref, wk_ref, wv_ref, *rest):
+def window_kernel(wvalid_ref, cvalid_ref, q_ref, wk_ref, wv_ref, c_ref, acc_ref, m_ref, l_ref):
+    cap_rows = c_ref.shape[0] // 2
+    tile_len = c_ref.shape[1]
+    score_scale = HS ** (-0.5)
+    dims = (((1,), (1,)), ((), ()))
+    head_q = q_ref[...]
+    cache_k = c_ref[:cap_rows].reshape(cap_rows * tile_len, HS)
+    cache_v = c_ref[cap_rows:].reshape(cap_rows * tile_len, HS)
+    window_scores = (
+        lax.dot_general(head_q, wk_ref[...], dims, preferred_element_type=jnp.float32)
+        * score_scale
+    )
+    window_scores = jnp.where(wvalid_ref[...] > 0, window_scores, MASKED)
+    cache_scores = (
+        lax.dot_general(head_q, cache_k, dims, preferred_element_type=jnp.float32) * score_scale
+    )
+    cache_scores = jnp.where(cvalid_ref[...] > 0, cache_scores, MASKED)
+    row_top = jnp.maximum(
+        jnp.max(window_scores, axis=1, keepdims=True), jnp.max(cache_scores, axis=1, keepdims=True)
+    )
+    window_exp = jnp.exp(window_scores - row_top)
+    cache_exp = jnp.exp(cache_scores - row_top)
+    row_total = jnp.sum(window_exp, axis=1, keepdims=True) + jnp.sum(
+        cache_exp, axis=1, keepdims=True
+    )
+    acc_ref[...] = jnp.dot(
+        window_exp.astype(jnp.bfloat16), wv_ref[...], preferred_element_type=jnp.float32
+    ) + jnp.dot(cache_exp.astype(jnp.bfloat16), cache_v, preferred_element_type=jnp.float32)
+    m_ref[...] = jnp.broadcast_to(row_top, m_ref.shape)
+    l_ref[...] = jnp.broadcast_to(row_total, l_ref.shape)
+
+
+def cache_kernel(cvalid_ref, q_ref, acc_ref, m_ref, l_ref, *rest):
     cache_refs = rest[:-1]
     o_ref = rest[-1]
     cap_rows = cache_refs[0].shape[0] // 2
@@ -69,30 +101,19 @@
     cache_v = jnp.concatenate(
         [ref[cap_rows:].reshape(cap_rows * tile_len, HS) for ref in cache_refs], axis=0
     )
-    window_scores = (
-        lax.dot_general(head_q, wk_ref[...], dims, preferred_element_type=jnp.float32)
-        * score_scale
-    )
-    window_scores = jnp.where(wvalid_ref[...] > 0, window_scores, MASKED)
     cache_scores = (
         lax.dot_general(head_q, cache_k, dims, preferred_element_type=jnp.float32) * score_scale
     )
     cache_scores = jnp.where(cvalid_ref[...] > 0, cache_scores, MASKED)
-    row_top = jnp.maximum(
-        jnp.max(window_scores, axis=1, keepdims=True), jnp.max(cache_scores, axis=1, keepdims=True)
-    )
-    window_exp = jnp.exp(window_scores - row_top)
+    first_top = m_ref[:, :1]
+    row_top = jnp.maximum(first_top, jnp.max(cache_scores, axis=1, keepdims=True))
+    rescale = jnp.exp(first_top - row_top)
     cache_exp = jnp.exp(cache_scores - row_top)
-    row_total = jnp.sum(window_exp, axis=1, keepdims=True) + jnp.sum(
-        cache_exp, axis=1, keepdims=True
-    )
-    row_scale = 1.0 / row_total
-    window_probs = (window_exp * row_scale).astype(jnp.bfloat16)
-    cache_probs = (cache_exp * row_scale).astype(jnp.bfloat16)
-    mixed_out = jnp.dot(window_probs, wv_ref[...], preferred_element_type=jnp.float32) + jnp.dot(
-        cache_probs, cache_v, preferred_element_type=jnp.float32
-    )
-    o_ref[...] = mixed_out.astype(jnp.bfloat16)
+    row_total = l_ref[:, :1] * rescale + jnp.sum(cache_exp, axis=1, keepdims=True)
+    mixed_out = acc_ref[...] * rescale + jnp.dot(
+        cache_exp.astype(jnp.bfloat16), cache_v, preferred_element_type=jnp.float32
+    )
+    o_ref[...] = (mixed_out * (1.0 / row_total)).astype(jnp.bfloat16)
 
 
 def pick_kernel(idx_ref, k_ref, v_ref, *o_refs):
@@ -205,30 +226,52 @@
     head_count = channels // HS
     query_rows = flat_q.shape[0]
     window_len = flat_wk.shape[0]
-    cache_len = cache_valid.shape[0]
-    cache_list = [cache_in[step] for step in STEPS]
-    heads_out = pl.pallas_call(
-        attend_kernel,
+    block_len = 2 * cap * tile_len // 2
+    cache_valid = cache_valid.astype(jnp.int32).reshape(9, block_len)
+    center_valid = cache_valid[4][None, :]
+    remote_valid = jnp.concatenate([cache_valid[:4], cache_valid[5:]], axis=0).reshape(1, -1)
+    remote_list = [cache_in[step] for step in STEPS if step != (0, 0)]
+    cache_spec = pl.BlockSpec((2 * cap, tile_len, HS), lambda h: (0, 0, h))
+    head_spec = pl.BlockSpec((query_rows, HS), lambda h: (0, h))
+    wide_shape = jax.ShapeDtypeStruct((query_rows, channels), jnp.float32)
+    params = pltpu.CompilerParams(vmem_limit_bytes=60 * 1024 * 1024)
+    first_acc, first_top, first_total = pl.pallas_call(
+        window_kernel,
         grid=(head_count,),
         in_specs=[
             pl.BlockSpec((1, window_len), lambda h: (0, 0)),
-            pl.BlockSpec((1, cache_len), lambda h: (0, 0)),
-            pl.BlockSpec((query_rows, HS), lambda h: (0, h)),
+            pl.BlockSpec((1, block_len), lambda h: (0, 0)),
+            head_spec,
             pl.BlockSpec((window_len, HS), lambda h: (0, h)),
             pl.BlockSpec((window_len, HS), lambda h: (0, h)),
-        ]
-        + [pl.BlockSpec((2 * cap, tile_len, HS), lambda h: (0, 0, h)) for _ in cache_list],
-        out_specs=pl.BlockSpec((query_rows, HS), lambda h: (0, h)),
-        out_shape=jax.ShapeDtypeStruct((query_rows, channels), jnp.bfloat16),
-        compiler_params=pltpu.CompilerParams(vmem_limit_bytes=60 * 1024 * 1024),
+            cache_spec,
+        ],
+        out_specs=[head_spec, head_spec, head_spec],
+        out_shape=[wide_shape, wide_shape, wide_shape],
+        compiler_params=params,
     )(
         window_valid.astype(jnp.int32)[None, :],
-        cache_valid.astype(jnp.int32)[None, :],
+        center_valid,
         flat_q,
         flat_wk,
         flat_wv,
-        *cache_list,
-    )
+        cache_in[0, 0],
+    )
+    heads_out = pl.pallas_call(
+        cache_kernel,
+        grid=(head_count,),
+        in_specs=[
+            pl.BlockSpec((1, remote_valid.shape[1]), lambda h: (0, 0)),
+            head_spec,
+            head_spec,
+            head_spec,
+            head_spec,
+        ]
+        + [cache_spec for _ in remote_list],
+        out_specs=head_spec,
+        out_shape=jax.ShapeDtypeStruct((query_rows, channels), jnp.bfloat16),
+        compiler_params=params,
+    )(remote_valid, flat_q, first_acc, first_top, first_total, *remote_list)
     result = heads_out.reshape(1, frames_now, tile_len, channels)
     return result
 

time: 221 us -> 210 us (0.950)
  the two profiles are of different devices: /device:TPU:228 before, /device:TPU:65 now
where the time goes in v6:
time: 210 us; the launch traced here: 209 us
  starting transfers between devices  83.9 us (40%)
  waiting for transfers between devices  76 us (36%)
  Pallas kernels  25.7 us (12%)
  other arithmetic  11 us (5%)
  local copies, waits for them, and re-layouts  8.92 us (4%)
  between operations  3.04 us (1%)
    ppermute x16, starting transfers between devices, shifted(): return lax.ppermute(x, axis, pairs)  76.5 us
    ppermute x16, waiting for transfers between devices, shifted(): return lax.ppermute(x, axis, pairs)  76 us
    pallas_call x1, Pallas kernels, body(): pl.pallas_call(cache_kernel, grid=(head_count,), in_specs=[pl.BlockSpec((...  10.7 us
    pallas_call x1, Pallas kernels, body(): pl.pallas_call(window_kernel, grid=(head_count,), in_specs=[pl.BlockSpec(...  9.68 us
    ppermute x2, starting transfers between devices, hd_sum(): x = x + lax.ppermute(x, 'hd', pairs)  7.42 us
    pallas_call x1, Pallas kernels, body(): pl.pallas_call(pick_kernel, grid_spec=pltpu.PrefetchScalarGridSpec(num_sc...  5.36 us
  transfers between devices with their start and end apart: 18, of which 4 were waited for; matrix products, arithmetic and copies ran while one was open for 8% of the time, Pallas kernels for 7%

profile of v6, /device:TPU:65, one launch (start us, length us, event | category | flops | bytes accessed | tf_op | source)
XLA Modules:
  0.0 208.6 jit_solution(7597530214510154055)
XLA Ops:
  0.0 1.3 multiply_reduce_fusion.1
  1.3 1.2 multiply_reduce_fusion
  2.5 3.2 %collective-permute-start = (f32[2,3,128]{2,1,0:T(4,128)S(1)}, f32[2,3,128]{2,1,0:T(4,128)S(1)}, u32[]{:S(2)}, u32[]{:S(2)}) collective-permute-start(f32[2,3,128]{2,1,0:T(4,128)S(1)} %pad_maximum_fusion.1), channel_id=1, source_target_pairs={{0,1},{1,0},{2,3},{3,2},{4,5},{5,4},{6,7},{7,6},{8,9},{9,8},{10,11... | collective-permute-start | bytes 9224 | tf_op jit(solution)/shard_map/ppermute | solution.py:43
  5.8 1.5 fusion.29
  7.2 0.9 copy.19
  8.2 1.4 fusion.26
  9.6 0.1 copy.15
  9.7 0.1 copy.16
  9.8 0.1 copy.17
  9.8 0.1 copy.18
  9.9 0.1 broadcast_bitcast_fusion
  10.0 0.1 broadcast_bitcast_fusion.1
  10.1 0.7 gather_fusion
  12.1 0.0 collective-permute-done
  12.2 4.2 %collective-permute-start.1 = (f32[2,3,128]{2,1,0:T(4,128)S(1)}, f32[2,3,128]{2,1,0:T(4,128)S(1)}, u32[]{:S(2)}, u32[]{:S(2)}) collective-permute-start(f32[2,3,128]{2,1,0:T(4,128)S(1)} %fusion.25), channel_id=1, source_target_pairs={{0,2},{1,3},{2,0},{3,1},{4,6},{5,7},{6,4},{7,5},{8,10},{9,11},{10,... | collective-permute-start | bytes 9224 | tf_op jit(solution)/shard_map/ppermute | solution.py:43
  17.0 0.6 copy.22
  17.6 0.6 min.22.idx_ref
  18.9 5.4 %shard_map.91 = (bf16[4,128,640]{2,1,0:T(8,128)(2,1)}, bf16[4,128,640]{2,1,0:T(8,128)(2,1)}, bf16[4,128,640]{2,1,0:T(8,128)(2,1)}, bf16[4,128,640]{2,1,0:T(8,128...) custom-call(s32[18]{0:T(128)} %min.22.idx_ref, ...), custom_call_target="tpu_custom_call" | custom-call | tf_op jit(solution)/shard_map/pallas_call | solution.py:149
  24.2 0.0 collective-permute-done.1
  24.3 0.1 rsqrt.23
  24.4 0.0 copy-start.2
  24.4 0.0 copy-start.8
  24.4 0.2 multiply_convert_fusion
  24.6 0.2 fusion.6
  24.8 8.3 %collective-permute-start.2 = (bf16[2,3,4,4,640]{4,3,2,1,0:T(4,128)(2,1)S(1)}, bf16[2,3,4,4,640]{4,3,2,1,0:T(4,128)(2,1)}, u32[]{:S(2)}, u32[]{:S(2)}) collective-permute-start(bf16[2,3,4,4,640]{4,3,2,1,0:T(4,128)(2,1)S(1)} %get-tuple-element.33), channel_id=1, source_target_pairs={{0,36},{4,40},{8,44},{12,48},{16,52},{20,56},{24,60},{28,64},{32,6... | collective-permute-start | bytes 368648 | tf_op jit(solution)/shard_map/ppermute | solution.py:23
  33.1 1.9 collective-permute-start.4
  35.1 10.9 %collective-permute-start.7 = (bf16[2,3,4,4,640]{4,3,2,1,0:T(4,128)(2,1)S(1)}, bf16[2,3,4,4,640]{4,3,2,1,0:T(4,128)(2,1)}, u32[]{:S(2)}, u32[]{:S(2)}) collective-permute-start(bf16[2,3,4,4,640]{4,3,2,1,0:T(4,128)(2,1)S(1)} %get-tuple-element.35), channel_id=1, source_target_pairs={{28,0},{32,4},{36,8},{40,12},{44,16},{48,20},{52,24},{56,28},{60,3... | collective-permute-start | bytes 368648 | tf_op jit(solution)/shard_map/ppermute | solution.py:23
  45.9 1.9 collective-permute-start.9
  47.8 0.3 fusion.4
  48.1 8.1 %collective-permute-start.5 = (bf16[2,3,8,4,640]{4,3,2,1,0:T(4,128)(2,1)S(1)}, bf16[2,3,8,4,640]{4,3,2,1,0:T(4,128)(2,1)S(1)}, u32[]{:S(2)}, u32[]{:S(2)}) collective-permute-start(bf16[2,3,8,4,640]{4,3,2,1,0:T(4,128)(2,1)S(1)} %get-tuple-element.39), channel_id=1, source_target_pairs={{0,4},{4,8},{8,12},{12,16},{16,20},{20,24},{24,28},{28,32},{32,36}... | collective-permute-start | bytes 737288 | tf_op jit(solution)/shard_map/ppermute | solution.py:23
  56.3 1.9 collective-permute-start.6
  58.2 0.0 collective-permute-done.4
  58.2 9.4 %collective-permute-start.10 = (bf16[4,128,640]{2,1,0:T(8,128)(2,1)}, bf16[4,128,640]{2,1,0:T(8,128)(2,1)S(1)}, u32[]{:S(2)}, u32[]{:S(2)}) collective-permute-start(bf16[4,128,640]{2,1,0:T(8,128)(2,1)} %get-tuple-element.21), channel_id=1, source_target_pairs={{0,36},{4,40},{8,44},{12,48},{16,52},{20,56},{24,60},{28,64},{32,6... | collective-permute-start | bytes 1966088 | tf_op jit(solution)/shard_map/ppermute | solution.py:23
  67.6 0.0 collective-permute-done.7
  67.6 3.9 %collective-permute-start.11 = (bf16[4,128,640]{2,1,0:T(8,128)(2,1)}, bf16[4,128,640]{2,1,0:T(8,128)(2,1)S(1)}, u32[]{:S(2)}, u32[]{:S(2)}) collective-permute-start(bf16[4,128,640]{2,1,0:T(8,128)(2,1)} %get-tuple-element.22), channel_id=1, source_target_pairs={{0,32},{4,36},{8,40},{12,44},{16,48},{20,52},{24,56},{28,60},{32,6... | collective-permute-start | bytes 1966088 | tf_op jit(solution)/shard_map/ppermute | solution.py:23
  71.6 0.0 collective-permute-done.9
  71.6 1.9 collective-permute-start.12
  73.5 1.1 fusion.3
  74.6 4.6 %collective-permute-start.3 = (bf16[2,3,4,16,640]{4,3,2,1,0:T(8,128)(2,1)}, bf16[2,3,4,16,640]{4,3,2,1,0:T(8,128)(2,1)S(1)}, u32[]{:S(2)}, u32[]{:S(2)}) collective-permute-start(bf16[2,3,4,16,640]{4,3,2,1,0:T(8,128)(2,1)} %get-tuple-element.37), channel_id=1, source_target_pairs={{0,32},{4,36},{8,40},{12,44},{16,48},{20,52},{24,56},{28,60},{32,6... | collective-permute-start | bytes 1474568 | tf_op jit(solution)/shard_map/ppermute | solution.py:23
  79.3 3.0 %collective-permute-start.8 = (bf16[2,3,4,16,640]{4,3,2,1,0:T(8,128)(2,1)}, bf16[2,3,4,16,640]{4,3,2,1,0:T(8,128)(2,1)}, u32[]{:S(2)}, u32[]{:S(2)}) collective-permute-start(bf16[2,3,4,16,640]{4,3,2,1,0:T(8,128)(2,1)} %get-tuple-element.38), channel_id=1, source_target_pairs={{32,0},{36,4},{40,8},{44,12},{48,16},{52,20},{56,24},{60,28},{64,3... | collective-permute-start | bytes 1474568 | tf_op jit(solution)/shard_map/ppermute | solution.py:23
  82.3 0.1 and_convert_fusion
  82.4 0.7 convert_element_type.74.wvalid_ref
  83.1 0.7 fusion.14
  83.8 1.0 fusion.1.q_ref
  84.8 36.1 %collective-permute-done.3 = bf16[2,3,4,16,640]{4,3,2,1,0:T(8,128)(2,1)S(1)} collective-permute-done((bf16[2,3,4,16,640]{4,3,2,1,0:T(8,128)(2,1)}, bf16[2,3,4,16,640]{4,3,2,1,0:T(8,128)(2,1)S(1)}, u32[]{:S(2)}, u32[]{:S(2)}) %collective-permute-start.3) | collective-permute-done | bytes 491552 | tf_op jit(solution)/shard_map/ppermute | solution.py:23
  120.9 0.8 copy-done.6
  121.7 10.9 %collective-permute-start.13 = (bf16[4,128,640]{2,1,0:T(8,128)(2,1)}, bf16[4,128,640]{2,1,0:T(8,128)(2,1)S(1)}, u32[]{:S(2)}, u32[]{:S(2)}) collective-permute-start(bf16[4,128,640]{2,1,0:T(8,128)(2,1)} %get-tuple-element.24), channel_id=1, source_target_pairs={{0,4},{4,8},{8,12},{12,16},{16,20},{20,24},{24,28},{28,32},{32,36}... | collective-permute-start | bytes 1966088 | tf_op jit(solution)/shard_map/ppermute | solution.py:23
  132.6 0.0 collective-permute-done.8
  132.6 1.9 collective-permute-start.14
  134.5 0.0 collective-permute-done.10.rest_0_
  134.5 3.8 %collective-permute-start.15 = (bf16[4,128,640]{2,1,0:T(8,128)(2,1)}, bf16[4,128,640]{2,1,0:T(8,128)(2,1)}, u32[]{:S(2)}, u32[]{:S(2)}) collective-permute-start(bf16[4,128,640]{2,1,0:T(8,128)(2,1)} %get-tuple-element.26), channel_id=1, source_target_pairs={{28,0},{32,4},{36,8},{40,12},{44,16},{48,20},{52,24},{56,28},{60,3... | collective-permute-start | bytes 1966088 | tf_op jit(solution)/shard_map/ppermute | solution.py:23
  138.4 0.0 collective-permute-done.11.rest_1_
  138.4 1.9 collective-permute-start.16
  140.3 0.0 collective-permute-done.12.rest_2_
  140.3 1.9 collective-permute-start.17
  142.3 3.5 %maximum_maximum_fusion = bf16[2,3,16,24,640]{4,3,2,1,0:T(8,128)(2,1)S(1)} fusion(bf16[2,3,4,4,640]{4,3,2,1,0:T(4,128)(2,1)} %collective-permute-done.9, bf16[2,3,4,16,640]{4,3,2,1,0:T(8,128)(2,1)} %collective-permute-done.8, bf16[2,3,4,4,640]{4,3,2,1,0:T(4,128)(2,1)} %collective-permute-done.7, bf16[2,3,8,4,640]{4,3,2,1,0:T(4,128)(2,1)} %collective-permute-done.6, ...), kind=kLoop, calls=%fused_computation.1 | loop fusion | flops 29491200 | bytes 5898240 | tf_op jit(solution)/shard_map/concatenate | solution.py:195
  145.8 1.9 fusion.27
  147.7 0.6 broadcast_in_dim.11
  148.4 9.7 %shard_map.92 = (f32[384,640]{1,0:T(8,128)}, f32[384,640]{1,0:T(8,128)}, f32[384,640]{1,0:T(8,128)}) custom-call(s32[1,1152]{1,0:T(1,128)} %convert_element_type.74.wvalid_ref, s32[1,256]{1,0:T(1,128)} %bitcast.57, bf16[384,640]{1,0:T(8,128)(2,1)} %fusion.1.q_ref, bf16[1152,640]{1,0:T(8,128)(2,1)} %bitcast.44, bf16[1152,640]{1,0:T(8,128)(2,1)} %bitcast.43, ...), custom_call_target="tpu_custom_call" | custom-call | tf_op jit(solution)/shard_map/pallas_call | solution.py:238
  158.0 0.0 collective-permute-done.13.rest_3_
  158.1 5.1 %collective-permute-done.14.rest_4_ = bf16[4,128,640]{2,1,0:T(8,128)(2,1)} collective-permute-done((bf16[4,128,640]{2,1,0:T(8,128)(2,1)}, bf16[4,128,640]{2,1,0:T(8,128)(2,1)}, u32[]{:S(2)}, u32[]{:S(2)}) %collective-permute-start.14) | collective-permute-done | bytes 655392 | tf_op jit(solution)/shard_map/ppermute | solution.py:23
  163.1 10.4 %collective-permute-done.15.rest_5_ = bf16[4,128,640]{2,1,0:T(8,128)(2,1)} collective-permute-done((bf16[4,128,640]{2,1,0:T(8,128)(2,1)}, bf16[4,128,640]{2,1,0:T(8,128)(2,1)}, u32[]{:S(2)}, u32[]{:S(2)}) %collective-permute-start.15) | collective-permute-done | bytes 655392 | tf_op jit(solution)/shard_map/ppermute | solution.py:23
  173.6 24.4 %collective-permute-done.17.rest_7_ = bf16[4,128,640]{2,1,0:T(8,128)(2,1)} collective-permute-done((bf16[4,128,640]{2,1,0:T(8,128)(2,1)}, bf16[4,128,640]{2,1,0:T(8,128)(2,1)}, u32[]{:S(2)}, u32[]{:S(2)}) %collective-permute-start.17) | collective-permute-done | bytes 655392 | tf_op jit(solution)/shard_map/ppermute | solution.py:23
  197.9 10.7 %shard_map.93 = bf16[384,640]{1,0:T(8,128)(2,1)} custom-call(s32[1,2048]{1,0:T(1,128)} %bitcast.54, bf16[384,640]{1,0:T(8,128)(2,1)} %fusion.1.q_ref, f32[384,640]{1,0:T(8,128)} %get-tuple-element.18.acc_ref, f32[384,640]{1,0:T(8,128)} %get-tuple-element.19.m_ref, f32[384,640]{1,0:T(8,128)} %get-tuple-element.20.l_ref, bf16[4,128,640]{2,1,0:T(8,128)(2,1)} %copy-done.3, ...), custom_call_target="tpu_custom_call" | custom-call | tf_op jit(solution)/shard_map/pallas_call | solution.py:260
  (31 shorter events, 0.1 us)
Async XLA Ops:
  0.0 24.4 %copy-start.1 = (bf16[1,3,128,640]{3,2,1,0:T(8,128)(2,1)S(1)}, bf16[1,3,128,640]{3,2,1,0:T(8,128)(2,1)}, u32[]{:S(2)}) copy-start(bf16[1,3,128,640]{3,2,1,0:T(8,128)(2,1)} %param.10) | copy-start | bytes 1474564
  0.0 24.4 %copy-start.7 = (f32[640]{0:T(1024)S(1)}, f32[640]{0:T(1024)}, u32[]{:S(2)}) copy-start(f32[640]{0:T(1024)} %param.15) | copy-start | bytes 7684
  0.0 24.6 %copy-start = (bf16[1,3,128,640]{3,2,1,0:T(8,128)(2,1)S(1)}, bf16[1,3,128,640]{3,2,1,0:T(8,128)(2,1)}, u32[]{:S(2)}) copy-start(bf16[1,3,128,640]{3,2,1,0:T(8,128)(2,1)} %param.11) | copy-start | bytes 1474564
  2.5 9.6 %collective-permute-start = (f32[2,3,128]{2,1,0:T(4,128)S(1)}, f32[2,3,128]{2,1,0:T(4,128)S(1)}, u32[]{:S(2)}, u32[]{:S(2)}) collective-permute-start(f32[2,3,128]{2,1,0:T(4,128)S(1)} %pad_maximum_fusion.1), channel_id=1, source_target_pairs={{0,1},{1,0},{2,3},{3,2},{4,5},{5,4},{6,7},{7,6},{8,9},{9,8},{10,11... | collective-permute-start | bytes 9224 | tf_op jit(solution)/shard_map/ppermute | solution.py:43
  12.2 12.1 %collective-permute-start.1 = (f32[2,3,128]{2,1,0:T(4,128)S(1)}, f32[2,3,128]{2,1,0:T(4,128)S(1)}, u32[]{:S(2)}, u32[]{:S(2)}) collective-permute-start(f32[2,3,128]{2,1,0:T(4,128)S(1)} %fusion.25), channel_id=1, source_target_pairs={{0,2},{1,3},{2,0},{3,1},{4,6},{5,7},{6,4},{7,5},{8,10},{9,11},{10,... | collective-permute-start | bytes 9224 | tf_op jit(solution)/shard_map/ppermute | solution.py:43
  24.4 59.4 %copy-start.2 = (bf16[1,3,128,640]{3,2,1,0:T(8,128)(2,1)S(1)}, bf16[1,3,128,640]{3,2,1,0:T(8,128)(2,1)}, u32[]{:S(2)}) copy-start(bf16[1,3,128,640]{3,2,1,0:T(8,128)(2,1)} %param.9) | copy-start | bytes 1474564
  24.4 59.4 %copy-start.8 = (f32[640]{0:T(1024)S(1)}, f32[640]{0:T(1024)}, u32[]{:S(2)}) copy-start(f32[640]{0:T(1024)} %param.14) | copy-start | bytes 7684
  24.8 31.5 %collective-permute-start.2 = (bf16[2,3,4,4,640]{4,3,2,1,0:T(4,128)(2,1)S(1)}, bf16[2,3,4,4,640]{4,3,2,1,0:T(4,128)(2,1)}, u32[]{:S(2)}, u32[]{:S(2)}) collective-permute-start(bf16[2,3,4,4,640]{4,3,2,1,0:T(4,128)(2,1)S(1)} %get-tuple-element.33), channel_id=1, source_target_pairs={{0,36},{4,40},{8,44},{12,48},{16,52},{20,56},{24,60},{28,64},{32,6... | collective-permute-start | bytes 368648 | tf_op jit(solution)/shard_map/ppermute | solution.py:23
  33.1 25.1 %collective-permute-start.4 = (bf16[2,3,4,4,640]{4,3,2,1,0:T(4,128)(2,1)S(1)}, bf16[2,3,4,4,640]{4,3,2,1,0:T(4,128)(2,1)}, u32[]{:S(2)}, u32[]{:S(2)}) collective-permute-start(bf16[2,3,4,4,640]{4,3,2,1,0:T(4,128)(2,1)S(1)} %get-tuple-element.34), channel_id=1, source_target_pairs={{0,28},{4,32},{8,36},{12,40},{16,44},{20,48},{24,52},{28,56},{32,6... | collective-permute-start | bytes 368648 | tf_op jit(solution)/shard_map/ppermute | solution.py:23
  35.1 32.6 %collective-permute-start.7 = (bf16[2,3,4,4,640]{4,3,2,1,0:T(4,128)(2,1)S(1)}, bf16[2,3,4,4,640]{4,3,2,1,0:T(4,128)(2,1)}, u32[]{:S(2)}, u32[]{:S(2)}) collective-permute-start(bf16[2,3,4,4,640]{4,3,2,1,0:T(4,128)(2,1)S(1)} %get-tuple-element.35), channel_id=1, source_target_pairs={{28,0},{32,4},{36,8},{40,12},{44,16},{48,20},{52,24},{56,28},{60,3... | collective-permute-start | bytes 368648 | tf_op jit(solution)/shard_map/ppermute | solution.py:23
  45.9 25.7 %collective-permute-start.9 = (bf16[2,3,4,4,640]{4,3,2,1,0:T(4,128)(2,1)S(1)}, bf16[2,3,4,4,640]{4,3,2,1,0:T(4,128)(2,1)}, u32[]{:S(2)}, u32[]{:S(2)}) collective-permute-start(bf16[2,3,4,4,640]{4,3,2,1,0:T(4,128)(2,1)S(1)} %get-tuple-element.36), channel_id=1, source_target_pairs={{36,0},{40,4},{44,8},{48,12},{52,16},{56,20},{60,24},{64,28},{68,3... | collective-permute-start | bytes 368648 | tf_op jit(solution)/shard_map/ppermute | solution.py:23
  48.1 26.5 %collective-permute-start.5 = (bf16[2,3,8,4,640]{4,3,2,1,0:T(4,128)(2,1)S(1)}, bf16[2,3,8,4,640]{4,3,2,1,0:T(4,128)(2,1)S(1)}, u32[]{:S(2)}, u32[]{:S(2)}) collective-permute-start(bf16[2,3,8,4,640]{4,3,2,1,0:T(4,128)(2,1)S(1)} %get-tuple-element.39), channel_id=1, source_target_pairs={{0,4},{4,8},{8,12},{12,16},{16,20},{20,24},{24,28},{28,32},{32,36}... | collective-permute-start | bytes 737288 | tf_op jit(solution)/shard_map/ppermute | solution.py:23
  56.3 23.0 %collective-permute-start.6 = (bf16[2,3,8,4,640]{4,3,2,1,0:T(4,128)(2,1)S(1)}, bf16[2,3,8,4,640]{4,3,2,1,0:T(4,128)(2,1)}, u32[]{:S(2)}, u32[]{:S(2)}) collective-permute-start(bf16[2,3,8,4,640]{4,3,2,1,0:T(4,128)(2,1)S(1)} %get-tuple-element.40), channel_id=1, source_target_pairs={{4,0},{8,4},{12,8},{16,12},{20,16},{24,20},{28,24},{32,28},{36,32}... | collective-permute-start | bytes 737288 | tf_op jit(solution)/shard_map/ppermute | solution.py:23
  58.2 76.3 %collective-permute-start.10 = (bf16[4,128,640]{2,1,0:T(8,128)(2,1)}, bf16[4,128,640]{2,1,0:T(8,128)(2,1)S(1)}, u32[]{:S(2)}, u32[]{:S(2)}) collective-permute-start(bf16[4,128,640]{2,1,0:T(8,128)(2,1)} %get-tuple-element.21), channel_id=1, source_target_pairs={{0,36},{4,40},{8,44},{12,48},{16,52},{20,56},{24,60},{28,64},{32,6... | collective-permute-start | bytes 1966088 | tf_op jit(solution)/shard_map/ppermute | solution.py:23
  67.6 70.7 %collective-permute-start.11 = (bf16[4,128,640]{2,1,0:T(8,128)(2,1)}, bf16[4,128,640]{2,1,0:T(8,128)(2,1)S(1)}, u32[]{:S(2)}, u32[]{:S(2)}) collective-permute-start(bf16[4,128,640]{2,1,0:T(8,128)(2,1)} %get-tuple-element.22), channel_id=1, source_target_pairs={{0,32},{4,36},{8,40},{12,44},{16,48},{20,52},{24,56},{28,60},{32,6... | collective-permute-start | bytes 1966088 | tf_op jit(solution)/shard_map/ppermute | solution.py:23
  71.6 68.7 %collective-permute-start.12 = (bf16[4,128,640]{2,1,0:T(8,128)(2,1)}, bf16[4,128,640]{2,1,0:T(8,128)(2,1)}, u32[]{:S(2)}, u32[]{:S(2)}) collective-permute-start(bf16[4,128,640]{2,1,0:T(8,128)(2,1)} %get-tuple-element.23), channel_id=1, source_target_pairs={{0,28},{4,32},{8,36},{12,40},{16,44},{20,48},{24,52},{28,56},{32,6... | collective-permute-start | bytes 1966088 | tf_op jit(solution)/shard_map/ppermute | solution.py:23
  74.6 46.3 %collective-permute-start.3 = (bf16[2,3,4,16,640]{4,3,2,1,0:T(8,128)(2,1)}, bf16[2,3,4,16,640]{4,3,2,1,0:T(8,128)(2,1)S(1)}, u32[]{:S(2)}, u32[]{:S(2)}) collective-permute-start(bf16[2,3,4,16,640]{4,3,2,1,0:T(8,128)(2,1)} %get-tuple-element.37), channel_id=1, source_target_pairs={{0,32},{4,36},{8,40},{12,44},{16,48},{20,52},{24,56},{28,60},{32,6... | collective-permute-start | bytes 1474568 | tf_op jit(solution)/shard_map/ppermute | solution.py:23
  79.3 53.3 %collective-permute-start.8 = (bf16[2,3,4,16,640]{4,3,2,1,0:T(8,128)(2,1)}, bf16[2,3,4,16,640]{4,3,2,1,0:T(8,128)(2,1)}, u32[]{:S(2)}, u32[]{:S(2)}) collective-permute-start(bf16[2,3,4,16,640]{4,3,2,1,0:T(8,128)(2,1)} %get-tuple-element.38), channel_id=1, source_target_pairs={{32,0},{36,4},{40,8},{44,12},{48,16},{52,20},{56,24},{60,28},{64,3... | collective-permute-start | bytes 1474568 | tf_op jit(solution)/shard_map/ppermute | solution.py:23
  120.9 0.8 copy-start.6
  121.7 36.4 %collective-permute-start.13 = (bf16[4,128,640]{2,1,0:T(8,128)(2,1)}, bf16[4,128,640]{2,1,0:T(8,128)(2,1)S(1)}, u32[]{:S(2)}, u32[]{:S(2)}) collective-permute-start(bf16[4,128,640]{2,1,0:T(8,128)(2,1)} %get-tuple-element.24), channel_id=1, source_target_pairs={{0,4},{4,8},{8,12},{12,16},{16,20},{20,24},{24,28},{28,32},{32,36}... | collective-permute-start | bytes 1966088 | tf_op jit(solution)/shard_map/ppermute | solution.py:23
  132.6 30.6 %collective-permute-start.14 = (bf16[4,128,640]{2,1,0:T(8,128)(2,1)}, bf16[4,128,640]{2,1,0:T(8,128)(2,1)}, u32[]{:S(2)}, u32[]{:S(2)}) collective-permute-start(bf16[4,128,640]{2,1,0:T(8,128)(2,1)} %get-tuple-element.25), channel_id=1, source_target_pairs={{4,0},{8,4},{12,8},{16,12},{20,16},{24,20},{28,24},{32,28},{36,32}... | collective-permute-start | bytes 1966088 | tf_op jit(solution)/shard_map/ppermute | solution.py:23
  134.5 11.3 %copy-start.3 = (bf16[4,128,640]{2,1,0:T(8,128)(2,1)}, bf16[4,128,640]{2,1,0:T(8,128)(2,1)S(1)}, u32[]{:S(2)}) copy-start(bf16[4,128,640]{2,1,0:T(8,128)(2,1)S(1)} %collective-permute-done.10.rest_0_) | copy-start | bytes 1966084
  134.5 39.0 %collective-permute-start.15 = (bf16[4,128,640]{2,1,0:T(8,128)(2,1)}, bf16[4,128,640]{2,1,0:T(8,128)(2,1)}, u32[]{:S(2)}, u32[]{:S(2)}) collective-permute-start(bf16[4,128,640]{2,1,0:T(8,128)(2,1)} %get-tuple-element.26), channel_id=1, source_target_pairs={{28,0},{32,4},{36,8},{40,12},{44,16},{48,20},{52,24},{56,28},{60,3... | collective-permute-start | bytes 1966088 | tf_op jit(solution)/shard_map/ppermute | solution.py:23
  138.4 7.4 %copy-start.4 = (bf16[4,128,640]{2,1,0:T(8,128)(2,1)}, bf16[4,128,640]{2,1,0:T(8,128)(2,1)S(1)}, u32[]{:S(2)}) copy-start(bf16[4,128,640]{2,1,0:T(8,128)(2,1)S(1)} %collective-permute-done.11.rest_1_) | copy-start | bytes 1966084
  138.4 35.2 %collective-permute-start.16 = (bf16[4,128,640]{2,1,0:T(8,128)(2,1)}, bf16[4,128,640]{2,1,0:T(8,128)(2,1)}, u32[]{:S(2)}, u32[]{:S(2)}) collective-permute-start(bf16[4,128,640]{2,1,0:T(8,128)(2,1)} %get-tuple-element.27), channel_id=1, source_target_pairs={{32,0},{36,4},{40,8},{44,12},{48,16},{52,20},{56,24},{60,28},{64,3... | collective-permute-start | bytes 1966088 | tf_op jit(solution)/shard_map/ppermute | solution.py:23
  140.3 57.6 %collective-permute-start.17 = (bf16[4,128,640]{2,1,0:T(8,128)(2,1)}, bf16[4,128,640]{2,1,0:T(8,128)(2,1)}, u32[]{:S(2)}, u32[]{:S(2)}) collective-permute-start(bf16[4,128,640]{2,1,0:T(8,128)(2,1)} %get-tuple-element.28), channel_id=1, source_target_pairs={{36,0},{40,4},{44,8},{48,12},{52,16},{56,20},{60,24},{64,28},{68,3... | collective-permute-start | bytes 1966088 | tf_op jit(solution)/shard_map/ppermute | solution.py:23
  158.1 39.9 %copy-start.5 = (bf16[4,128,640]{2,1,0:T(8,128)(2,1)}, bf16[4,128,640]{2,1,0:T(8,128)(2,1)S(1)}, u32[]{:S(2)}) copy-start(bf16[4,128,640]{2,1,0:T(8,128)(2,1)S(1)} %collective-permute-done.13.rest_3_) | copy-start | bytes 1966084

commit v7 on v6

--- a/solution.py
+++ b/solution.py
@@ -166,16 +166,7 @@
         else:
             cache_in[row_step, col_step] = picked[slot]
 
-    query_wide = query[0].astype(jnp.float32)
-    keys_wide = keys[0].astype(jnp.float32)
-    query_total, keys_total = hd_sum(
-        jnp.stack(
-            [jnp.sum(query_wide * query_wide, axis=-1), jnp.sum(keys_wide * keys_wide, axis=-1)]
-        )
-    )
-    query_normed = normalize(query[0], q_gain, query_total, width_all)
-    keys_normed = normalize(keys[0], k_gain, keys_total, width_all)
-    key_grid = keys_normed.reshape(frames_now, TH, TW, channels)
+    key_grid = keys[0].reshape(frames_now, TH, TW, channels)
     value_grid = values[0].reshape(frames_now, TH, TW, channels)
     both_grid = jnp.stack([key_grid, value_grid])
 
@@ -193,7 +184,17 @@
             jnp.concatenate([edge_in[row_step, col_step] for col_step in (-1, 0, 1)], axis=3)
         )
     window = jnp.concatenate(bands, axis=2)
-    flat_wk = window[0].reshape(-1, channels)
+    window_raw = window[0].reshape(-1, channels)
+    query_wide = query[0].reshape(-1, channels).astype(jnp.float32)
+    window_wide = window_raw.astype(jnp.float32)
+    query_rows = query_wide.shape[0]
+    row_sums = hd_sum(
+        jnp.concatenate(
+            [jnp.sum(query_wide * query_wide, axis=-1), jnp.sum(window_wide * window_wide, axis=-1)]
+        )
+    )
+    query_normed = normalize(query[0].reshape(-1, channels), q_gain, row_sums[:query_rows], width_all)
+    flat_wk = normalize(window_raw, k_gain, row_sums[query_rows:], width_all)
     flat_wv = window[1].reshape(-1, channels)
     flat_q = query_normed.reshape(-1, channels)
     margins = window_margins[0]

time: 210 us -> 198 us (0.943)
  the two profiles are of different devices: /device:TPU:65 before, /device:TPU:236 now
where the time goes in v7:
time: 198 us; the launch traced here: 197 us
  starting transfers between devices  82.9 us (42%)
  waiting for transfers between devices  64.5 us (33%)
  Pallas kernels  25.7 us (13%)
  other arithmetic  13.8 us (7%)
  local copies, waits for them, and re-layouts  6.82 us (3%)
  between operations  3.02 us (2%)
    ppermute x16, starting transfers between devices, shifted(): return lax.ppermute(x, axis, pairs)  77.6 us
    ppermute x16, waiting for transfers between devices, shifted(): return lax.ppermute(x, axis, pairs)  38.1 us
    ppermute x2, waiting for transfers between devices, hd_sum(): x = x + lax.ppermute(x, 'hd', pairs)  26.3 us
    pallas_call x1, Pallas kernels, body(): pl.pallas_call(cache_kernel, grid=(head_count,), in_specs=[pl.BlockSpec((...  10.7 us
    pallas_call x1, Pallas kernels, body(): pl.pallas_call(window_kernel, grid=(head_count,), in_specs=[pl.BlockSpec(...  9.67 us
    pallas_call x1, Pallas kernels, body(): pl.pallas_call(pick_kernel, grid_spec=pltpu.PrefetchScalarGridSpec(num_sc...  5.34 us
    ppermute x2, starting transfers between devices, hd_sum(): x = x + lax.ppermute(x, 'hd', pairs)  5.31 us
    another operation x3, other arithmetic, body(): both_grid = jnp.stack([key_grid, value_grid])  4.02 us
  transfers between devices with their start and end apart: 18, of which 7 were waited for; matrix products, arithmetic and copies ran while one was open for 9% of the time, Pallas kernels for 8%

profile of v7, /device:TPU:236, one launch (start us, length us, event | category | flops | bytes accessed | tf_op | source)
XLA Modules:
  0.0 196.8 jit_solution(11545887724899380475)
XLA Ops:
  0.0 0.0 copy-start.2
  0.0 2.3 %fusion.8 = (bf16[2,3,4,4,640]{4,3,2,1,0:T(4,128)(2,1)}, bf16[2,3,4,4,640]{4,3,2,1,0:T(4,128)(2,1)}, bf16[2,3,4,4,640]{4,3,2,1,0:T(4,128)(2,1)}, bf16[2,3,4,4,640]{4,3,2,1,0:T(4,128)(2,1)}) fusion(bf16[1,3,8,16,640]{4,3,2,1,0:T(8,128)(2,1)} %bitcast.40, bf16[1,3,8,16,640]{4,3,2,1,0:T(8,128)(2,1)} %bitcast.44), kind=kLoop, calls=%fused_computation.29 | loop fusion | flops 983040 | bytes 1474560 | tf_op jit(solution)/shard_map/stack | solution.py:171
  2.3 4.9 %collective-permute-start = (bf16[2,3,4,4,640]{4,3,2,1,0:T(4,128)(2,1)}, bf16[2,3,4,4,640]{4,3,2,1,0:T(4,128)(2,1)}, u32[]{:S(2)}, u32[]{:S(2)}) collective-permute-start(bf16[2,3,4,4,640]{4,3,2,1,0:T(4,128)(2,1)} %get-tuple-element.33), channel_id=1, source_target_pairs={{0,36},{4,40},{8,44},{12,48},{16,52},{20,56},{24,60},{28,64},{32,6... | collective-permute-start | bytes 368648 | tf_op jit(solution)/shard_map/ppermute | solution.py:23
  7.2 10.0 %collective-permute-start.2 = (bf16[2,3,4,4,640]{4,3,2,1,0:T(4,128)(2,1)}, bf16[2,3,4,4,640]{4,3,2,1,0:T(4,128)(2,1)}, u32[]{:S(2)}, u32[]{:S(2)}) collective-permute-start(bf16[2,3,4,4,640]{4,3,2,1,0:T(4,128)(2,1)} %get-tuple-element.34), channel_id=1, source_target_pairs={{0,28},{4,32},{8,36},{12,40},{16,44},{20,48},{24,52},{28,56},{32,6... | collective-permute-start | bytes 368648 | tf_op jit(solution)/shard_map/ppermute | solution.py:23
  17.2 1.9 collective-permute-start.5
  19.2 1.4 fusion.5
  20.6 3.3 %collective-permute-start.1 = (bf16[2,3,4,16,640]{4,3,2,1,0:T(8,128)(2,1)S(1)}, bf16[2,3,4,16,640]{4,3,2,1,0:T(8,128)(2,1)S(1)}, u32[]{:S(2)}, u32[]{:S(2)}) collective-permute-start(bf16[2,3,4,16,640]{4,3,2,1,0:T(8,128)(2,1)S(1)} %get-tuple-element.37), channel_id=1, source_target_pairs={{0,32},{4,36},{8,40},{12,44},{16,48},{20,52},{24,56},{28,60},{32,6... | collective-permute-start | bytes 1474568 | tf_op jit(solution)/shard_map/ppermute | solution.py:23
  23.9 4.0 %collective-permute-start.6 = (bf16[2,3,4,16,640]{4,3,2,1,0:T(8,128)(2,1)S(1)}, bf16[2,3,4,16,640]{4,3,2,1,0:T(8,128)(2,1)}, u32[]{:S(2)}, u32[]{:S(2)}) collective-permute-start(bf16[2,3,4,16,640]{4,3,2,1,0:T(8,128)(2,1)S(1)} %get-tuple-element.38), channel_id=1, source_target_pairs={{32,0},{36,4},{40,8},{44,12},{48,16},{52,20},{56,24},{60,28},{64,3... | collective-permute-start | bytes 1474568 | tf_op jit(solution)/shard_map/ppermute | solution.py:23
  28.0 0.7 fusion.29
  30.0 0.2 copy.19
  30.2 0.7 fusion.26
  30.9 0.1 copy.15
  31.0 0.1 copy.16
  31.1 0.1 copy.17
  31.2 0.1 copy.18
  31.3 0.1 broadcast_bitcast_fusion
  31.4 0.7 broadcast_bitcast_fusion.1
  32.1 0.7 gather_fusion
  34.0 0.7 copy_bitcast_fusion
  34.7 0.1 and_convert_fusion
  34.8 0.3 fusion.6
  35.1 0.0 collective-permute-done
  35.1 8.2 %collective-permute-start.7 = (bf16[2,3,4,4,640]{4,3,2,1,0:T(4,128)(2,1)}, bf16[2,3,4,4,640]{4,3,2,1,0:T(4,128)(2,1)}, u32[]{:S(2)}, u32[]{:S(2)}) collective-permute-start(bf16[2,3,4,4,640]{4,3,2,1,0:T(4,128)(2,1)} %get-tuple-element.36), channel_id=1, source_target_pairs={{36,0},{40,4},{44,8},{48,12},{52,16},{56,20},{60,24},{64,28},{68,3... | collective-permute-start | bytes 368648 | tf_op jit(solution)/shard_map/ppermute | solution.py:23
  43.3 1.9 collective-permute-start.3
  45.2 0.0 collective-permute-done.5
  45.2 7.5 %collective-permute-start.4 = (bf16[2,3,8,4,640]{4,3,2,1,0:T(4,128)(2,1)S(1)}, bf16[2,3,8,4,640]{4,3,2,1,0:T(4,128)(2,1)S(1)}, u32[]{:S(2)}, u32[]{:S(2)}) collective-permute-start(bf16[2,3,8,4,640]{4,3,2,1,0:T(4,128)(2,1)S(1)} %get-tuple-element.40), channel_id=1, source_target_pairs={{4,0},{8,4},{12,8},{16,12},{20,16},{24,20},{28,24},{32,28},{36,32}... | collective-permute-start | bytes 737288 | tf_op jit(solution)/shard_map/ppermute | solution.py:23
  52.8 0.2 multiply_reduce_fusion.1
  52.9 0.6 min.22.idx_ref
  53.5 5.3 %shard_map.91 = (bf16[4,128,640]{2,1,0:T(8,128)(2,1)}, bf16[4,128,640]{2,1,0:T(8,128)(2,1)}, bf16[4,128,640]{2,1,0:T(8,128)(2,1)}, bf16[4,128,640]{2,1,0:T(8,128...) custom-call(s32[18]{0:T(128)} %min.22.idx_ref, ...), custom_call_target="tpu_custom_call" | custom-call | tf_op jit(solution)/shard_map/pallas_call | solution.py:149
  58.9 0.0 collective-permute-done.7
  58.9 2.1 %collective-permute-start.10 = (bf16[4,128,640]{2,1,0:T(8,128)(2,1)}, bf16[4,128,640]{2,1,0:T(8,128)(2,1)}, u32[]{:S(2)}, u32[]{:S(2)}) collective-permute-start(bf16[4,128,640]{2,1,0:T(8,128)(2,1)} %get-tuple-element.21), channel_id=1, source_target_pairs={{0,36},{4,40},{8,44},{12,48},{16,52},{20,56},{24,60},{28,64},{32,6... | collective-permute-start | bytes 1966088 | tf_op jit(solution)/shard_map/ppermute | solution.py:23
  61.0 0.5 collective-permute-done.3
  61.5 6.9 %collective-permute-start.11 = (bf16[4,128,640]{2,1,0:T(8,128)(2,1)}, bf16[4,128,640]{2,1,0:T(8,128)(2,1)}, u32[]{:S(2)}, u32[]{:S(2)}) collective-permute-start(bf16[4,128,640]{2,1,0:T(8,128)(2,1)} %get-tuple-element.22), channel_id=1, source_target_pairs={{0,32},{4,36},{8,40},{12,44},{16,48},{20,52},{24,56},{28,60},{32,6... | collective-permute-start | bytes 1966088 | tf_op jit(solution)/shard_map/ppermute | solution.py:23
  68.5 9.7 %collective-permute-start.12 = (bf16[4,128,640]{2,1,0:T(8,128)(2,1)}, bf16[4,128,640]{2,1,0:T(8,128)(2,1)}, u32[]{:S(2)}, u32[]{:S(2)}) collective-permute-start(bf16[4,128,640]{2,1,0:T(8,128)(2,1)} %get-tuple-element.23), channel_id=1, source_target_pairs={{0,28},{4,32},{8,36},{12,40},{16,44},{20,48},{24,52},{28,56},{32,6... | collective-permute-start | bytes 1966088 | tf_op jit(solution)/shard_map/ppermute | solution.py:23
  78.2 0.0 collective-permute-done.1
  78.2 0.0 copy-start.8
  78.2 1.9 collective-permute-start.13
  80.2 3.8 %maximum_maximum_fusion = bf16[2,3,16,24,640]{4,3,2,1,0:T(8,128)(2,1)S(1)} fusion(bf16[2,3,4,4,640]{4,3,2,1,0:T(4,128)(2,1)} %collective-permute-done.7, bf16[2,3,4,16,640]{4,3,2,1,0:T(8,128)(2,1)} %collective-permute-done.6, bf16[2,3,4,4,640]{4,3,2,1,0:T(4,128)(2,1)} %collective-permute-done.5, bf16[2,3,8,4,640]{4,3,2,1,0:T(4,128)(2,1)} %copy-done.10, ...), kind=kLoop, calls=%fused_computation.1 | loop fusion | flops 29491200 | bytes 5898240 | tf_op jit(solution)/shard_map/concatenate | solution.py:186
  84.0 0.4 multiply_reduce_fusion
  84.3 0.1 reduce_sum.25
  84.4 3.3 %collective-permute-start.8 = (f32[1536]{0:T(1024)S(1)}, f32[1536]{0:T(1024)S(1)}, u32[]{:S(2)}, u32[]{:S(2)}) collective-permute-start(f32[1536]{0:T(1024)S(1)} %pad_maximum_fusion.1), channel_id=1, source_target_pairs={{0,1},{1,0},{2,3},{3,2},{4,5},{5,4},{6,7},{7,6},{8,9},{9,8},{10,11... | collective-permute-start | bytes 18440 | tf_op jit(solution)/shard_map/ppermute | solution.py:43
  87.7 0.7 fusion.15
  88.4 0.6 copy.22
  89.0 0.7 convert_element_type.58.wvalid_ref
  89.7 23.3 %collective-permute-done.8 = f32[1536]{0:T(1024)S(1)} collective-permute-done((f32[1536]{0:T(1024)S(1)}, f32[1536]{0:T(1024)S(1)}, u32[]{:S(2)}, u32[]{:S(2)}) %collective-permute-start.8) | collective-permute-done | bytes 6176 | tf_op jit(solution)/shard_map/ppermute | solution.py:43
  113.0 0.0 copy-start.13
  113.0 0.0 copy-start.14
  113.0 2.1 %collective-permute-start.9 = (f32[1536]{0:T(1024)S(1)}, f32[1536]{0:T(1024)S(1)}, u32[]{:S(2)}, u32[]{:S(2)}) collective-permute-start(f32[1536]{0:T(1024)S(1)} %fusion.30), channel_id=1, source_target_pairs={{0,2},{1,3},{2,0},{3,1},{4,6},{5,7},{6,4},{7,5},{8,10},{9,11},{10,... | collective-permute-start | bytes 18440 | tf_op jit(solution)/shard_map/ppermute | solution.py:43
  115.1 1.5 fusion.27
  116.6 3.0 %collective-permute-done.9 = f32[1536]{0:T(1024)S(1)} collective-permute-done((f32[1536]{0:T(1024)S(1)}, f32[1536]{0:T(1024)S(1)}, u32[]{:S(2)}, u32[]{:S(2)}) %collective-permute-start.9) | collective-permute-done | bytes 6176 | tf_op jit(solution)/shard_map/ppermute | solution.py:43
  119.6 5.5 %collective-permute-start.14 = (bf16[4,128,640]{2,1,0:T(8,128)(2,1)}, bf16[4,128,640]{2,1,0:T(8,128)(2,1)S(1)}, u32[]{:S(2)}, u32[]{:S(2)}) collective-permute-start(bf16[4,128,640]{2,1,0:T(8,128)(2,1)} %get-tuple-element.25), channel_id=1, source_target_pairs={{4,0},{8,4},{12,8},{16,12},{20,16},{24,20},{28,24},{32,28},{36,32}... | collective-permute-start | bytes 1966088 | tf_op jit(solution)/shard_map/ppermute | solution.py:23
  125.2 1.0 fusion.3.q_ref
  126.2 1.9 collective-permute-start.15
  128.1 1.9 collective-permute-start.16
  130.1 5.8 %collective-permute-start.17 = (bf16[4,128,640]{2,1,0:T(8,128)(2,1)}, bf16[4,128,640]{2,1,0:T(8,128)(2,1)S(1)}, u32[]{:S(2)}, u32[]{:S(2)}) collective-permute-start(bf16[4,128,640]{2,1,0:T(8,128)(2,1)} %get-tuple-element.28), channel_id=1, source_target_pairs={{36,0},{40,4},{44,8},{48,12},{52,16},{56,20},{60,24},{64,28},{68,3... | collective-permute-start | bytes 1966088 | tf_op jit(solution)/shard_map/ppermute | solution.py:23
  135.9 1.4 fusion.1.wk_ref
  137.4 0.6 broadcast_in_dim.11
  138.0 9.7 %shard_map.92 = (f32[384,640]{1,0:T(8,128)}, f32[384,640]{1,0:T(8,128)}, f32[384,640]{1,0:T(8,128)}) custom-call(s32[1,1152]{1,0:T(1,128)} %convert_element_type.58.wvalid_ref, s32[1,256]{1,0:T(1,128)} %bitcast.56, bf16[384,640]{1,0:T(8,128)(2,1)} %fusion.3.q_ref, bf16[1152,640]{1,0:T(8,128)(2,1)} %fusion.1.wk_ref, bf16[1152,640]{1,0:T(8,128)(2,1)} %bitcast.48, ...), custom_call_target="tpu_custom_call" | custom-call | tf_op jit(solution)/shard_map/pallas_call | solution.py:239
  147.6 6.2 %collective-permute-done.14.rest_4_ = bf16[4,128,640]{2,1,0:T(8,128)(2,1)S(1)} collective-permute-done((bf16[4,128,640]{2,1,0:T(8,128)(2,1)}, bf16[4,128,640]{2,1,0:T(8,128)(2,1)S(1)}, u32[]{:S(2)}, u32[]{:S(2)}) %collective-permute-start.14) | collective-permute-done | bytes 655392 | tf_op jit(solution)/shard_map/ppermute | solution.py:23
  153.8 12.0 %collective-permute-done.15.rest_5_ = bf16[4,128,640]{2,1,0:T(8,128)(2,1)S(1)} collective-permute-done((bf16[4,128,640]{2,1,0:T(8,128)(2,1)}, bf16[4,128,640]{2,1,0:T(8,128)(2,1)S(1)}, u32[]{:S(2)}, u32[]{:S(2)}) %collective-permute-start.15) | collective-permute-done | bytes 655392 | tf_op jit(solution)/shard_map/ppermute | solution.py:23
  165.8 16.7 %collective-permute-done.16.rest_6_ = bf16[4,128,640]{2,1,0:T(8,128)(2,1)S(1)} collective-permute-done((bf16[4,128,640]{2,1,0:T(8,128)(2,1)}, bf16[4,128,640]{2,1,0:T(8,128)(2,1)S(1)}, u32[]{:S(2)}, u32[]{:S(2)}) %collective-permute-start.16) | collective-permute-done | bytes 655392 | tf_op jit(solution)/shard_map/ppermute | solution.py:23
  182.5 2.7 %collective-permute-done.17.rest_7_ = bf16[4,128,640]{2,1,0:T(8,128)(2,1)S(1)} collective-permute-done((bf16[4,128,640]{2,1,0:T(8,128)(2,1)}, bf16[4,128,640]{2,1,0:T(8,128)(2,1)S(1)}, u32[]{:S(2)}, u32[]{:S(2)}) %collective-permute-start.17) | collective-permute-done | bytes 655392 | tf_op jit(solution)/shard_map/ppermute | solution.py:23
  185.2 0.8 copy-done.7
  186.1 10.7 %shard_map.93 = bf16[384,640]{1,0:T(8,128)(2,1)} custom-call(s32[1,2048]{1,0:T(1,128)} %bitcast.51, bf16[384,640]{1,0:T(8,128)(2,1)} %fusion.3.q_ref, f32[384,640]{1,0:T(8,128)} %get-tuple-element.18.acc_ref, f32[384,640]{1,0:T(8,128)} %get-tuple-element.19.m_ref, f32[384,640]{1,0:T(8,128)} %get-tuple-element.20.l_ref, ...), custom_call_target="tpu_custom_call" | custom-call | tf_op jit(solution)/shard_map/pallas_call | solution.py:261
  (44 shorter events, 0.2 us)
Async XLA Ops:
  0.0 34.8 %copy-start.1 = (bf16[1,3,128,640]{3,2,1,0:T(8,128)(2,1)S(1)}, bf16[1,3,128,640]{3,2,1,0:T(8,128)(2,1)}, u32[]{:S(2)}) copy-start(bf16[1,3,128,640]{3,2,1,0:T(8,128)(2,1)} %param.11) | copy-start | bytes 1474564
  0.0 34.8 %copy-start = (bf16[1,3,128,640]{3,2,1,0:T(8,128)(2,1)S(1)}, bf16[1,3,128,640]{3,2,1,0:T(8,128)(2,1)}, u32[]{:S(2)}) copy-start(bf16[1,3,128,640]{3,2,1,0:T(8,128)(2,1)} %param.10) | copy-start | bytes 1474564
  0.0 28.0 %copy-start.12 = (s32[1,4]{1,0:T(1,128)S(1)}, s32[1,4]{1,0:T(1,128)}, u32[]{:S(2)}) copy-start(s32[1,4]{1,0:T(1,128)} %param.16) | copy-start | bytes 52
  0.0 30.0 %copy-start.11 = (s32[128,9,2]{0,2,1:T(2,128)S(1)}, s32[128,9,2]{0,2,1:T(2,128)}, u32[]{:S(2)}) copy-start(s32[128,9,2]{0,2,1:T(2,128)} %param.17) | copy-start | bytes 27652
  0.0 52.7 %copy-start.2 = (bf16[1,3,128,640]{3,2,1,0:T(8,128)(2,1)S(1)}, bf16[1,3,128,640]{3,2,1,0:T(8,128)(2,1)}, u32[]{:S(2)}) copy-start(bf16[1,3,128,640]{3,2,1,0:T(8,128)(2,1)} %param.9) | copy-start | bytes 1474564
  2.3 32.7 %collective-permute-start = (bf16[2,3,4,4,640]{4,3,2,1,0:T(4,128)(2,1)}, bf16[2,3,4,4,640]{4,3,2,1,0:T(4,128)(2,1)}, u32[]{:S(2)}, u32[]{:S(2)}) collective-permute-start(bf16[2,3,4,4,640]{4,3,2,1,0:T(4,128)(2,1)} %get-tuple-element.33), channel_id=1, source_target_pairs={{0,36},{4,40},{8,44},{12,48},{16,52},{20,56},{24,60},{28,64},{32,6... | collective-permute-start | bytes 368648 | tf_op jit(solution)/shard_map/ppermute | solution.py:23
  7.2 36.0 %collective-permute-start.2 = (bf16[2,3,4,4,640]{4,3,2,1,0:T(4,128)(2,1)}, bf16[2,3,4,4,640]{4,3,2,1,0:T(4,128)(2,1)}, u32[]{:S(2)}, u32[]{:S(2)}) collective-permute-start(bf16[2,3,4,4,640]{4,3,2,1,0:T(4,128)(2,1)} %get-tuple-element.34), channel_id=1, source_target_pairs={{0,28},{4,32},{8,36},{12,40},{16,44},{20,48},{24,52},{28,56},{32,6... | collective-permute-start | bytes 368648 | tf_op jit(solution)/shard_map/ppermute | solution.py:23
  17.2 27.9 %collective-permute-start.5 = (bf16[2,3,4,4,640]{4,3,2,1,0:T(4,128)(2,1)}, bf16[2,3,4,4,640]{4,3,2,1,0:T(4,128)(2,1)}, u32[]{:S(2)}, u32[]{:S(2)}) collective-permute-start(bf16[2,3,4,4,640]{4,3,2,1,0:T(4,128)(2,1)} %get-tuple-element.35), channel_id=1, source_target_pairs={{28,0},{32,4},{36,8},{40,12},{44,16},{48,20},{52,24},{56,28},{60,3... | collective-permute-start | bytes 368648 | tf_op jit(solution)/shard_map/ppermute | solution.py:23
  20.6 57.6 %collective-permute-start.1 = (bf16[2,3,4,16,640]{4,3,2,1,0:T(8,128)(2,1)S(1)}, bf16[2,3,4,16,640]{4,3,2,1,0:T(8,128)(2,1)S(1)}, u32[]{:S(2)}, u32[]{:S(2)}) collective-permute-start(bf16[2,3,4,16,640]{4,3,2,1,0:T(8,128)(2,1)S(1)} %get-tuple-element.37), channel_id=1, source_target_pairs={{0,32},{4,36},{8,40},{12,44},{16,48},{20,52},{24,56},{28,60},{32,6... | collective-permute-start | bytes 1474568 | tf_op jit(solution)/shard_map/ppermute | solution.py:23
  23.9 56.2 %collective-permute-start.6 = (bf16[2,3,4,16,640]{4,3,2,1,0:T(8,128)(2,1)S(1)}, bf16[2,3,4,16,640]{4,3,2,1,0:T(8,128)(2,1)}, u32[]{:S(2)}, u32[]{:S(2)}) collective-permute-start(bf16[2,3,4,16,640]{4,3,2,1,0:T(8,128)(2,1)S(1)} %get-tuple-element.38), channel_id=1, source_target_pairs={{32,0},{36,4},{40,8},{44,12},{48,16},{52,20},{56,24},{60,28},{64,3... | collective-permute-start | bytes 1474568 | tf_op jit(solution)/shard_map/ppermute | solution.py:23
  35.1 23.8 %collective-permute-start.7 = (bf16[2,3,4,4,640]{4,3,2,1,0:T(4,128)(2,1)}, bf16[2,3,4,4,640]{4,3,2,1,0:T(4,128)(2,1)}, u32[]{:S(2)}, u32[]{:S(2)}) collective-permute-start(bf16[2,3,4,4,640]{4,3,2,1,0:T(4,128)(2,1)} %get-tuple-element.36), channel_id=1, source_target_pairs={{36,0},{40,4},{44,8},{48,12},{52,16},{56,20},{60,24},{64,28},{68,3... | collective-permute-start | bytes 368648 | tf_op jit(solution)/shard_map/ppermute | solution.py:23
  43.3 18.3 %collective-permute-start.3 = (bf16[2,3,8,4,640]{4,3,2,1,0:T(4,128)(2,1)S(1)}, bf16[2,3,8,4,640]{4,3,2,1,0:T(4,128)(2,1)S(1)}, u32[]{:S(2)}, u32[]{:S(2)}) collective-permute-start(bf16[2,3,8,4,640]{4,3,2,1,0:T(4,128)(2,1)S(1)} %get-tuple-element.39), channel_id=1, source_target_pairs={{0,4},{4,8},{8,12},{12,16},{16,20},{20,24},{24,28},{28,32},{32,36}... | collective-permute-start | bytes 737288 | tf_op jit(solution)/shard_map/ppermute | solution.py:23
  45.2 23.3 %collective-permute-start.4 = (bf16[2,3,8,4,640]{4,3,2,1,0:T(4,128)(2,1)S(1)}, bf16[2,3,8,4,640]{4,3,2,1,0:T(4,128)(2,1)S(1)}, u32[]{:S(2)}, u32[]{:S(2)}) collective-permute-start(bf16[2,3,8,4,640]{4,3,2,1,0:T(4,128)(2,1)S(1)} %get-tuple-element.40), channel_id=1, source_target_pairs={{4,0},{8,4},{12,8},{16,12},{20,16},{24,20},{28,24},{32,28},{36,32}... | collective-permute-start | bytes 737288 | tf_op jit(solution)/shard_map/ppermute | solution.py:23
  58.9 67.3 %collective-permute-start.10 = (bf16[4,128,640]{2,1,0:T(8,128)(2,1)}, bf16[4,128,640]{2,1,0:T(8,128)(2,1)}, u32[]{:S(2)}, u32[]{:S(2)}) collective-permute-start(bf16[4,128,640]{2,1,0:T(8,128)(2,1)} %get-tuple-element.21), channel_id=1, source_target_pairs={{0,36},{4,40},{8,44},{12,48},{16,52},{20,56},{24,60},{28,64},{32,6... | collective-permute-start | bytes 1966088 | tf_op jit(solution)/shard_map/ppermute | solution.py:23
  61.5 18.6 %copy-start.9 = (bf16[2,3,8,4,640]{4,3,2,1,0:T(4,128)(2,1)}, bf16[2,3,8,4,640]{4,3,2,1,0:T(4,128)(2,1)S(1)}, u32[]{:S(2)}) copy-start(bf16[2,3,8,4,640]{4,3,2,1,0:T(4,128)(2,1)S(1)} %collective-permute-done.3) | copy-start | bytes 737284
  61.5 66.6 %collective-permute-start.11 = (bf16[4,128,640]{2,1,0:T(8,128)(2,1)}, bf16[4,128,640]{2,1,0:T(8,128)(2,1)}, u32[]{:S(2)}, u32[]{:S(2)}) collective-permute-start(bf16[4,128,640]{2,1,0:T(8,128)(2,1)} %get-tuple-element.22), channel_id=1, source_target_pairs={{0,32},{4,36},{8,40},{12,44},{16,48},{20,52},{24,56},{28,60},{32,6... | collective-permute-start | bytes 1966088 | tf_op jit(solution)/shard_map/ppermute | solution.py:23
  68.5 11.7 %copy-start.10 = (bf16[2,3,8,4,640]{4,3,2,1,0:T(4,128)(2,1)}, bf16[2,3,8,4,640]{4,3,2,1,0:T(4,128)(2,1)S(1)}, u32[]{:S(2)}) copy-start(bf16[2,3,8,4,640]{4,3,2,1,0:T(4,128)(2,1)S(1)} %collective-permute-done.4) | copy-start | bytes 737284
  68.5 61.5 %collective-permute-start.12 = (bf16[4,128,640]{2,1,0:T(8,128)(2,1)}, bf16[4,128,640]{2,1,0:T(8,128)(2,1)}, u32[]{:S(2)}, u32[]{:S(2)}) collective-permute-start(bf16[4,128,640]{2,1,0:T(8,128)(2,1)} %get-tuple-element.23), channel_id=1, source_target_pairs={{0,28},{4,32},{8,36},{12,40},{16,44},{20,48},{24,52},{28,56},{32,6... | collective-permute-start | bytes 1966088 | tf_op jit(solution)/shard_map/ppermute | solution.py:23
  78.2 2.0 copy-start.8
  78.2 69.4 %collective-permute-start.13 = (bf16[4,128,640]{2,1,0:T(8,128)(2,1)}, bf16[4,128,640]{2,1,0:T(8,128)(2,1)}, u32[]{:S(2)}, u32[]{:S(2)}) collective-permute-start(bf16[4,128,640]{2,1,0:T(8,128)(2,1)} %get-tuple-element.24), channel_id=1, source_target_pairs={{0,4},{4,8},{8,12},{12,16},{16,20},{20,24},{24,28},{28,32},{32,36}... | collective-permute-start | bytes 1966088 | tf_op jit(solution)/shard_map/ppermute | solution.py:23
  84.4 28.6 %collective-permute-start.8 = (f32[1536]{0:T(1024)S(1)}, f32[1536]{0:T(1024)S(1)}, u32[]{:S(2)}, u32[]{:S(2)}) collective-permute-start(f32[1536]{0:T(1024)S(1)} %pad_maximum_fusion.1), channel_id=1, source_target_pairs={{0,1},{1,0},{2,3},{3,2},{4,5},{5,4},{6,7},{7,6},{8,9},{9,8},{10,11... | collective-permute-start | bytes 18440 | tf_op jit(solution)/shard_map/ppermute | solution.py:43
  113.0 12.1 %copy-start.3 = (bf16[1,3,128,640]{3,2,1,0:T(8,128)(2,1)S(1)}, bf16[1,3,128,640]{3,2,1,0:T(8,128)(2,1)}, u32[]{:S(2)}) copy-start(bf16[1,3,128,640]{3,2,1,0:T(8,128)(2,1)} %param.9) | copy-start | bytes 1474564
  113.0 12.1 %copy-start.13 = (f32[640]{0:T(1024)S(1)}, f32[640]{0:T(1024)}, u32[]{:S(2)}) copy-start(f32[640]{0:T(1024)} %param.14) | copy-start | bytes 7684
  113.0 22.9 %copy-start.14 = (f32[640]{0:T(1024)S(1)}, f32[640]{0:T(1024)}, u32[]{:S(2)}) copy-start(f32[640]{0:T(1024)} %param.15) | copy-start | bytes 7684
  113.0 6.6 %collective-permute-start.9 = (f32[1536]{0:T(1024)S(1)}, f32[1536]{0:T(1024)S(1)}, u32[]{:S(2)}, u32[]{:S(2)}) collective-permute-start(f32[1536]{0:T(1024)S(1)} %fusion.30), channel_id=1, source_target_pairs={{0,2},{1,3},{2,0},{3,1},{4,6},{5,7},{6,4},{7,5},{8,10},{9,11},{10,... | collective-permute-start | bytes 18440 | tf_op jit(solution)/shard_map/ppermute | solution.py:43
  119.6 34.2 %collective-permute-start.14 = (bf16[4,128,640]{2,1,0:T(8,128)(2,1)}, bf16[4,128,640]{2,1,0:T(8,128)(2,1)S(1)}, u32[]{:S(2)}, u32[]{:S(2)}) collective-permute-start(bf16[4,128,640]{2,1,0:T(8,128)(2,1)} %get-tuple-element.25), channel_id=1, source_target_pairs={{4,0},{8,4},{12,8},{16,12},{20,16},{24,20},{28,24},{32,28},{36,32}... | collective-permute-start | bytes 1966088 | tf_op jit(solution)/shard_map/ppermute | solution.py:23
  126.2 39.6 %collective-permute-start.15 = (bf16[4,128,640]{2,1,0:T(8,128)(2,1)}, bf16[4,128,640]{2,1,0:T(8,128)(2,1)S(1)}, u32[]{:S(2)}, u32[]{:S(2)}) collective-permute-start(bf16[4,128,640]{2,1,0:T(8,128)(2,1)} %get-tuple-element.26), channel_id=1, source_target_pairs={{28,0},{32,4},{36,8},{40,12},{44,16},{48,20},{52,24},{56,28},{60,3... | collective-permute-start | bytes 1966088 | tf_op jit(solution)/shard_map/ppermute | solution.py:23
  128.1 54.4 %collective-permute-start.16 = (bf16[4,128,640]{2,1,0:T(8,128)(2,1)}, bf16[4,128,640]{2,1,0:T(8,128)(2,1)S(1)}, u32[]{:S(2)}, u32[]{:S(2)}) collective-permute-start(bf16[4,128,640]{2,1,0:T(8,128)(2,1)} %get-tuple-element.27), channel_id=1, source_target_pairs={{32,0},{36,4},{40,8},{44,12},{48,16},{52,20},{56,24},{60,28},{64,3... | collective-permute-start | bytes 1966088 | tf_op jit(solution)/shard_map/ppermute | solution.py:23
  130.1 55.2 %collective-permute-start.17 = (bf16[4,128,640]{2,1,0:T(8,128)(2,1)}, bf16[4,128,640]{2,1,0:T(8,128)(2,1)S(1)}, u32[]{:S(2)}, u32[]{:S(2)}) collective-permute-start(bf16[4,128,640]{2,1,0:T(8,128)(2,1)} %get-tuple-element.28), channel_id=1, source_target_pairs={{36,0},{40,4},{44,8},{48,12},{52,16},{56,20},{60,24},{64,28},{68,3... | collective-permute-start | bytes 1966088 | tf_op jit(solution)/shard_map/ppermute | solution.py:23
  153.8 31.4 %copy-start.4 = (bf16[4,128,640]{2,1,0:T(8,128)(2,1)}, bf16[4,128,640]{2,1,0:T(8,128)(2,1)S(1)}, u32[]{:S(2)}) copy-start(bf16[4,128,640]{2,1,0:T(8,128)(2,1)S(1)} %collective-permute-done.14.rest_4_) | copy-start | bytes 1966084
  165.8 19.4 %copy-start.5 = (bf16[4,128,640]{2,1,0:T(8,128)(2,1)}, bf16[4,128,640]{2,1,0:T(8,128)(2,1)S(1)}, u32[]{:S(2)}) copy-start(bf16[4,128,640]{2,1,0:T(8,128)(2,1)S(1)} %collective-permute-done.15.rest_5_) | copy-start | bytes 1966084
  182.5 2.8 %copy-start.6 = (bf16[4,128,640]{2,1,0:T(8,128)(2,1)}, bf16[4,128,640]{2,1,0:T(8,128)(2,1)S(1)}, u32[]{:S(2)}) copy-start(bf16[4,128,640]{2,1,0:T(8,128)(2,1)S(1)} %collective-permute-done.16.rest_6_) | copy-start | bytes 1966084
  185.2 0.8 copy-start.7

commit v8 on v6

--- a/solution.py
+++ b/solution.py
@@ -88,8 +88,14 @@
 
 
 def cache_kernel(cvalid_ref, q_ref, acc_ref, m_ref, l_ref, *rest):
-    cache_refs = rest[:-1]
-    o_ref = rest[-1]
+    merge_step(cvalid_ref, q_ref, acc_ref, m_ref, l_ref, rest[:-1], rest[-1:])
+
+
+def partial_kernel(cvalid_ref, q_ref, acc_ref, m_ref, l_ref, *rest):
+    merge_step(cvalid_ref, q_ref, acc_ref, m_ref, l_ref, rest[:-3], rest[-3:])
+
+
+def merge_step(cvalid_ref, q_ref, acc_ref, m_ref, l_ref, cache_refs, out_refs):
     cap_rows = cache_refs[0].shape[0] // 2
     tile_len = cache_refs[0].shape[1]
     score_scale = HS ** (-0.5)
@@ -113,7 +119,12 @@
     mixed_out = acc_ref[...] * rescale + jnp.dot(
         cache_exp.astype(jnp.bfloat16), cache_v, preferred_element_type=jnp.float32
     )
-    o_ref[...] = (mixed_out * (1.0 / row_total)).astype(jnp.bfloat16)
+    if len(out_refs) == 1:
+        out_refs[0][...] = (mixed_out * (1.0 / row_total)).astype(jnp.bfloat16)
+    else:
+        out_refs[0][...] = mixed_out
+        out_refs[1][...] = jnp.broadcast_to(row_top, out_refs[1].shape)
+        out_refs[2][...] = jnp.broadcast_to(row_total, out_refs[2].shape)
 
 
 def pick_kernel(idx_ref, k_ref, v_ref, *o_refs):
@@ -257,21 +268,46 @@
         flat_wv,
         cache_in[0, 0],
     )
-    heads_out = pl.pallas_call(
+    half = len(remote_list) // 2
+    remote_valid = remote_valid.reshape(2, -1)
+
+    def merge_call(kernel, valid, acc, top, total, blocks, out_specs, out_shape):
+        return pl.pallas_call(
+            kernel,
+            grid=(head_count,),
+            in_specs=[
+                pl.BlockSpec((1, valid.shape[1]), lambda h: (0, 0)),
+                head_spec,
+                head_spec,
+                head_spec,
+                head_spec,
+            ]
+            + [cache_spec for _ in blocks],
+            out_specs=out_specs,
+            out_shape=out_shape,
+            compiler_params=params,
+        )(valid, flat_q, acc, top, total, *blocks)
+
+    mid_acc, mid_top, mid_total = merge_call(
+        partial_kernel,
+        remote_valid[:1],
+        first_acc,
+        first_top,
+        first_total,
+        remote_list[:half],
+        [head_spec, head_spec, head_spec],
+        [wide_shape, wide_shape, wide_shape],
+    )
+    heads_out = merge_call(
         cache_kernel,
-        grid=(head_count,),
-        in_specs=[
-            pl.BlockSpec((1, remote_valid.shape[1]), lambda h: (0, 0)),
-            head_spec,
-            head_spec,
-            head_spec,
-            head_spec,
-        ]
-        + [cache_spec for _ in remote_list],
-        out_specs=head_spec,
-        out_shape=jax.ShapeDtypeStruct((query_rows, channels), jnp.bfloat16),
-        compiler_params=params,
-    )(remote_valid, flat_q, first_acc, first_top, first_total, *remote_list)
+        remote_valid[1:],
+        mid_acc,
+        mid_top,
+        mid_total,
+        remote_list[half:],
+        head_spec,
+        jax.ShapeDtypeStruct((query_rows, channels), jnp.bfloat16),
+    )
     result = heads_out.reshape(1, frames_now, tile_len, channels)
     return result
 

time: 210 us -> 207 us (0.986)
  the two profiles are of different devices: /device:TPU:65 before, /device:TPU:199 now
where the time goes in v8:
time: 207 us; the launch traced here: 206 us
  starting transfers between devices  84 us (41%)
  waiting for transfers between devices  65.9 us (32%)
  Pallas kernels  31.8 us (15%)
  other arithmetic  11.7 us (6%)
  local copies, waits for them, and re-layouts  9.28 us (4%)
  between operations  3.03 us (1%)
    ppermute x16, starting transfers between devices, shifted(): return lax.ppermute(x, axis, pairs)  76.6 us
    ppermute x16, waiting for transfers between devices, shifted(): return lax.ppermute(x, axis, pairs)  65.9 us
    pallas_call x2, Pallas kernels, merge_call(): pl.pallas_call(kernel, grid=(head_count,), in_specs=[pl.BlockSpec((1, val...  16.8 us
    pallas_call x1, Pallas kernels, body(): pl.pallas_call(window_kernel, grid=(head_count,), in_specs=[pl.BlockSpec(...  9.67 us
    ppermute x2, starting transfers between devices, hd_sum(): x = x + lax.ppermute(x, 'hd', pairs)  7.42 us
    pallas_call x1, Pallas kernels, body(): pl.pallas_call(pick_kernel, grid_spec=pltpu.PrefetchScalarGridSpec(num_sc...  5.33 us
  transfers between devices with their start and end apart: 18, of which 3 were waited for; matrix products, arithmetic and copies ran while one was open for 8% of the time, Pallas kernels for 11%

profile of v8, /device:TPU:199, one launch (start us, length us, event | category | flops | bytes accessed | tf_op | source)
XLA Modules:
  0.0 205.8 jit_solution(12314925187561934884)
XLA Ops:
  0.0 1.3 multiply_reduce_fusion.1
  1.3 1.2 multiply_reduce_fusion
  2.5 3.2 %collective-permute-start = (f32[2,3,128]{2,1,0:T(4,128)S(1)}, f32[2,3,128]{2,1,0:T(4,128)S(1)}, u32[]{:S(2)}, u32[]{:S(2)}) collective-permute-start(f32[2,3,128]{2,1,0:T(4,128)S(1)} %pad_maximum_fusion.1), channel_id=1, source_target_pairs={{0,1},{1,0},{2,3},{3,2},{4,5},{5,4},{6,7},{7,6},{8,9},{9,8},{10,11... | collective-permute-start | bytes 9224 | tf_op jit(solution)/shard_map/ppermute | solution.py:43
  5.8 0.9 copy.19
  6.7 1.4 fusion.26
  8.1 0.7 gather_fusion
  8.8 1.5 fusion.29
  11.5 0.0 collective-permute-done
  11.6 4.2 %collective-permute-start.1 = (f32[2,3,128]{2,1,0:T(4,128)S(1)}, f32[2,3,128]{2,1,0:T(4,128)S(1)}, u32[]{:S(2)}, u32[]{:S(2)}) collective-permute-start(f32[2,3,128]{2,1,0:T(4,128)S(1)} %fusion.25), channel_id=1, source_target_pairs={{0,2},{1,3},{2,0},{3,1},{4,6},{5,7},{6,4},{7,5},{8,10},{9,11},{10,... | collective-permute-start | bytes 9224 | tf_op jit(solution)/shard_map/ppermute | solution.py:43
  16.4 0.1 copy.17
  16.5 0.7 copy.18
  17.2 0.1 copy.15
  17.3 0.1 copy.16
  17.4 0.6 min.22.idx_ref
  18.6 5.3 %shard_map.91 = (bf16[4,128,640]{2,1,0:T(8,128)(2,1)}, bf16[4,128,640]{2,1,0:T(8,128)(2,1)}, bf16[4,128,640]{2,1,0:T(8,128)(2,1)}, bf16[4,128,640]{2,1,0:T(8,128...) custom-call(s32[18]{0:T(128)} %min.22.idx_ref, ...), custom_call_target="tpu_custom_call" | custom-call | tf_op jit(solution)/shard_map/pallas_call | solution.py:160
  24.0 0.0 collective-permute-done.1
  24.0 0.1 rsqrt.23
  24.1 0.0 copy-start.2
  24.1 0.2 multiply_convert_fusion
  24.3 0.2 fusion.6
  24.5 9.7 %collective-permute-start.2 = (bf16[2,3,4,4,640]{4,3,2,1,0:T(4,128)(2,1)S(1)}, bf16[2,3,4,4,640]{4,3,2,1,0:T(4,128)(2,1)}, u32[]{:S(2)}, u32[]{:S(2)}) collective-permute-start(bf16[2,3,4,4,640]{4,3,2,1,0:T(4,128)(2,1)S(1)} %get-tuple-element.39), channel_id=1, source_target_pairs={{0,36},{4,40},{8,44},{12,48},{16,52},{20,56},{24,60},{28,64},{32,6... | collective-permute-start | bytes 368648 | tf_op jit(solution)/shard_map/ppermute | solution.py:23
  34.2 1.9 collective-permute-start.4
  36.2 10.0 %collective-permute-start.7 = (bf16[2,3,4,4,640]{4,3,2,1,0:T(4,128)(2,1)S(1)}, bf16[2,3,4,4,640]{4,3,2,1,0:T(4,128)(2,1)}, u32[]{:S(2)}, u32[]{:S(2)}) collective-permute-start(bf16[2,3,4,4,640]{4,3,2,1,0:T(4,128)(2,1)S(1)} %get-tuple-element.41), channel_id=1, source_target_pairs={{28,0},{32,4},{36,8},{40,12},{44,16},{48,20},{52,24},{56,28},{60,3... | collective-permute-start | bytes 368648 | tf_op jit(solution)/shard_map/ppermute | solution.py:23
  46.1 1.9 collective-permute-start.9
  48.1 0.3 fusion.4
  48.4 7.0 %collective-permute-start.5 = (bf16[2,3,8,4,640]{4,3,2,1,0:T(4,128)(2,1)S(1)}, bf16[2,3,8,4,640]{4,3,2,1,0:T(4,128)(2,1)S(1)}, u32[]{:S(2)}, u32[]{:S(2)}) collective-permute-start(bf16[2,3,8,4,640]{4,3,2,1,0:T(4,128)(2,1)S(1)} %get-tuple-element.45), channel_id=1, source_target_pairs={{0,4},{4,8},{8,12},{12,16},{16,20},{20,24},{24,28},{28,32},{32,36}... | collective-permute-start | bytes 737288 | tf_op jit(solution)/shard_map/ppermute | solution.py:23
  55.4 0.0 collective-permute-done.2
  55.4 1.9 collective-permute-start.6
  57.3 0.0 collective-permute-done.4
  57.3 12.6 %collective-permute-start.10 = (bf16[4,128,640]{2,1,0:T(8,128)(2,1)}, bf16[4,128,640]{2,1,0:T(8,128)(2,1)S(1)}, u32[]{:S(2)}, u32[]{:S(2)}) collective-permute-start(bf16[4,128,640]{2,1,0:T(8,128)(2,1)} %get-tuple-element.24), channel_id=1, source_target_pairs={{0,36},{4,40},{8,44},{12,48},{16,52},{20,56},{24,60},{28,64},{32,6... | collective-permute-start | bytes 1966088 | tf_op jit(solution)/shard_map/ppermute | solution.py:23
  70.0 0.0 collective-permute-done.7
  70.0 3.8 %collective-permute-start.11 = (bf16[4,128,640]{2,1,0:T(8,128)(2,1)}, bf16[4,128,640]{2,1,0:T(8,128)(2,1)S(1)}, u32[]{:S(2)}, u32[]{:S(2)}) collective-permute-start(bf16[4,128,640]{2,1,0:T(8,128)(2,1)} %get-tuple-element.25), channel_id=1, source_target_pairs={{0,32},{4,36},{8,40},{12,44},{16,48},{20,52},{24,56},{28,60},{32,6... | collective-permute-start | bytes 1966088 | tf_op jit(solution)/shard_map/ppermute | solution.py:23
  73.7 0.0 collective-permute-done.9
  73.7 1.9 collective-permute-start.12
  75.7 1.1 fusion.3
  76.7 0.0 collective-permute-done.5
  76.7 2.7 %collective-permute-start.3 = (bf16[2,3,4,16,640]{4,3,2,1,0:T(8,128)(2,1)}, bf16[2,3,4,16,640]{4,3,2,1,0:T(8,128)(2,1)S(1)}, u32[]{:S(2)}, u32[]{:S(2)}) collective-permute-start(bf16[2,3,4,16,640]{4,3,2,1,0:T(8,128)(2,1)} %get-tuple-element.43), channel_id=1, source_target_pairs={{0,32},{4,36},{8,40},{12,44},{16,48},{20,52},{24,56},{28,60},{32,6... | collective-permute-start | bytes 1474568 | tf_op jit(solution)/shard_map/ppermute | solution.py:23
  79.5 0.0 collective-permute-done.6
  79.5 4.1 %collective-permute-start.8 = (bf16[2,3,4,16,640]{4,3,2,1,0:T(8,128)(2,1)}, bf16[2,3,4,16,640]{4,3,2,1,0:T(8,128)(2,1)}, u32[]{:S(2)}, u32[]{:S(2)}) collective-permute-start(bf16[2,3,4,16,640]{4,3,2,1,0:T(8,128)(2,1)} %get-tuple-element.44), channel_id=1, source_target_pairs={{32,0},{36,4},{40,8},{44,12},{48,16},{52,20},{56,24},{60,28},{64,3... | collective-permute-start | bytes 1474568 | tf_op jit(solution)/shard_map/ppermute | solution.py:23
  83.5 0.1 and_convert_fusion
  83.6 0.7 convert_element_type.74.wvalid_ref
  84.3 0.8 fusion.14
  85.1 1.7 fusion.1.q_ref
  86.7 41.4 %collective-permute-done.3 = bf16[2,3,4,16,640]{4,3,2,1,0:T(8,128)(2,1)S(1)} collective-permute-done((bf16[2,3,4,16,640]{4,3,2,1,0:T(8,128)(2,1)}, bf16[2,3,4,16,640]{4,3,2,1,0:T(8,128)(2,1)S(1)}, u32[]{:S(2)}, u32[]{:S(2)}) %collective-permute-start.3) | collective-permute-done | bytes 491552 | tf_op jit(solution)/shard_map/ppermute | solution.py:23
  128.1 1.9 collective-permute-start.13
  130.0 0.0 collective-permute-done.8
  130.1 2.4 %collective-permute-start.14 = (bf16[4,128,640]{2,1,0:T(8,128)(2,1)}, bf16[4,128,640]{2,1,0:T(8,128)(2,1)S(1)}, u32[]{:S(2)}, u32[]{:S(2)}) collective-permute-start(bf16[4,128,640]{2,1,0:T(8,128)(2,1)} %get-tuple-element.31), channel_id=1, source_target_pairs={{4,0},{8,4},{12,8},{16,12},{20,16},{24,20},{28,24},{32,28},{36,32}... | collective-permute-start | bytes 1966088 | tf_op jit(solution)/shard_map/ppermute | solution.py:23
  132.5 0.0 collective-permute-done.10.rest_0_
  132.5 6.6 %collective-permute-start.15 = (bf16[4,128,640]{2,1,0:T(8,128)(2,1)}, bf16[4,128,640]{2,1,0:T(8,128)(2,1)}, u32[]{:S(2)}, u32[]{:S(2)}) collective-permute-start(bf16[4,128,640]{2,1,0:T(8,128)(2,1)} %get-tuple-element.32), channel_id=1, source_target_pairs={{28,0},{32,4},{36,8},{40,12},{44,16},{48,20},{52,24},{56,28},{60,3... | collective-permute-start | bytes 1966088 | tf_op jit(solution)/shard_map/ppermute | solution.py:23
  139.1 4.8 %collective-permute-start.16 = (bf16[4,128,640]{2,1,0:T(8,128)(2,1)}, bf16[4,128,640]{2,1,0:T(8,128)(2,1)}, u32[]{:S(2)}, u32[]{:S(2)}) collective-permute-start(bf16[4,128,640]{2,1,0:T(8,128)(2,1)} %get-tuple-element.33), channel_id=1, source_target_pairs={{32,0},{36,4},{40,8},{44,12},{48,16},{52,20},{56,24},{60,28},{64,3... | collective-permute-start | bytes 1966088 | tf_op jit(solution)/shard_map/ppermute | solution.py:23
  143.9 0.0 collective-permute-done.12.rest_2_
  143.9 3.4 %collective-permute-start.17 = (bf16[4,128,640]{2,1,0:T(8,128)(2,1)}, bf16[4,128,640]{2,1,0:T(8,128)(2,1)}, u32[]{:S(2)}, u32[]{:S(2)}) collective-permute-start(bf16[4,128,640]{2,1,0:T(8,128)(2,1)} %get-tuple-element.34), channel_id=1, source_target_pairs={{36,0},{40,4},{44,8},{48,12},{52,16},{56,20},{60,24},{64,28},{68,3... | collective-permute-start | bytes 1966088 | tf_op jit(solution)/shard_map/ppermute | solution.py:23
  147.3 3.5 %maximum_maximum_fusion = bf16[2,3,16,24,640]{4,3,2,1,0:T(8,128)(2,1)S(1)} fusion(bf16[2,3,4,4,640]{4,3,2,1,0:T(4,128)(2,1)} %collective-permute-done.9, bf16[2,3,4,16,640]{4,3,2,1,0:T(8,128)(2,1)} %collective-permute-done.8, bf16[2,3,4,4,640]{4,3,2,1,0:T(4,128)(2,1)} %collective-permute-done.7, bf16[2,3,8,4,640]{4,3,2,1,0:T(4,128)(2,1)} %collective-permute-done.6, ...), kind=kLoop, calls=%fused_computation.1 | loop fusion | flops 29491200 | bytes 5898240 | tf_op jit(solution)/shard_map/concatenate | solution.py:206
  150.9 1.9 fusion.27
  152.8 0.6 broadcast_in_dim.11
  153.4 9.7 %shard_map.92 = (f32[384,640]{1,0:T(8,128)}, f32[384,640]{1,0:T(8,128)}, f32[384,640]{1,0:T(8,128)}) custom-call(s32[1,1152]{1,0:T(1,128)} %convert_element_type.74.wvalid_ref, s32[1,256]{1,0:T(1,128)} %bitcast.48, bf16[384,640]{1,0:T(8,128)(2,1)} %fusion.1.q_ref, bf16[1152,640]{1,0:T(8,128)(2,1)} %bitcast.34, bf16[1152,640]{1,0:T(8,128)(2,1)} %bitcast.33, ...), custom_call_target="tpu_custom_call" | custom-call | tf_op jit(solution)/shard_map/pallas_call | solution.py:249
  163.1 0.0 collective-permute-done.13.rest_3_
  163.1 0.7 broadcast_in_dim.9
  163.8 8.5 %shard_map.93 = (f32[384,640]{1,0:T(8,128)}, f32[384,640]{1,0:T(8,128)}, f32[384,640]{1,0:T(8,128)}) custom-call(s32[1,1024]{1,0:T(1,128)} %bitcast.44, bf16[384,640]{1,0:T(8,128)(2,1)} %fusion.1.q_ref, f32[384,640]{1,0:T(8,128)} %get-tuple-element.21.acc_ref, f32[384,640]{1,0:T(8,128)} %get-tuple-element.22.m_ref, f32[384,640]{1,0:T(8,128)} %get-tuple-element.23.l_ref, ...), custom_call_target="tpu_custom_call" | custom-call | tf_op jit(solution)/shard_map/pallas_call | solution.py:275
  172.3 0.0 collective-permute-done.14.rest_0_
  172.3 1.7 collective-permute-done.16.rest_2_
  174.0 22.8 %collective-permute-done.17.rest_3_ = bf16[4,128,640]{2,1,0:T(8,128)(2,1)} collective-permute-done((bf16[4,128,640]{2,1,0:T(8,128)(2,1)}, bf16[4,128,640]{2,1,0:T(8,128)(2,1)}, u32[]{:S(2)}, u32[]{:S(2)}) %collective-permute-start.17) | collective-permute-done | bytes 655392 | tf_op jit(solution)/shard_map/ppermute | solution.py:23
  196.8 0.7 broadcast_in_dim.8
  197.5 8.3 %shard_map.94 = bf16[384,640]{1,0:T(8,128)(2,1)} custom-call(s32[1,1024]{1,0:T(1,128)} %bitcast.45, bf16[384,640]{1,0:T(8,128)(2,1)} %fusion.1.q_ref, f32[384,640]{1,0:T(8,128)} %get-tuple-element.28.acc_ref, f32[384,640]{1,0:T(8,128)} %get-tuple-element.29.m_ref, f32[384,640]{1,0:T(8,128)} %get-tuple-element.30.l_ref, bf16[4,128,640]{2,1,0:T(8,128)(2,1)} %copy-done.5, ...), custom_call_target="tpu_custom_call" | custom-call | tf_op jit(solution)/shard_map/pallas_call | solution.py:275
  (29 shorter events, 0.1 us)
Async XLA Ops:
  0.0 24.1 %copy-start.1 = (bf16[1,3,128,640]{3,2,1,0:T(8,128)(2,1)S(1)}, bf16[1,3,128,640]{3,2,1,0:T(8,128)(2,1)}, u32[]{:S(2)}) copy-start(bf16[1,3,128,640]{3,2,1,0:T(8,128)(2,1)} %param.10) | copy-start | bytes 1474564
  0.0 24.1 %copy-start.8 = (f32[640]{0:T(1024)S(1)}, f32[640]{0:T(1024)}, u32[]{:S(2)}) copy-start(f32[640]{0:T(1024)} %param.15) | copy-start | bytes 7684
  0.0 24.3 %copy-start = (bf16[1,3,128,640]{3,2,1,0:T(8,128)(2,1)S(1)}, bf16[1,3,128,640]{3,2,1,0:T(8,128)(2,1)}, u32[]{:S(2)}) copy-start(bf16[1,3,128,640]{3,2,1,0:T(8,128)(2,1)} %param.11) | copy-start | bytes 1474564
  2.5 9.0 %collective-permute-start = (f32[2,3,128]{2,1,0:T(4,128)S(1)}, f32[2,3,128]{2,1,0:T(4,128)S(1)}, u32[]{:S(2)}, u32[]{:S(2)}) collective-permute-start(f32[2,3,128]{2,1,0:T(4,128)S(1)} %pad_maximum_fusion.1), channel_id=1, source_target_pairs={{0,1},{1,0},{2,3},{3,2},{4,5},{5,4},{6,7},{7,6},{8,9},{9,8},{10,11... | collective-permute-start | bytes 9224 | tf_op jit(solution)/shard_map/ppermute | solution.py:43
  11.6 12.4 %collective-permute-start.1 = (f32[2,3,128]{2,1,0:T(4,128)S(1)}, f32[2,3,128]{2,1,0:T(4,128)S(1)}, u32[]{:S(2)}, u32[]{:S(2)}) collective-permute-start(f32[2,3,128]{2,1,0:T(4,128)S(1)} %fusion.25), channel_id=1, source_target_pairs={{0,2},{1,3},{2,0},{3,1},{4,6},{5,7},{6,4},{7,5},{8,10},{9,11},{10,... | collective-permute-start | bytes 9224 | tf_op jit(solution)/shard_map/ppermute | solution.py:43
  24.1 61.0 %copy-start.2 = (bf16[1,3,128,640]{3,2,1,0:T(8,128)(2,1)S(1)}, bf16[1,3,128,640]{3,2,1,0:T(8,128)(2,1)}, u32[]{:S(2)}) copy-start(bf16[1,3,128,640]{3,2,1,0:T(8,128)(2,1)} %param.9) | copy-start | bytes 1474564
  24.5 30.9 %collective-permute-start.2 = (bf16[2,3,4,4,640]{4,3,2,1,0:T(4,128)(2,1)S(1)}, bf16[2,3,4,4,640]{4,3,2,1,0:T(4,128)(2,1)}, u32[]{:S(2)}, u32[]{:S(2)}) collective-permute-start(bf16[2,3,4,4,640]{4,3,2,1,0:T(4,128)(2,1)S(1)} %get-tuple-element.39), channel_id=1, source_target_pairs={{0,36},{4,40},{8,44},{12,48},{16,52},{20,56},{24,60},{28,64},{32,6... | collective-permute-start | bytes 368648 | tf_op jit(solution)/shard_map/ppermute | solution.py:23
  34.2 23.1 %collective-permute-start.4 = (bf16[2,3,4,4,640]{4,3,2,1,0:T(4,128)(2,1)S(1)}, bf16[2,3,4,4,640]{4,3,2,1,0:T(4,128)(2,1)}, u32[]{:S(2)}, u32[]{:S(2)}) collective-permute-start(bf16[2,3,4,4,640]{4,3,2,1,0:T(4,128)(2,1)S(1)} %get-tuple-element.40), channel_id=1, source_target_pairs={{0,28},{4,32},{8,36},{12,40},{16,44},{20,48},{24,52},{28,56},{32,6... | collective-permute-start | bytes 368648 | tf_op jit(solution)/shard_map/ppermute | solution.py:23
  36.2 33.8 %collective-permute-start.7 = (bf16[2,3,4,4,640]{4,3,2,1,0:T(4,128)(2,1)S(1)}, bf16[2,3,4,4,640]{4,3,2,1,0:T(4,128)(2,1)}, u32[]{:S(2)}, u32[]{:S(2)}) collective-permute-start(bf16[2,3,4,4,640]{4,3,2,1,0:T(4,128)(2,1)S(1)} %get-tuple-element.41), channel_id=1, source_target_pairs={{28,0},{32,4},{36,8},{40,12},{44,16},{48,20},{52,24},{56,28},{60,3... | collective-permute-start | bytes 368648 | tf_op jit(solution)/shard_map/ppermute | solution.py:23
  46.1 27.6 %collective-permute-start.9 = (bf16[2,3,4,4,640]{4,3,2,1,0:T(4,128)(2,1)S(1)}, bf16[2,3,4,4,640]{4,3,2,1,0:T(4,128)(2,1)}, u32[]{:S(2)}, u32[]{:S(2)}) collective-permute-start(bf16[2,3,4,4,640]{4,3,2,1,0:T(4,128)(2,1)S(1)} %get-tuple-element.42), channel_id=1, source_target_pairs={{36,0},{40,4},{44,8},{48,12},{52,16},{56,20},{60,24},{64,28},{68,3... | collective-permute-start | bytes 368648 | tf_op jit(solution)/shard_map/ppermute | solution.py:23
  48.4 28.4 %collective-permute-start.5 = (bf16[2,3,8,4,640]{4,3,2,1,0:T(4,128)(2,1)S(1)}, bf16[2,3,8,4,640]{4,3,2,1,0:T(4,128)(2,1)S(1)}, u32[]{:S(2)}, u32[]{:S(2)}) collective-permute-start(bf16[2,3,8,4,640]{4,3,2,1,0:T(4,128)(2,1)S(1)} %get-tuple-element.45), channel_id=1, source_target_pairs={{0,4},{4,8},{8,12},{12,16},{16,20},{20,24},{24,28},{28,32},{32,36}... | collective-permute-start | bytes 737288 | tf_op jit(solution)/shard_map/ppermute | solution.py:23
  55.4 24.1 %collective-permute-start.6 = (bf16[2,3,8,4,640]{4,3,2,1,0:T(4,128)(2,1)S(1)}, bf16[2,3,8,4,640]{4,3,2,1,0:T(4,128)(2,1)}, u32[]{:S(2)}, u32[]{:S(2)}) collective-permute-start(bf16[2,3,8,4,640]{4,3,2,1,0:T(4,128)(2,1)S(1)} %get-tuple-element.46), channel_id=1, source_target_pairs={{4,0},{8,4},{12,8},{16,12},{20,16},{24,20},{28,24},{32,28},{36,32}... | collective-permute-start | bytes 737288 | tf_op jit(solution)/shard_map/ppermute | solution.py:23
  57.3 75.2 %collective-permute-start.10 = (bf16[4,128,640]{2,1,0:T(8,128)(2,1)}, bf16[4,128,640]{2,1,0:T(8,128)(2,1)S(1)}, u32[]{:S(2)}, u32[]{:S(2)}) collective-permute-start(bf16[4,128,640]{2,1,0:T(8,128)(2,1)} %get-tuple-element.24), channel_id=1, source_target_pairs={{0,36},{4,40},{8,44},{12,48},{16,52},{20,56},{24,60},{28,64},{32,6... | collective-permute-start | bytes 1966088 | tf_op jit(solution)/shard_map/ppermute | solution.py:23
  70.0 69.1 %collective-permute-start.11 = (bf16[4,128,640]{2,1,0:T(8,128)(2,1)}, bf16[4,128,640]{2,1,0:T(8,128)(2,1)S(1)}, u32[]{:S(2)}, u32[]{:S(2)}) collective-permute-start(bf16[4,128,640]{2,1,0:T(8,128)(2,1)} %get-tuple-element.25), channel_id=1, source_target_pairs={{0,32},{4,36},{8,40},{12,44},{16,48},{20,52},{24,56},{28,60},{32,6... | collective-permute-start | bytes 1966088 | tf_op jit(solution)/shard_map/ppermute | solution.py:23
  73.7 70.2 %collective-permute-start.12 = (bf16[4,128,640]{2,1,0:T(8,128)(2,1)}, bf16[4,128,640]{2,1,0:T(8,128)(2,1)}, u32[]{:S(2)}, u32[]{:S(2)}) collective-permute-start(bf16[4,128,640]{2,1,0:T(8,128)(2,1)} %get-tuple-element.26), channel_id=1, source_target_pairs={{0,28},{4,32},{8,36},{12,40},{16,44},{20,48},{24,52},{28,56},{32,6... | collective-permute-start | bytes 1966088 | tf_op jit(solution)/shard_map/ppermute | solution.py:23
  76.7 51.4 %collective-permute-start.3 = (bf16[2,3,4,16,640]{4,3,2,1,0:T(8,128)(2,1)}, bf16[2,3,4,16,640]{4,3,2,1,0:T(8,128)(2,1)S(1)}, u32[]{:S(2)}, u32[]{:S(2)}) collective-permute-start(bf16[2,3,4,16,640]{4,3,2,1,0:T(8,128)(2,1)} %get-tuple-element.43), channel_id=1, source_target_pairs={{0,32},{4,36},{8,40},{12,44},{16,48},{20,52},{24,56},{28,60},{32,6... | collective-permute-start | bytes 1474568 | tf_op jit(solution)/shard_map/ppermute | solution.py:23
  79.5 50.6 %collective-permute-start.8 = (bf16[2,3,4,16,640]{4,3,2,1,0:T(8,128)(2,1)}, bf16[2,3,4,16,640]{4,3,2,1,0:T(8,128)(2,1)}, u32[]{:S(2)}, u32[]{:S(2)}) collective-permute-start(bf16[2,3,4,16,640]{4,3,2,1,0:T(8,128)(2,1)} %get-tuple-element.44), channel_id=1, source_target_pairs={{32,0},{36,4},{40,8},{44,12},{48,16},{52,20},{56,24},{60,28},{64,3... | collective-permute-start | bytes 1474568 | tf_op jit(solution)/shard_map/ppermute | solution.py:23
  128.1 1.9 copy-start.6
  128.1 35.0 %collective-permute-start.13 = (bf16[4,128,640]{2,1,0:T(8,128)(2,1)}, bf16[4,128,640]{2,1,0:T(8,128)(2,1)}, u32[]{:S(2)}, u32[]{:S(2)}) collective-permute-start(bf16[4,128,640]{2,1,0:T(8,128)(2,1)} %get-tuple-element.27), channel_id=1, source_target_pairs={{0,4},{4,8},{8,12},{12,16},{16,20},{20,24},{24,28},{28,32},{32,36}... | collective-permute-start | bytes 1966088 | tf_op jit(solution)/shard_map/ppermute | solution.py:23
  130.1 42.3 %collective-permute-start.14 = (bf16[4,128,640]{2,1,0:T(8,128)(2,1)}, bf16[4,128,640]{2,1,0:T(8,128)(2,1)S(1)}, u32[]{:S(2)}, u32[]{:S(2)}) collective-permute-start(bf16[4,128,640]{2,1,0:T(8,128)(2,1)} %get-tuple-element.31), channel_id=1, source_target_pairs={{4,0},{8,4},{12,8},{16,12},{20,16},{24,20},{28,24},{32,28},{36,32}... | collective-permute-start | bytes 1966088 | tf_op jit(solution)/shard_map/ppermute | solution.py:23
  132.5 18.4 %copy-start.3 = (bf16[4,128,640]{2,1,0:T(8,128)(2,1)}, bf16[4,128,640]{2,1,0:T(8,128)(2,1)S(1)}, u32[]{:S(2)}) copy-start(bf16[4,128,640]{2,1,0:T(8,128)(2,1)S(1)} %collective-permute-done.10.rest_0_) | copy-start | bytes 1966084
  132.5 39.8 %collective-permute-start.15 = (bf16[4,128,640]{2,1,0:T(8,128)(2,1)}, bf16[4,128,640]{2,1,0:T(8,128)(2,1)}, u32[]{:S(2)}, u32[]{:S(2)}) collective-permute-start(bf16[4,128,640]{2,1,0:T(8,128)(2,1)} %get-tuple-element.32), channel_id=1, source_target_pairs={{28,0},{32,4},{36,8},{40,12},{44,16},{48,20},{52,24},{56,28},{60,3... | collective-permute-start | bytes 1966088 | tf_op jit(solution)/shard_map/ppermute | solution.py:23
  139.1 11.8 %copy-start.4 = (bf16[4,128,640]{2,1,0:T(8,128)(2,1)}, bf16[4,128,640]{2,1,0:T(8,128)(2,1)S(1)}, u32[]{:S(2)}) copy-start(bf16[4,128,640]{2,1,0:T(8,128)(2,1)S(1)} %collective-permute-done.11.rest_1_) | copy-start | bytes 1966084
  139.1 34.9 %collective-permute-start.16 = (bf16[4,128,640]{2,1,0:T(8,128)(2,1)}, bf16[4,128,640]{2,1,0:T(8,128)(2,1)}, u32[]{:S(2)}, u32[]{:S(2)}) collective-permute-start(bf16[4,128,640]{2,1,0:T(8,128)(2,1)} %get-tuple-element.33), channel_id=1, source_target_pairs={{32,0},{36,4},{40,8},{44,12},{48,16},{52,20},{56,24},{60,28},{64,3... | collective-permute-start | bytes 1966088 | tf_op jit(solution)/shard_map/ppermute | solution.py:23
  143.9 52.9 %collective-permute-start.17 = (bf16[4,128,640]{2,1,0:T(8,128)(2,1)}, bf16[4,128,640]{2,1,0:T(8,128)(2,1)}, u32[]{:S(2)}, u32[]{:S(2)}) collective-permute-start(bf16[4,128,640]{2,1,0:T(8,128)(2,1)} %get-tuple-element.34), channel_id=1, source_target_pairs={{36,0},{40,4},{44,8},{48,12},{52,16},{56,20},{60,24},{64,28},{68,3... | collective-permute-start | bytes 1966088 | tf_op jit(solution)/shard_map/ppermute | solution.py:23
  152.8 10.3 %copy-start.7 = (s32[4,2]{1,0:T(4,128)S(1)}, s32[4,2]{1,0:T(4,128)}, u32[]{:S(2)}) copy-start(s32[4,2]{1,0:T(4,128)} %copy.18) | copy-start | bytes 100
  172.3 25.2 %copy-start.5 = (bf16[4,128,640]{2,1,0:T(8,128)(2,1)}, bf16[4,128,640]{2,1,0:T(8,128)(2,1)S(1)}, u32[]{:S(2)}) copy-start(bf16[4,128,640]{2,1,0:T(8,128)(2,1)S(1)} %collective-permute-done.14.rest_0_) | copy-start | bytes 1966084
